TPU v7x, 512 devices: a whole 4x8x8 slice. The times are simulated.
512 devices in a mesh: ep: 128 (over z, y, core), dp: 4 (over x).
Axes of the slice: x: 4, y: 8, z: 8, core: 2. Of those that a mesh axis runs over, the one named last changes fastest.
Arguments:
- tokens: bfloat16 [8192, 2048], P('ep', 'dp'), may hold values from -6 to 6
- expert_ids: int32 [8192, 8], P('ep'), may hold values from 0 to 127, as said below
- gate_probs: float32 [8192, 8], P('ep'), may hold values from 0.05 to 1
- gate_weight: bfloat16 [128, 2048, 1024], P('ep', None, 'dp'), may hold values from -0.125 to 0.125
- up_weight: bfloat16 [128, 2048, 1024], P('ep', None, 'dp'), may hold values from -0.125 to 0.125
- down_weight: bfloat16 [128, 1024, 2048], P('ep', None, 'dp'), may hold values from -0.1875 to 0.1875
Outputs:
- combined: bfloat16 [8192, 2048], P('ep', 'dp')
Inputs may be any that keep to these rules, and one draw needn't show every extreme that they name: `expert_ids`: each row names 8 different experts. The same 2 experts, the same pair on every device, are each named exactly 16 times among the 64 rows of each device, and every other expert at most 4 times among a device's rows, some exactly 4 times.
All inputs are finite; a program needn't handle non-finite values.
Results may differ from a plain program's by a relative error of at most 0.0057.
Values may be sent and summed in bfloat16 or wider, within the bound.
No kernel may reach another device: no remote copies, remote signals or barrier semaphores. Data moves between devices by JAX's collectives and lax.ppermute only.
A program may use at most 64 MiB of HBM per device.

v0:
```python
import jax
import jax.numpy as jnp
from jax import lax
from jax.sharding import PartitionSpec as P

HOT = 2


def from_root(block, axis, holder):
    block = jnp.where(lax.axis_index(axis) == holder, block, jnp.zeros_like(block))
    return lax.psum(block, axis)


def silu_product(gate_part, up_part):
    return (jax.nn.silu(gate_part) * up_part).astype(jnp.bfloat16)


def local(tokens, expert_ids, gate_probs, gate_weight, up_weight, down_weight):
    ep_count = lax.axis_size("ep")
    dp_count = lax.axis_size("dp")
    ep_index = lax.axis_index("ep")
    tok_rows, top_count = expert_ids.shape
    exp_dev = gate_weight.shape[0]
    expert_count = exp_dev * ep_count
    model_width = tokens.shape[1] * dp_count
    hot_load = min(tok_rows * 3 // 4, 4 * tok_rows * top_count // expert_count)
    cold_total = tok_rows * top_count - HOT * hot_load
    capacity = (cold_total + expert_count - HOT - 1) // (expert_count - HOT)
    host_count = ep_count // HOT
    spread_count = min(hot_load // 2, host_count)
    spare_slots = hot_load // spread_count
    primary_slots = exp_dev * capacity
    per_owner = primary_slots + spare_slots
    total_slots = ep_count * per_owner
    flat_ids = expert_ids.reshape(-1)
    expert_range = jnp.arange(expert_count, dtype=jnp.int32)
    matches = (flat_ids[:, None] == expert_range[None, :]).astype(jnp.int32)
    expert_loads = jnp.sum(matches, axis=0)
    _, hot_ids = lax.top_k(expert_loads * expert_count + (expert_count - 1 - expert_range), HOT)
    earlier = jnp.cumsum(matches, axis=0) - matches
    order_rank = jnp.sum(earlier * matches, axis=1)
    hot_match = (flat_ids[:, None] == hot_ids[None, :]).astype(jnp.int32)
    is_hot = jnp.sum(hot_match, axis=1) > 0
    which_hot = jnp.sum(hot_match * jnp.arange(HOT, dtype=jnp.int32)[None, :], axis=1)
    host_slot = (ep_index * spread_count + order_rank // spare_slots) % host_count
    hot_target = (
        (host_slot * HOT + which_hot) * per_owner + primary_slots + order_rank % spare_slots
    )
    cold_target = flat_ids // exp_dev * per_owner + flat_ids % exp_dev * capacity + order_rank
    target = jnp.where(is_hot, hot_target, cold_target)
    source_row = jnp.full((total_slots,), tok_rows, jnp.int32)
    source_row = source_row.at[target].set(
        jnp.arange(tok_rows * top_count, dtype=jnp.int32) // top_count
    )
    replica = None
    for position in range(HOT):
        chosen = hot_ids[position]
        local_index = chosen % exp_dev
        own_parts = (gate_weight[local_index], up_weight[local_index], down_weight[local_index])
        delivered = (
            from_root(own_parts[0], "ep", chosen // exp_dev),
            from_root(own_parts[1], "ep", chosen // exp_dev),
            from_root(own_parts[2], "ep", chosen // exp_dev),
        )
        if replica is None:
            replica = delivered
        else:
            is_mine = ep_index % HOT == position
            replica = tuple(
                (jnp.where(is_mine, fresh, older) for fresh, older in zip(delivered, replica))
            )
    spare_gate, spare_up, spare_down = replica
    features = lax.all_gather(tokens, "dp", axis=1, tiled=True)
    outgoing = jnp.take(features, source_row, axis=0, mode="fill", fill_value=0)
    incoming = lax.all_to_all(
        outgoing.reshape(ep_count, per_owner, model_width),
        "ep",
        split_axis=0,
        concat_axis=0,
        tiled=True,
    )
    primary_rows = incoming[:, :primary_slots].reshape(ep_count, exp_dev, capacity, model_width)
    spare_rows = incoming[:, primary_slots:]
    gate_primary = jnp.einsum(
        "secd,edf->secf", primary_rows, gate_weight, preferred_element_type=jnp.float32
    )
    up_primary = jnp.einsum(
        "secd,edf->secf", primary_rows, up_weight, preferred_element_type=jnp.float32
    )
    gate_spare = jnp.einsum(
        "srd,df->srf", spare_rows, spare_gate, preferred_element_type=jnp.float32
    )
    up_spare = jnp.einsum("srd,df->srf", spare_rows, spare_up, preferred_element_type=jnp.float32)
    hidden_primary = silu_product(gate_primary, up_primary).reshape(ep_count, primary_slots, -1)
    hidden_spare = silu_product(gate_spare, up_spare)
    hidden = jnp.concatenate([hidden_primary, hidden_spare], axis=1)
    feature_local = down_weight.shape[2]
    portion = lax.all_gather(hidden, "dp", axis=2, tiled=True)
    length = portion.shape[2]
    primary_part = portion[:, :primary_slots].reshape(ep_count, exp_dev, capacity, length)
    spare_part = portion[:, primary_slots:]
    out_primary = jnp.einsum(
        "secf,efd->secd", primary_part, down_weight, preferred_element_type=jnp.float32
    )
    out_spare = jnp.einsum(
        "srf,fd->srd", spare_part, spare_down, preferred_element_type=jnp.float32
    )
    results = jnp.concatenate(
        [out_primary.reshape(ep_count, primary_slots, feature_local), out_spare], axis=1
    ).astype(jnp.bfloat16)
    returned = lax.all_to_all(results, "ep", split_axis=0, concat_axis=0, tiled=True).reshape(
        total_slots, feature_local
    )
    fetched = jnp.take(returned, target, axis=0).reshape(tok_rows, top_count, feature_local)
    combined = jnp.sum(gate_probs[:, :, None] * fetched.astype(jnp.float32), axis=1)
    return combined.astype(jnp.bfloat16)


def solution(mesh):
    in_specs = (
        P("ep", "dp"),
        P("ep", None),
        P("ep", None),
        P("ep", None, "dp"),
        P("ep", None, "dp"),
        P("ep", None, "dp"),
    )
    out_specs = P("ep", "dp")
    return jax.shard_map(local, mesh=mesh, in_specs=in_specs, out_specs=out_specs, check_vma=False)
```

profile of v0, /device:TPU:1, one launch (start us, length us, event | category | flops | bytes accessed | tf_op | source)
XLA Modules:
  0.0 442.6 jit_solution(2798610445282375256)
XLA Ops:
  6.5 0.7 broadcast_multiply_fusion
  7.2 0.8 copy.37
  8.8 0.2 fusion.36
  9.0 2.5 top_k.11
  11.7 2.4 scatter_custom_fusion
  14.4 10.8 %all_gather.6 = bf16[64,2048]{1,0:T(8,128)(2,1)S(1)} all-gather(bf16[64,512]{1,0:T(8,128)(2,1)} %param.6), channel_id=1, replica_groups=mesh['ep'=128,'dp'=4] {'dp'}, dimensions={1}, use_global_device_ids=true | all-gather | bytes 327680 | tf_op jit(solution)/shard_map/all_gather | solution.py:73
  25.1 3.4 gather_fusion
  28.6 2.9 gather.13
  31.4 4.6 %broadcast_select_fusion = bf16[128,6,2048]{2,1,0:T(8,128)(2,1)} fusion(bf16[128,6,2048]{2,1,0:T(8,128)(2,1)} %gather.13, pred[128,6]{1,0:T(8,128)(4,1)S(1)} %broadcast_in_dim.34), kind=kLoop, calls=%fused_computation.3 | loop fusion | flops 1572864 | bytes 6292224 | tf_op jit(solution)/shard_map/jit(_take)/select_n | solution.py:74
  36.0 21.1 %all-to-all-start = ((bf16[128,6,2048]{2,1,0:T(8,128)(2,1)}), bf16[128,6,2048]{2,1,0:T(8,128)(2,1)}, u32[]{:S(2)}, u32[]{:S(2)}) async-start(bf16[128,6,2048]{2,1,0:T(8,128)(2,1)} %broadcast_select_fusion), calls=%async_computation | async-start | bytes 8388608 | tf_op jit(solution)/shard_map/all_to_all | solution.py:75
  57.2 0.6 fusion.61
  59.0 1.4 bitcast_select_fusion.1
  60.4 2.1 bitcast_select_fusion.3
  62.5 0.2 all-gather.2.cloned.1.call-start
  62.8 93.7 %all-to-all-done = bf16[128,6,2048]{2,1,0:T(8,128)(2,1)} async-done(((bf16[128,6,2048]{2,1,0:T(8,128)(2,1)}), bf16[128,6,2048]{2,1,0:T(8,128)(2,1)}, u32[]{:S(2)}, u32[]{:S(2)}) %all-to-all-start) | async-done | bytes 3145760 | tf_op jit(solution)/shard_map/all_to_all | solution.py:75
  156.4 3.4 slice.42
  159.9 3.3 slice.41
  163.1 2.4 fusion.4
  165.5 2.4 fusion.16
  167.9 176.6 %all-reduce.3.cloned.1.call-done = (bf16[2048,256]{1,0:T(8,128)(2,1)}, bf16[2048,256]{1,0:T(8,128)(2,1)}, bf16[2048,256]{1,0:T(8,128)(2,1)}, bf16[2048,256]{1,0:...) async-done(((bf16[2048,256]{1,0:T(8,128)(2,1)}, bf16[2048,256]{1,0:T(8,128)(2,1)}, bf16[2048,256]{1,0:T(8,128)(2,1)}, bf16[2048,256]{1,0:T(8,128)(2,1)}, ...) | async-done | bytes 6291472 | tf_op jit(solution)/shard_map/psum | solution.py:11
  344.5 2.1 fusion.23
  346.7 0.8 fusion.19
  347.4 0.8 pad_maximum_fusion.1
  348.2 33.2 %all-gather.2.cloned.1.call-done = bf16[128,6,1024]{2,0,1:T(8,128)(2,1)} async-done(((bf16[128,6,256]{2,0,1:T(8,128)(2,1)}), bf16[128,6,1024]{2,0,1:T(8,128)(2,1)}) %all-gather.2.cloned.1.call-update) | async-done | bytes 1572880 | tf_op jit(solution)/shard_map/all_gather | solution.py:98
  381.4 1.9 convolution_convert_fusion
  383.4 1.5 convolution_convert_fusion.1
  385.0 1.4 copy.52
  386.4 15.1 %all-to-all-start.1 = ((bf16[128,6,512]{2,1,0:T(8,128)(2,1)}), bf16[128,6,512]{2,1,0:T(8,128)(2,1)S(1)}, u32[]{:S(2)}, u32[]{:S(2)}) async-start(bf16[128,6,512]{2,1,0:T(8,128)(2,1)} %copy.52), calls=%async_computation.1 | async-start | bytes 2097152 | tf_op jit(solution)/shard_map/all_to_all | solution.py:111
  402.3 30.2 %all-to-all-done.1 = bf16[128,6,512]{2,1,0:T(8,128)(2,1)S(1)} async-done(((bf16[128,6,512]{2,1,0:T(8,128)(2,1)}), bf16[128,6,512]{2,1,0:T(8,128)(2,1)S(1)}, u32[]{:S(2)}, u32[]{:S(2)}) %all-to-all-start.1) | async-done | bytes 786464 | tf_op jit(solution)/shard_map/all_to_all | solution.py:111
  432.5 0.3 reshape.246
  432.8 2.0 gather_fusion.1
  434.7 1.1 multiply_reduce_fusion
  (56 shorter events, 2.0 us)
Async XLA Ops:
  36.0 23.0 %copy-start = (bf16[1,1024,512]{2,1,0:T(8,128)(2,1)S(1)}, bf16[1,1024,512]{2,1,0:T(8,128)(2,1)}, u32[]{:S(2)}) copy-start(bf16[1,1024,512]{2,1,0:T(8,128)(2,1)} %param.11) | copy-start | bytes 3145732
  36.0 120.4 %all-to-all-start = ((bf16[128,6,2048]{2,1,0:T(8,128)(2,1)}), bf16[128,6,2048]{2,1,0:T(8,128)(2,1)}, u32[]{:S(2)}, u32[]{:S(2)}) async-start(bf16[128,6,2048]{2,1,0:T(8,128)(2,1)} %broadcast_select_fusion), calls=%async_computation | async-start | bytes 8388608 | tf_op jit(solution)/shard_map/all_to_all | solution.py:75
  57.1 3.3 copy-start.1
  57.1 3.3 copy-start.2
  57.1 287.4 %all-reduce.3.cloned.1.call-start = ((), (), s32[]{:S(2)}) async-start(), calls=%async_computation.3 | async-start | bytes 12582912 | tf_op jit(solution)/shard_map/psum | solution.py:11
  62.5 318.9 %all-gather.2.cloned.1.call-start = ((), (), s32[]{:S(2)}) async-start(), calls=%async_computation.2 | async-start | bytes 1966080 | tf_op jit(solution)/shard_map/all_gather | solution.py:98
  163.1 2.4 copy-start.3
  344.5 2.1 copy-start.8
  344.5 2.1 copy-start.9
  348.2 35.1 %copy-start.6 = (bf16[1024,512]{1,0:T(8,128)(2,1)S(1)}, bf16[1024,512]{1,0:T(8,128)(2,1)}, u32[]{:S(2)}) copy-start(bf16[1024,512]{1,0:T(8,128)(2,1)} %get-tuple-element.17) | copy-start | bytes 3145732
  348.2 35.2 %copy-start.7 = (bf16[1024,512]{1,0:T(8,128)(2,1)S(1)}, bf16[1024,512]{1,0:T(8,128)(2,1)}, u32[]{:S(2)}) copy-start(bf16[1024,512]{1,0:T(8,128)(2,1)} %get-tuple-element.18) | copy-start | bytes 3145732
  385.0 16.9 %copy-start.5 = (f32[64,8]{0,1:T(8,128)S(1)}, f32[64,8]{0,1:T(8,128)}, u32[]{:S(2)}) copy-start(f32[64,8]{0,1:T(8,128)} %param.8) | copy-start | bytes 6148
  385.0 17.2 %copy-start.4 = (s32[64,8]{0,1:T(8,128)S(1)}, s32[64,8]{0,1:T(8,128)}, u32[]{:S(2)}) copy-start(s32[64,8]{0,1:T(8,128)} %param.7) | copy-start | bytes 6148
  386.4 46.1 %all-to-all-start.1 = ((bf16[128,6,512]{2,1,0:T(8,128)(2,1)}), bf16[128,6,512]{2,1,0:T(8,128)(2,1)S(1)}, u32[]{:S(2)}, u32[]{:S(2)}) async-start(bf16[128,6,512]{2,1,0:T(8,128)(2,1)} %copy.52), calls=%async_computation.1 | async-start | bytes 2097152 | tf_op jit(solution)/shard_map/all_to_all | solution.py:111
Sparse Core Ops, SparseCore 0:
  62.6 281.8 all-reduce.2
  348.4 33.0 all-gather.1
where the time goes:
time: 443 us
  waiting for transfers between devices  334 us (75%)
  starting transfers between devices  36.5 us (8%)
  local copies, waits for them, and re-layouts  21.7 us (5%)
  between operations  15 us (3%)
  other arithmetic  13.9 us (3%)
  matrix products  11.1 us (3%)
  blocking collectives  10.8 us (2%)
    psum x1, waiting for transfers between devices, from_root(): return lax.psum(block, axis)  177 us
    all_to_all x1, waiting for transfers between devices, local(): lax.all_to_all(outgoing.reshape(ep_count, per_owner, model_width), 'ep',...  93.7 us
    all_gather x1, waiting for transfers between devices, local(): portion = lax.all_gather(hidden, 'dp', axis=2, tiled=True)  33.2 us
    all_to_all x1, waiting for transfers between devices, local(): lax.all_to_all(results, 'ep', split_axis=0, concat_axis=0, tiled=True)  30.2 us
    all_to_all x1, starting transfers between devices, local(): lax.all_to_all(outgoing.reshape(ep_count, per_owner, model_width), 'ep',...  21.1 us
    all_to_all x1, starting transfers between devices, local(): lax.all_to_all(results, 'ep', split_axis=0, concat_axis=0, tiled=True)  15.1 us
    all_gather x1, blocking collectives, local(): features = lax.all_gather(tokens, 'dp', axis=1, tiled=True)  10.8 us
  transfers between devices with their start and end apart: 4, of which 4 were waited for; matrix products, arithmetic and copies ran while one was open for 4% of the time, Pallas kernels for 0%

commit v1 on v0

v1 whole, which is shorter than its diff:
```python
import math

import jax
import jax.numpy as jnp
from jax import lax
from jax.sharding import Mesh
from jax.sharding import PartitionSpec as P

HOT = 2
EP = ("eph", "c")


def silu_product(gate_part, up_part):
    return (jax.nn.silu(gate_part) * up_part).astype(jnp.bfloat16)


def local(tokens, expert_ids, gate_probs, gate_weight, up_weight, down_weight):
    pair_count = lax.axis_size("eph")
    ep_count = pair_count * HOT
    dp_count = lax.axis_size("dp")
    parity = lax.axis_index("c")
    ep_index = lax.axis_index("eph") * HOT + parity
    tok_rows, top_count = expert_ids.shape
    exp_dev = gate_weight.shape[0]
    expert_count = exp_dev * ep_count
    hot_load = min(tok_rows * 3 // 4, 4 * tok_rows * top_count // expert_count)
    cold_total = tok_rows * top_count - HOT * hot_load
    capacity = (cold_total + expert_count - HOT - 1) // (expert_count - HOT)
    host_count = pair_count
    spare_slots = max(1, math.ceil(hot_load / host_count))
    primary_slots = exp_dev * capacity

    flat_ids = expert_ids.reshape(-1)
    expert_range = jnp.arange(expert_count, dtype=jnp.int32)
    matches = (flat_ids[:, None] == expert_range[None, :]).astype(jnp.int32)
    expert_loads = jnp.sum(matches, axis=0)
    _, hot_ids = lax.top_k(expert_loads * expert_count + (expert_count - 1 - expert_range), HOT)

    own = (gate_weight[0], up_weight[0], down_weight[0])
    swapped = tuple(lax.ppermute(w, "c", [(0, 1), (1, 0)]) for w in own)
    mine = hot_ids[parity]
    my_expert = ep_index
    sibling_expert = ep_index ^ 1
    take_own = mine == my_expert
    take_sib = mine == sibling_expert
    contrib = tuple(
        jnp.where(take_own, a, jnp.where(take_sib, b, jnp.zeros_like(a)))
        for a, b in zip(own, swapped)
    )
    spare_gate, spare_up, spare_down = (lax.psum(w, "eph") for w in contrib)

    earlier = jnp.cumsum(matches, axis=0) - matches
    order_rank = jnp.sum(earlier * matches, axis=1)
    hot_match = (flat_ids[:, None] == hot_ids[None, :]).astype(jnp.int32)
    is_hot = jnp.sum(hot_match, axis=1) > 0
    which_hot = jnp.sum(hot_match * jnp.arange(HOT, dtype=jnp.int32)[None, :], axis=1)
    spread = (ep_index * hot_load + order_rank) % host_count
    hot_target = (spread * HOT + which_hot) * spare_slots + order_rank // host_count
    cold_target = (
        flat_ids // exp_dev * primary_slots + flat_ids % exp_dev * capacity + order_rank
    )
    pick_row = jnp.arange(tok_rows * top_count, dtype=jnp.int32) // top_count
    primary_total = ep_count * primary_slots
    spare_total = ep_count * spare_slots
    cold_source = jnp.full((primary_total,), tok_rows, jnp.int32)
    cold_source = cold_source.at[jnp.where(is_hot, primary_total, cold_target)].set(
        pick_row, mode="drop"
    )
    hot_source = jnp.full((spare_total,), tok_rows, jnp.int32)
    hot_source = hot_source.at[jnp.where(is_hot, hot_target, spare_total)].set(
        pick_row, mode="drop"
    )

    features = lax.all_gather(tokens, "dp", axis=1, tiled=True)
    model_width = features.shape[1]
    source_row = jnp.concatenate(
        [cold_source.reshape(ep_count, primary_slots), hot_source.reshape(ep_count, spare_slots)],
        axis=1,
    )
    outgoing = jnp.take(features, source_row, axis=0, mode="fill", fill_value=0)
    incoming = lax.all_to_all(outgoing, EP, split_axis=0, concat_axis=0, tiled=True)
    primary_rows = incoming[:, :primary_slots].reshape(ep_count, exp_dev, capacity, model_width)
    spare_rows = incoming[:, primary_slots:]

    gate_primary = jnp.einsum(
        "secd,edf->secf", primary_rows, gate_weight, preferred_element_type=jnp.float32
    )
    up_primary = jnp.einsum(
        "secd,edf->secf", primary_rows, up_weight, preferred_element_type=jnp.float32
    )
    hidden_primary = silu_product(gate_primary, up_primary)
    stacked = jnp.broadcast_to(hidden_primary[None], (dp_count,) + hidden_primary.shape)
    part_primary = lax.all_to_all(stacked, "dp", split_axis=0, concat_axis=0, tiled=True)
    feature_local = down_weight.shape[2]
    down_split = down_weight.reshape(exp_dev, dp_count, -1, feature_local)
    out_primary = jnp.einsum(
        "nsecf,enfd->secd", part_primary, down_split, preferred_element_type=jnp.float32
    ).astype(jnp.bfloat16)
    back_primary = lax.all_to_all(
        out_primary.reshape(ep_count, primary_slots, feature_local),
        EP,
        split_axis=0,
        concat_axis=0,
        tiled=True,
    ).reshape(primary_total, feature_local)

    gate_spare = jnp.einsum(
        "srd,df->srf", spare_rows, spare_gate, preferred_element_type=jnp.float32
    )
    up_spare = jnp.einsum("srd,df->srf", spare_rows, spare_up, preferred_element_type=jnp.float32)
    hidden_spare = silu_product(gate_spare, up_spare)
    part_spare = lax.all_gather(hidden_spare, "dp", axis=2, tiled=True)
    out_spare = jnp.einsum(
        "srf,fd->srd", part_spare, spare_down, preferred_element_type=jnp.float32
    ).astype(jnp.bfloat16)
    back_spare = lax.all_to_all(out_spare, EP, split_axis=0, concat_axis=0, tiled=True).reshape(
        spare_total, feature_local
    )

    returned = jnp.concatenate([back_primary, back_spare], axis=0)
    target = jnp.where(is_hot, primary_total + hot_target, cold_target)
    fetched = jnp.take(returned, target, axis=0).reshape(tok_rows, top_count, feature_local)
    combined = jnp.sum(gate_probs[:, :, None] * fetched.astype(jnp.float32), axis=1)
    return combined.astype(jnp.bfloat16)


def solution(mesh):
    ep_size, dp_size = mesh.devices.shape
    split = Mesh(mesh.devices.reshape(ep_size // HOT, HOT, dp_size), ("eph", "c", "dp"))
    in_specs = (
        P(EP, "dp"),
        P(EP, None),
        P(EP, None),
        P(EP, None, "dp"),
        P(EP, None, "dp"),
        P(EP, None, "dp"),
    )
    out_specs = P(EP, "dp")
    return jax.shard_map(local, mesh=split, in_specs=in_specs, out_specs=out_specs, check_vma=False)
```

time: 443 us -> 386 us (0.87)
  waiting for transfers between devices: 334 us -> 246 us
  starting transfers between devices: 36.5 us -> 53.7 us
  blocking collectives: 10.8 us -> 20.6 us
  local copies, waits for them, and re-layouts: 21.7 us -> 26.9 us
    psum x1, waiting for transfers between devices: 177 us -> 126 us  [local(): spare_gate, spare_up, spare_down = (lax.psum(w, 'eph') for w in contrib)]
    all_gather x1 -> x0, waiting for transfers between devices: 33.2 us -> none  [local(): portion = lax.all_gather(hidden, 'dp', axis=2, tiled=True)]
    all_to_all x2 -> x4, starting transfers between devices: 36.2 us -> 46.3 us  [the longest x1 21.2 us: local(): lax.all_to_all(outgoing, EP, split_axis=0, concat_axis=0, tiled=True)]
    all_gather x0 -> x1, blocking collectives: none -> 10.1 us  [local(): part_spare = lax.all_gather(hidden_spare, 'dp', axis=2, tiled=True)]
    ppermute x0 -> x3, starting transfers between devices: none -> 7.39 us  [local(): swapped = tuple((lax.ppermute(w, 'c', [(0, 1), (1, 0)]) for w in own))]
    all_to_all x2 -> x4, waiting for transfers between devices: 124 us -> 120 us  [the longest x1 89.3 us: local(): lax.all_to_all(outgoing, EP, split_axis=0, concat_axis=0, tiled=True)]
  transfers between devices with their start and end apart: 4 -> 8, of which waited for: 4 -> 4; matrix products, arithmetic and copies ran while one was open for 4% -> 6% of each run, Pallas kernels for 0% -> 0%
where the time goes in v1:
time: 386 us; the launch traced here: 385 us
  waiting for transfers between devices  246 us (64%)
  starting transfers between devices  53.7 us (14%)
  local copies, waits for them, and re-layouts  26.9 us (7%)
  blocking collectives  20.6 us (5%)
  between operations  15.1 us (4%)
  other arithmetic  13.7 us (4%)
  matrix products  9.25 us (2%)
    psum x1, waiting for transfers between devices, local(): spare_gate, spare_up, spare_down = (lax.psum(w, 'eph') for w in contrib)  126 us
    all_to_all x1, waiting for transfers between devices, local(): lax.all_to_all(outgoing, EP, split_axis=0, concat_axis=0, tiled=True)  89.3 us
    all_to_all x1, starting transfers between devices, local(): lax.all_to_all(outgoing, EP, split_axis=0, concat_axis=0, tiled=True)  21.2 us
    all_to_all x1, waiting for transfers between devices, local(): lax.all_to_all(out_primary.reshape(ep_count, primary_slots, feature_local...  19.8 us
    all_to_all x1, starting transfers between devices, local(): lax.all_to_all(out_spare, EP, split_axis=0, concat_axis=0, tiled=True)  15.7 us
    all_to_all x1, waiting for transfers between devices, local(): lax.all_to_all(out_spare, EP, split_axis=0, concat_axis=0, tiled=True)  10.8 us
    all_gather x1, blocking collectives, local(): features = lax.all_gather(tokens, 'dp', axis=1, tiled=True)  10.5 us
    all_gather x1, blocking collectives, local(): part_spare = lax.all_gather(hidden_spare, 'dp', axis=2, tiled=True)  10.1 us
  transfers between devices with their start and end apart: 8, of which 4 were waited for; matrix products, arithmetic and copies ran while one was open for 6% of the time, Pallas kernels for 0%

profile of v1, /device:TPU:1, one launch (start us, length us, event | category | flops | bytes accessed | tf_op | source)
XLA Modules:
  0.0 384.9 jit_solution(6227106666028032948)
XLA Ops:
  8.9 2.5 top_k.11
  11.8 2.4 scatter_custom_fusion
  14.4 2.4 scatter_custom_fusion.1
  17.3 10.5 %all_gather.6 = bf16[64,2048]{1,0:T(8,128)(2,1)S(1)} all-gather(bf16[64,512]{1,0:T(8,128)(2,1)S(1)} %copy-done.4), channel_id=1, replica_groups=mesh['eph'=64,'c'=2,'dp'=4] {'dp'}, dimensions={1}, use_global_device_ids=true | all-gather | bytes 327680 | tf_op jit(solution)/shard_map/all_gather | solution.py:74
  27.9 3.4 gather_fusion
  31.3 2.8 reshape.387
  34.4 4.6 %broadcast_select_fusion = bf16[128,5,2048]{2,1,0:T(8,128)(2,1)} fusion(bf16[128,5,2048]{2,1,0:T(8,128)(2,1)} %reshape.387, pred[128,5]{1,0:T(8,128)(4,1)S(1)} %copy.81), kind=kLoop, calls=%fused_computation.4 | loop fusion | flops 1310720 | bytes 5243520 | tf_op jit(solution)/shard_map/jit(_take)/select_n | solution.py:80
  39.0 21.2 %all-to-all-start = ((bf16[128,5,2048]{2,1,0:T(8,128)(2,1)}), bf16[128,5,2048]{2,1,0:T(8,128)(2,1)}, u32[]{:S(2)}, u32[]{:S(2)}) async-start(bf16[128,5,2048]{2,1,0:T(8,128)(2,1)} %broadcast_select_fusion), calls=%async_computation | async-start | bytes 8388608 | tf_op jit(solution)/shard_map/all_to_all | solution.py:81
  60.3 2.9 collective-permute-start.2
  63.2 1.9 collective-permute-start
  65.1 2.6 collective-permute-start.1
  69.6 1.2 select_select_fusion
  70.8 1.1 select_select_fusion.2
  71.9 1.1 select_select_fusion.1
  73.0 89.3 %all-to-all-done = bf16[128,5,2048]{2,1,0:T(8,128)(2,1)} async-done(((bf16[128,5,2048]{2,1,0:T(8,128)(2,1)}), bf16[128,5,2048]{2,1,0:T(8,128)(2,1)}, u32[]{:S(2)}, u32[]{:S(2)}) %all-to-all-start) | async-done | bytes 2621472 | tf_op jit(solution)/shard_map/all_to_all | solution.py:81
  162.3 3.3 slice.23
  165.6 2.4 fusion.5
  168.0 2.4 fusion.17
  170.4 1.1 broadcast_in_dim.53
  171.5 3.6 all-to-all-start.1
  175.1 3.4 slice.24
  178.5 125.7 %all-reduce.3.cloned.1.call-done = (bf16[2048,256]{1,0:T(8,128)(2,1)}, bf16[2048,256]{1,0:T(8,128)(2,1)}, bf16[1024,512]{1,0:T(8,128)(2,1)}) async-done(((bf16[2048,256]{1,0:T(8,128)(2,1)}, bf16[2048,256]{1,0:T(8,128)(2,1)}, bf16[1024,512]{1,0:T(8,128)(2,1)}), (bf16[2048,256]{1,0:T(8,128)(2,1)}, bf16[2048,256]{1,0:T(8,128)(2,1)}, bf16[1024,512]{1,0:T(8,128)(2,1)})) %all-reduce.3.cloned.1.call-update) | async-done | bytes 3145744 | tf_op jit(solution)/shard_map/psum | solution.py:50
  304.2 1.8 fusion.30
  306.0 1.7 multiply_convert_fusion
  307.6 10.1 %all-gather = bf16[128,1024]{1,0:T(8,128)(2,1)S(1)} all-gather(bf16[128,256]{1,0:T(8,128)(2,1)S(1)} %multiply_convert_fusion), channel_id=2, replica_groups=mesh['eph'=64,'c'=2,'dp'=4] {'dp'}, dimensions={1}, use_global_device_ids=true | all-gather | bytes 327680 | tf_op jit(solution)/shard_map/all_gather | solution.py:112
  319.9 15.7 %all-to-all-start.3 = ((bf16[128,2,256]{2,1,0:T(2,128)(2,1)}), bf16[128,2,256]{2,1,0:T(2,128)(2,1)S(1)}, u32[]{:S(2)}, u32[]{:S(2)}) async-start(bf16[128,2,256]{2,1,0:T(2,128)(2,1)} %reshape.429), calls=%async_computation.3 | async-start | bytes 262144 | tf_op jit(solution)/shard_map/all_to_all | solution.py:116
  336.3 1.2 copy.86
  337.5 10.8 %all-to-all-done.3 = bf16[128,2,256]{2,1,0:T(2,128)(2,1)S(1)} async-done(((bf16[128,2,256]{2,1,0:T(2,128)(2,1)}), bf16[128,2,256]{2,1,0:T(2,128)(2,1)S(1)}, u32[]{:S(2)}, u32[]{:S(2)}) %all-to-all-start.3) | async-done | bytes 131104 | tf_op jit(solution)/shard_map/all_to_all | solution.py:116
  348.3 5.8 %all-to-all-start.2 = ((bf16[128,4,512]{2,1,0:T(4,128)(2,1)}), bf16[128,4,512]{2,1,0:T(4,128)(2,1)S(1)}, u32[]{:S(2)}, u32[]{:S(2)}) async-start(bf16[128,4,512]{2,1,0:T(4,128)(2,1)} %copy.86), calls=%async_computation.2 | async-start | bytes 1048576 | tf_op jit(solution)/shard_map/all_to_all | solution.py:99
  355.0 19.8 %all-to-all-done.2 = bf16[128,4,512]{2,1,0:T(4,128)(2,1)S(1)} async-done(((bf16[128,4,512]{2,1,0:T(4,128)(2,1)}), bf16[128,4,512]{2,1,0:T(4,128)(2,1)S(1)}, u32[]{:S(2)}, u32[]{:S(2)}) %all-to-all-start.2) | async-done | bytes 524320 | tf_op jit(solution)/shard_map/all_to_all | solution.py:99
  375.0 2.0 gather_fusion.1
  377.0 1.1 multiply_reduce_fusion
  (72 shorter events, 8.0 us)
Async XLA Ops:
  6.5 10.8 %copy-start.4 = (bf16[64,512]{1,0:T(8,128)(2,1)S(1)}, bf16[64,512]{1,0:T(8,128)(2,1)}, u32[]{:S(2)}) copy-start(bf16[64,512]{1,0:T(8,128)(2,1)} %param.6) | copy-start | bytes 196612
  39.0 21.3 %copy-start.2 = (bf16[1,1024,512]{2,1,0:T(8,128)(2,1)S(1)}, bf16[1,1024,512]{2,1,0:T(8,128)(2,1)}, u32[]{:S(2)}) copy-start(bf16[1,1024,512]{2,1,0:T(8,128)(2,1)} %param.11) | copy-start | bytes 3145732
  39.0 24.2 %copy-start = (bf16[1,2048,256]{2,1,0:T(8,128)(2,1)S(1)}, bf16[1,2048,256]{2,1,0:T(8,128)(2,1)}, u32[]{:S(2)}) copy-start(bf16[1,2048,256]{2,1,0:T(8,128)(2,1)} %param.9) | copy-start | bytes 3145732
  39.0 26.1 %copy-start.1 = (bf16[1,2048,256]{2,1,0:T(8,128)(2,1)S(1)}, bf16[1,2048,256]{2,1,0:T(8,128)(2,1)}, u32[]{:S(2)}) copy-start(bf16[1,2048,256]{2,1,0:T(8,128)(2,1)} %param.10) | copy-start | bytes 3145732
  39.0 123.3 %all-to-all-start = ((bf16[128,5,2048]{2,1,0:T(8,128)(2,1)}), bf16[128,5,2048]{2,1,0:T(8,128)(2,1)}, u32[]{:S(2)}, u32[]{:S(2)}) async-start(bf16[128,5,2048]{2,1,0:T(8,128)(2,1)} %broadcast_select_fusion), calls=%async_computation | async-start | bytes 8388608 | tf_op jit(solution)/shard_map/all_to_all | solution.py:81
  60.2 244.0 %all-reduce.3.cloned.1.call-start = ((), (), s32[]{:S(2)}) async-start(), calls=%async_computation.4 | async-start | bytes 6291456 | tf_op jit(solution)/shard_map/psum | solution.py:50
  60.3 9.3 %collective-permute-start.2 = (bf16[1024,512]{1,0:T(8,128)(2,1)S(1)}, bf16[1024,512]{1,0:T(8,128)(2,1)}, u32[]{:S(2)}, u32[]{:S(2)}) collective-permute-start(bf16[1024,512]{1,0:T(8,128)(2,1)S(1)} %bitcast.86), channel_id=1, source_target_pairs={{0,4},{4,0},{1,5},{5,1},{2,6},{6,2},{3,7},{7,3},{8,12},{12,8},{9,1... | collective-permute-start | bytes 3145736 | tf_op jit(solution)/shard_map/ppermute | solution.py:40
  63.2 7.6 %collective-permute-start = (bf16[2048,256]{1,0:T(8,128)(2,1)S(1)}, bf16[2048,256]{1,0:T(8,128)(2,1)}, u32[]{:S(2)}, u32[]{:S(2)}) collective-permute-start(bf16[2048,256]{1,0:T(8,128)(2,1)S(1)} %bitcast.84), channel_id=1, source_target_pairs={{0,4},{4,0},{1,5},{5,1},{2,6},{6,2},{3,7},{7,3},{8,12},{12,8},{9,1... | collective-permute-start | bytes 3145736 | tf_op jit(solution)/shard_map/ppermute | solution.py:40
  65.1 6.8 %collective-permute-start.1 = (bf16[2048,256]{1,0:T(8,128)(2,1)S(1)}, bf16[2048,256]{1,0:T(8,128)(2,1)}, u32[]{:S(2)}, u32[]{:S(2)}) collective-permute-start(bf16[2048,256]{1,0:T(8,128)(2,1)S(1)} %bitcast.85), channel_id=1, source_target_pairs={{0,4},{4,0},{1,5},{5,1},{2,6},{6,2},{3,7},{7,3},{8,12},{12,8},{9,1... | collective-permute-start | bytes 3145736 | tf_op jit(solution)/shard_map/ppermute | solution.py:40
  171.5 148.4 %all-to-all-start.1 = ((bf16[4,128,1,4,256]{4,1,3,2,0:T(8,128)(2,1)}), bf16[4,128,1,4,256]{4,1,3,2,0:T(8,128)(2,1)S(1)}, u32[]{:S(2)}, u32[]{:S(2)}) async-start(bf16[4,128,1,4,256]{4,1,3,2,0:T(8,128)(2,1)} %broadcast_in_dim.53), calls=%async_computation.1 | async-start | bytes 2097152 | tf_op jit(solution)/shard_map/all_to_all | solution.py:93
  304.2 13.5 %copy-start.3 = (bf16[1024,512]{1,0:T(8,128)(2,1)S(1)}, bf16[1024,512]{1,0:T(8,128)(2,1)}, u32[]{:S(2)}) copy-start(bf16[1024,512]{1,0:T(8,128)(2,1)} %get-tuple-element.15) | copy-start | bytes 3145732
  319.9 28.4 %all-to-all-start.3 = ((bf16[128,2,256]{2,1,0:T(2,128)(2,1)}), bf16[128,2,256]{2,1,0:T(2,128)(2,1)S(1)}, u32[]{:S(2)}, u32[]{:S(2)}) async-start(bf16[128,2,256]{2,1,0:T(2,128)(2,1)} %reshape.429), calls=%async_computation.3 | async-start | bytes 262144 | tf_op jit(solution)/shard_map/all_to_all | solution.py:116
  335.6 19.0 %copy-start.5 = (s32[64,8]{0,1:T(8,128)S(1)}, s32[64,8]{0,1:T(8,128)}, u32[]{:S(2)}) copy-start(s32[64,8]{0,1:T(8,128)} %param.7) | copy-start | bytes 6148
  335.6 19.2 %copy-start.6 = (f32[64,8]{0,1:T(8,128)S(1)}, f32[64,8]{0,1:T(8,128)}, u32[]{:S(2)}) copy-start(f32[64,8]{0,1:T(8,128)} %param.8) | copy-start | bytes 6148
  348.3 26.5 %all-to-all-start.2 = ((bf16[128,4,512]{2,1,0:T(4,128)(2,1)}), bf16[128,4,512]{2,1,0:T(4,128)(2,1)S(1)}, u32[]{:S(2)}, u32[]{:S(2)}) async-start(bf16[128,4,512]{2,1,0:T(4,128)(2,1)} %copy.86), calls=%async_computation.2 | async-start | bytes 1048576 | tf_op jit(solution)/shard_map/all_to_all | solution.py:99
Sparse Core Ops, SparseCore 0:
  73.1 231.0 all-reduce.2

commit v2 on v1

--- a/solution.py
+++ b/solution.py
@@ -8,6 +8,11 @@
 
 HOT = 2
 EP = ("eph", "c")
+
+
+def gather_dp(x, dp_count):
+    stacked = jnp.broadcast_to(x[None], (dp_count,) + x.shape)
+    return lax.all_to_all(stacked, "dp", split_axis=0, concat_axis=0, tiled=True)
 
 
 def silu_product(gate_part, up_part):
@@ -48,6 +53,7 @@
         for a, b in zip(own, swapped)
     )
     spare_gate, spare_up, spare_down = (lax.psum(w, "eph") for w in contrib)
+    tokens, contrib = lax.optimization_barrier((tokens, contrib))
 
     earlier = jnp.cumsum(matches, axis=0) - matches
     order_rank = jnp.sum(earlier * matches, axis=1)
@@ -71,7 +77,8 @@
         pick_row, mode="drop"
     )
 
-    features = lax.all_gather(tokens, "dp", axis=1, tiled=True)
+    feature_parts = gather_dp(tokens, dp_count)
+    features = jnp.moveaxis(feature_parts, 0, 1).reshape(tok_rows, -1)
     model_width = features.shape[1]
     source_row = jnp.concatenate(
         [cold_source.reshape(ep_count, primary_slots), hot_source.reshape(ep_count, spare_slots)],
@@ -89,8 +96,7 @@
         "secd,edf->secf", primary_rows, up_weight, preferred_element_type=jnp.float32
     )
     hidden_primary = silu_product(gate_primary, up_primary)
-    stacked = jnp.broadcast_to(hidden_primary[None], (dp_count,) + hidden_primary.shape)
-    part_primary = lax.all_to_all(stacked, "dp", split_axis=0, concat_axis=0, tiled=True)
+    part_primary = gather_dp(hidden_primary, dp_count)
     feature_local = down_weight.shape[2]
     down_split = down_weight.reshape(exp_dev, dp_count, -1, feature_local)
     out_primary = jnp.einsum(
@@ -104,14 +110,18 @@
         tiled=True,
     ).reshape(primary_total, feature_local)
 
+    back_primary, spare_gate, spare_up, spare_down = lax.optimization_barrier(
+        (back_primary, spare_gate, spare_up, spare_down)
+    )
     gate_spare = jnp.einsum(
         "srd,df->srf", spare_rows, spare_gate, preferred_element_type=jnp.float32
     )
     up_spare = jnp.einsum("srd,df->srf", spare_rows, spare_up, preferred_element_type=jnp.float32)
     hidden_spare = silu_product(gate_spare, up_spare)
-    part_spare = lax.all_gather(hidden_spare, "dp", axis=2, tiled=True)
+    part_spare = gather_dp(hidden_spare, dp_count)
+    spare_split = spare_down.reshape(dp_count, -1, feature_local)
     out_spare = jnp.einsum(
-        "srf,fd->srd", part_spare, spare_down, preferred_element_type=jnp.float32
+        "nsrf,nfd->srd", part_spare, spare_split, preferred_element_type=jnp.float32
     ).astype(jnp.bfloat16)
     back_spare = lax.all_to_all(out_spare, EP, split_axis=0, concat_axis=0, tiled=True).reshape(
         spare_total, feature_local

time: 386 us -> 375 us (0.972)
  waiting for transfers between devices: 246 us -> 227 us
  starting transfers between devices: 53.7 us -> 63.9 us
  blocking collectives: 20.6 us -> 16.7 us
    psum x1, waiting for transfers between devices: 126 us -> 83.5 us  [local(): spare_gate, spare_up, spare_down = (lax.psum(w, 'eph') for w in contrib)]
    all_gather x2 -> x0, blocking collectives: 20.6 us -> none  [the longest x1 10.5 us: local(): features = lax.all_gather(tokens, 'dp', axis=1, tiled=True)]
    all_to_all x0 -> x1, blocking collectives: none -> 16.7 us  [gather_dp(): lax.all_to_all(stacked, 'dp', split_axis=0, concat_axis=0, tiled=True)]
    all_to_all x1, waiting for transfers between devices: 89.3 us -> 101 us  [local(): lax.all_to_all(outgoing, EP, split_axis=0, concat_axis=0, tiled=True)]
    all_to_all x1 -> x2, waiting for transfers between devices: 0.01 us -> 11.7 us  [gather_dp(): lax.all_to_all(stacked, 'dp', split_axis=0, concat_axis=0, tiled=True)]
    all_to_all x1, starting transfers between devices: 5.78 us -> 14.8 us  [local(): lax.all_to_all(out_primary.reshape(ep_count, primary_slots, feature_local...]
    all_to_all x1, starting transfers between devices: 21.2 us -> 13.4 us  [local(): lax.all_to_all(outgoing, EP, split_axis=0, concat_axis=0, tiled=True)]
    ppermute x3, starting transfers between devices: 7.39 us -> 13.2 us  [local(): swapped = tuple((lax.ppermute(w, 'c', [(0, 1), (1, 0)]) for w in own))]
  transfers between devices with their start and end apart: 8 -> 9, of which waited for: 4 -> 6; matrix products, arithmetic and copies ran while one was open for 6% -> 7% of each run, Pallas kernels for 0% -> 0%
where the time goes in v2:
time: 375 us; the launch traced here: 374 us
  waiting for transfers between devices  227 us (61%)
  starting transfers between devices  63.9 us (17%)
  local copies, waits for them, and re-layouts  27.8 us (7%)
  blocking collectives  16.7 us (4%)
  between operations  15.1 us (4%)
  other arithmetic  13.7 us (4%)
  matrix products  9.2 us (2%)
    all_to_all x1, waiting for transfers between devices, local(): lax.all_to_all(outgoing, EP, split_axis=0, concat_axis=0, tiled=True)  101 us
    psum x1, waiting for transfers between devices, local(): spare_gate, spare_up, spare_down = (lax.psum(w, 'eph') for w in contrib)  83.5 us
    all_to_all x1, waiting for transfers between devices, local(): lax.all_to_all(out_primary.reshape(ep_count, primary_slots, feature_local...  17.8 us
    all_to_all x1, blocking collectives, gather_dp(): lax.all_to_all(stacked, 'dp', split_axis=0, concat_axis=0, tiled=True)  16.7 us
    all_to_all x1, starting transfers between devices, local(): lax.all_to_all(out_spare, EP, split_axis=0, concat_axis=0, tiled=True)  14.8 us
    all_to_all x1, starting transfers between devices, local(): lax.all_to_all(out_primary.reshape(ep_count, primary_slots, feature_local...  14.8 us
    all_to_all x1, starting transfers between devices, local(): lax.all_to_all(outgoing, EP, split_axis=0, concat_axis=0, tiled=True)  13.4 us
    ppermute x3, starting transfers between devices, local(): swapped = tuple((lax.ppermute(w, 'c', [(0, 1), (1, 0)]) for w in own))  13.2 us
  transfers between devices with their start and end apart: 9, of which 6 were waited for; matrix products, arithmetic and copies ran while one was open for 7% of the time, Pallas kernels for 0%

profile of v2, /device:TPU:1, one launch (start us, length us, event | category | flops | bytes accessed | tf_op | source)
XLA Modules:
  0.0 373.7 jit_solution(7552274465848636188)
XLA Ops:
  6.5 8.9 %collective-permute-start.2 = (bf16[1024,512]{1,0:T(8,128)(2,1)}, bf16[1024,512]{1,0:T(8,128)(2,1)}, u32[]{:S(2)}, u32[]{:S(2)}) collective-permute-start(bf16[1024,512]{1,0:T(8,128)(2,1)} %bitcast.97), channel_id=1, source_target_pairs={{0,4},{4,0},{1,5},{5,1},{2,6},{6,2},{3,7},{7,3},{8,12},{12,8},{9,1... | collective-permute-start | bytes 3145736 | tf_op jit(solution)/shard_map/ppermute | solution.py:45
  15.5 1.9 collective-permute-start.1
  17.4 2.4 collective-permute-start
  22.1 2.5 top_k.11
  25.0 2.4 scatter_custom_fusion
  29.6 2.4 scatter_custom_fusion.1
  32.5 1.2 select_select_fusion
  33.7 1.1 select_select_fusion.1
  35.3 1.1 select_select_fusion.2
  37.2 3.4 all-to-all-start
  40.7 6.6 %all-to-all-done = bf16[4,64,512]{2,1,0:T(8,128)(2,1)S(1)} async-done(((bf16[4,64,512]{2,1,0:T(8,128)(2,1)}), bf16[4,64,512]{2,1,0:T(8,128)(2,1)S(1)}, u32[]{:S(2)}, u32[]{:S(2)}) %all-to-all-start) | async-done | bytes 262176 | tf_op jit(solution)/shard_map/all_to_all | solution.py:15
  47.4 3.4 gather_fusion
  50.8 2.8 reshape.394
  53.7 4.6 %broadcast_select_fusion = bf16[128,5,2048]{2,1,0:T(8,128)(2,1)} fusion(bf16[128,5,2048]{2,1,0:T(8,128)(2,1)} %reshape.394, pred[128,5]{1,0:T(8,128)(4,1)S(1)} %copy.84), kind=kLoop, calls=%fused_computation.4 | loop fusion | flops 1310720 | bytes 5243520 | tf_op jit(solution)/shard_map/jit(_take)/select_n | solution.py:87
  58.3 13.4 %all-to-all-start.1 = ((bf16[128,5,2048]{2,1,0:T(8,128)(2,1)}), bf16[128,5,2048]{2,1,0:T(8,128)(2,1)}, u32[]{:S(2)}, u32[]{:S(2)}) async-start(bf16[128,5,2048]{2,1,0:T(8,128)(2,1)} %broadcast_select_fusion), calls=%async_computation.1 | async-start | bytes 8388608 | tf_op jit(solution)/shard_map/all_to_all | solution.py:88
  72.5 101.4 %all-to-all-done.1 = bf16[128,5,2048]{2,1,0:T(8,128)(2,1)} async-done(((bf16[128,5,2048]{2,1,0:T(8,128)(2,1)}), bf16[128,5,2048]{2,1,0:T(8,128)(2,1)}, u32[]{:S(2)}, u32[]{:S(2)}) %all-to-all-start.1) | async-done | bytes 2621472 | tf_op jit(solution)/shard_map/all_to_all | solution.py:88
  173.9 3.2 slice.23
  177.1 2.4 fusion.5
  179.5 2.4 fusion.17
  182.0 16.7 %all_to_all.30 = bf16[4,128,1,4,256]{4,1,3,2,0:T(8,128)(2,1)S(1)} all-to-all(bf16[4,128,1,4,256]{4,1,3,2,0:T(8,128)(2,1)S(1)} %broadcast_in_dim.67), channel_id=1, replica_groups=mesh['eph'=64,'c'=2,'dp'=4] {'dp'}, dimensions={0} | all-to-all | bytes 2097152 | tf_op jit(solution)/shard_map/all_to_all | solution.py:15
  199.4 1.2 copy.90
  200.6 14.8 %all-to-all-start.3 = ((bf16[128,4,512]{2,1,0:T(4,128)(2,1)}), bf16[128,4,512]{2,1,0:T(4,128)(2,1)S(1)}, u32[]{:S(2)}, u32[]{:S(2)}) async-start(bf16[128,4,512]{2,1,0:T(4,128)(2,1)} %copy.90), calls=%async_computation.3 | async-start | bytes 1048576 | tf_op jit(solution)/shard_map/all_to_all | solution.py:105
  215.4 3.4 slice.24
  218.9 17.8 %all-to-all-done.3 = bf16[128,4,512]{2,1,0:T(4,128)(2,1)S(1)} async-done(((bf16[128,4,512]{2,1,0:T(4,128)(2,1)}), bf16[128,4,512]{2,1,0:T(4,128)(2,1)S(1)}, u32[]{:S(2)}, u32[]{:S(2)}) %all-to-all-start.3) | async-done | bytes 524320 | tf_op jit(solution)/shard_map/all_to_all | solution.py:105
  236.8 83.5 %all-reduce.3.cloned.1.call-done = (bf16[2048,256]{1,0:T(8,128)(2,1)}, bf16[2048,256]{1,0:T(8,128)(2,1)}, bf16[1024,512]{1,0:T(8,128)(2,1)}) async-done(((bf16[2048,256]{1,0:T(8,128)(2,1)}, bf16[2048,256]{1,0:T(8,128)(2,1)}, bf16[1024,512]{1,0:T(8,128)(2,1)}), (bf16[2048,256]{1,0:T(8,128)(2,1)}, bf16[2048,256]{1,0:T(8,128)(2,1)}, bf16[1024,512]{1,0:T(8,128)(2,1)})) %all-reduce.3.cloned.1.call-update) | async-done | bytes 3145744 | tf_op jit(solution)/shard_map/psum | solution.py:55
  320.2 1.8 fusion.32
  322.0 1.7 fusion.22
  324.4 4.0 %all-to-all-start.4 = ((bf16[4,128,1,256]{3,1,2,0:T(8,128)(2,1)}), bf16[4,128,1,256]{3,1,2,0:T(8,128)(2,1)S(1)}, u32[]{:S(2)}, u32[]{:S(2)}) async-start(bf16[4,128,1,256]{3,1,2,0:T(8,128)(2,1)} %broadcast_in_dim.68), calls=%async_computation.4 | async-start | bytes 524288 | tf_op jit(solution)/shard_map/all_to_all | solution.py:15
  328.9 5.1 %all-to-all-done.4 = bf16[4,128,1,256]{3,1,2,0:T(8,128)(2,1)S(1)} async-done(((bf16[4,128,1,256]{3,1,2,0:T(8,128)(2,1)}), bf16[4,128,1,256]{3,1,2,0:T(8,128)(2,1)S(1)}, u32[]{:S(2)}, u32[]{:S(2)}) %all-to-all-start.4) | async-done | bytes 262176 | tf_op jit(solution)/shard_map/all_to_all | solution.py:15
  336.1 14.8 %all-to-all-start.5 = ((bf16[128,2,256]{2,1,0:T(2,128)(2,1)}), bf16[128,2,256]{2,1,0:T(2,128)(2,1)S(1)}, u32[]{:S(2)}, u32[]{:S(2)}) async-start(bf16[128,2,256]{2,1,0:T(2,128)(2,1)} %reshape.435), calls=%async_computation.5 | async-start | bytes 262144 | tf_op jit(solution)/shard_map/all_to_all | solution.py:126
  351.2 12.5 %all-to-all-done.5 = bf16[128,2,256]{2,1,0:T(2,128)(2,1)S(1)} async-done(((bf16[128,2,256]{2,1,0:T(2,128)(2,1)}), bf16[128,2,256]{2,1,0:T(2,128)(2,1)S(1)}, u32[]{:S(2)}, u32[]{:S(2)}) %all-to-all-start.5) | async-done | bytes 131104 | tf_op jit(solution)/shard_map/all_to_all | solution.py:126
  363.8 2.0 gather_fusion.1
  (82 shorter events, 11.7 us)
Async XLA Ops:
  6.5 26.0 %copy-start.4 = (bf16[1,1024,512]{2,1,0:T(8,128)(2,1)S(1)}, bf16[1,1024,512]{2,1,0:T(8,128)(2,1)}, u32[]{:S(2)}) copy-start(bf16[1,1024,512]{2,1,0:T(8,128)(2,1)} %param.11) | copy-start | bytes 3145732
  6.5 26.0 %collective-permute-start.2 = (bf16[1024,512]{1,0:T(8,128)(2,1)}, bf16[1024,512]{1,0:T(8,128)(2,1)}, u32[]{:S(2)}, u32[]{:S(2)}) collective-permute-start(bf16[1024,512]{1,0:T(8,128)(2,1)} %bitcast.97), channel_id=1, source_target_pairs={{0,4},{4,0},{1,5},{5,1},{2,6},{6,2},{3,7},{7,3},{8,12},{12,8},{9,1... | collective-permute-start | bytes 3145736 | tf_op jit(solution)/shard_map/ppermute | solution.py:45
  15.5 18.3 %collective-permute-start.1 = (bf16[2048,256]{1,0:T(8,128)(2,1)}, bf16[2048,256]{1,0:T(8,128)(2,1)}, u32[]{:S(2)}, u32[]{:S(2)}) collective-permute-start(bf16[2048,256]{1,0:T(8,128)(2,1)} %bitcast.96), channel_id=1, source_target_pairs={{0,4},{4,0},{1,5},{5,1},{2,6},{6,2},{3,7},{7,3},{8,12},{12,8},{9,1... | collective-permute-start | bytes 3145736 | tf_op jit(solution)/shard_map/ppermute | solution.py:45
  17.4 17.5 %collective-permute-start = (bf16[2048,256]{1,0:T(8,128)(2,1)}, bf16[2048,256]{1,0:T(8,128)(2,1)S(1)}, u32[]{:S(2)}, u32[]{:S(2)}) collective-permute-start(bf16[2048,256]{1,0:T(8,128)(2,1)} %bitcast.95), channel_id=1, source_target_pairs={{0,4},{4,0},{1,5},{5,1},{2,6},{6,2},{3,7},{7,3},{8,12},{12,8},{9,1... | collective-permute-start | bytes 3145736 | tf_op jit(solution)/shard_map/ppermute | solution.py:45
  21.9 11.8 %copy-start.2 = (bf16[1,2048,256]{2,1,0:T(8,128)(2,1)S(1)}, bf16[1,2048,256]{2,1,0:T(8,128)(2,1)}, u32[]{:S(2)}) copy-start(bf16[1,2048,256]{2,1,0:T(8,128)(2,1)} %param.10) | copy-start | bytes 3145732
  33.7 1.6 copy-start
  34.8 1.6 copy-start.7
  37.2 10.2 %all-to-all-start = ((bf16[4,64,512]{2,1,0:T(8,128)(2,1)}), bf16[4,64,512]{2,1,0:T(8,128)(2,1)S(1)}, u32[]{:S(2)}, u32[]{:S(2)}) async-start(bf16[4,64,512]{2,1,0:T(8,128)(2,1)} %broadcast_in_dim.64), calls=%async_computation | async-start | bytes 524288 | tf_op jit(solution)/shard_map/all_to_all | solution.py:15
  58.3 115.6 %all-to-all-start.1 = ((bf16[128,5,2048]{2,1,0:T(8,128)(2,1)}), bf16[128,5,2048]{2,1,0:T(8,128)(2,1)}, u32[]{:S(2)}, u32[]{:S(2)}) async-start(bf16[128,5,2048]{2,1,0:T(8,128)(2,1)} %broadcast_select_fusion), calls=%async_computation.1 | async-start | bytes 8388608 | tf_op jit(solution)/shard_map/all_to_all | solution.py:88
  71.7 248.5 %all-reduce.3.cloned.1.call-start = ((), (), s32[]{:S(2)}) async-start(), calls=%async_computation.6 | async-start | bytes 6291456 | tf_op jit(solution)/shard_map/psum | solution.py:55
  72.5 104.7 %copy-start.1 = (bf16[1,2048,256]{2,1,0:T(8,128)(2,1)S(1)}, bf16[1,2048,256]{2,1,0:T(8,128)(2,1)}, u32[]{:S(2)}) copy-start(bf16[1,2048,256]{2,1,0:T(8,128)(2,1)} %param.9) | copy-start | bytes 3145732
  177.1 2.4 copy-start.3
  181.9 16.8 %copy-start.5 = (bf16[1,1024,512]{2,1,0:T(8,128)(2,1)S(1)}, bf16[1,1024,512]{2,1,0:T(8,128)(2,1)}, u32[]{:S(2)}) copy-start(bf16[1,1024,512]{2,1,0:T(8,128)(2,1)} %param.11) | copy-start | bytes 3145732
  200.6 36.0 %all-to-all-start.3 = ((bf16[128,4,512]{2,1,0:T(4,128)(2,1)}), bf16[128,4,512]{2,1,0:T(4,128)(2,1)S(1)}, u32[]{:S(2)}, u32[]{:S(2)}) async-start(bf16[128,4,512]{2,1,0:T(4,128)(2,1)} %copy.90), calls=%async_computation.3 | async-start | bytes 1048576 | tf_op jit(solution)/shard_map/all_to_all | solution.py:105
  320.2 13.7 %copy-start.6 = (bf16[1024,512]{1,0:T(8,128)(2,1)S(1)}, bf16[1024,512]{1,0:T(8,128)(2,1)}, u32[]{:S(2)}) copy-start(bf16[1024,512]{1,0:T(8,128)(2,1)} %get-tuple-element.18) | copy-start | bytes 3145732
  323.7 27.2 %copy-start.8 = (s32[64,8]{0,1:T(8,128)S(1)}, s32[64,8]{0,1:T(8,128)}, u32[]{:S(2)}) copy-start(s32[64,8]{0,1:T(8,128)} %param.7) | copy-start | bytes 6148
  323.7 27.4 %copy-start.9 = (f32[64,8]{0,1:T(8,128)S(1)}, f32[64,8]{0,1:T(8,128)}, u32[]{:S(2)}) copy-start(f32[64,8]{0,1:T(8,128)} %param.8) | copy-start | bytes 6148
  324.4 9.5 %all-to-all-start.4 = ((bf16[4,128,1,256]{3,1,2,0:T(8,128)(2,1)}), bf16[4,128,1,256]{3,1,2,0:T(8,128)(2,1)S(1)}, u32[]{:S(2)}, u32[]{:S(2)}) async-start(bf16[4,128,1,256]{3,1,2,0:T(8,128)(2,1)} %broadcast_in_dim.68), calls=%async_computation.4 | async-start | bytes 524288 | tf_op jit(solution)/shard_map/all_to_all | solution.py:15
  336.1 27.6 %all-to-all-start.5 = ((bf16[128,2,256]{2,1,0:T(2,128)(2,1)}), bf16[128,2,256]{2,1,0:T(2,128)(2,1)S(1)}, u32[]{:S(2)}, u32[]{:S(2)}) async-start(bf16[128,2,256]{2,1,0:T(2,128)(2,1)} %reshape.435), calls=%async_computation.5 | async-start | bytes 262144 | tf_op jit(solution)/shard_map/all_to_all | solution.py:126
Sparse Core Ops, SparseCore 0:
  76.2 243.9 all-reduce.2

commit v3 on v2

--- a/solution.py
+++ b/solution.py
@@ -1,4 +1,4 @@
-import math
+import functools
 
 import jax
 import jax.numpy as jnp
@@ -10,6 +10,44 @@
 EP = ("eph", "c")
 
 
+def copy_plan(mesh):
+    column = mesh.devices[:, 0]
+    place = {}
+    for index, device in enumerate(column):
+        coords = getattr(device, "coords", None)
+        core = getattr(device, "core_on_chip", index % HOT)
+        if coords is None:
+            side = int(round((len(column) // HOT) ** 0.5))
+            coords = (0, index // HOT % side, index // HOT // side)
+        place[(coords[1], coords[2], core)] = index
+    ys = 1 + max(key[0] for key in place)
+    zs = 1 + max(key[1] for key in place)
+
+    def at(y, z, c):
+        return place[(y % ys, z % zs, c)]
+
+    anchors, hosts, round_one, round_two = [], [], [[] for _ in range(5)], [[], []]
+    for y0, z0 in ((0, 0), (ys // 2, zs // 2)):
+        a = at(y0, z0, 0)
+        first = [at(y0, z0, 1), at(y0 + 1, z0, 0), at(y0 - 1, z0, 0), at(y0, z0 + 1, 0), at(y0, z0 - 1, 0)]
+        for k, dst in enumerate(first):
+            round_one[k].append((a, dst))
+        sib, yp, ym, zp, zm = first
+        second_a = [
+            (yp, at(y0 + 1, z0, 1)), (ym, at(y0 - 1, z0, 1)), (zp, at(y0, z0 + 1, 1)),
+            (zm, at(y0, z0 - 1, 1)), (a, at(y0, z0 + 2, 0)), (sib, at(y0, z0 - 2, 1)),
+        ]
+        second_b = [
+            (yp, at(y0 + 2, z0, 0)), (ym, at(y0 - 2, z0, 0)), (zp, at(y0 + 1, z0 + 1, 0)),
+            (zm, at(y0 - 1, z0 - 1, 0)),
+        ]
+        round_two[0].extend(second_a)
+        round_two[1].extend(second_b)
+        anchors.append(a)
+        hosts.append([a] + first + [d for _, d in second_a] + [d for _, d in second_b])
+    return anchors, hosts, round_one, round_two
+
+
 def gather_dp(x, dp_count):
     stacked = jnp.broadcast_to(x[None], (dp_count,) + x.shape)
     return lax.all_to_all(stacked, "dp", split_axis=0, concat_axis=0, tiled=True)
@@ -19,7 +57,7 @@
     return (jax.nn.silu(gate_part) * up_part).astype(jnp.bfloat16)
 
 
-def local(tokens, expert_ids, gate_probs, gate_weight, up_weight, down_weight):
+def local(plan, tokens, expert_ids, gate_probs, gate_weight, up_weight, down_weight):
     pair_count = lax.axis_size("eph")
     ep_count = pair_count * HOT
     dp_count = lax.axis_size("dp")
@@ -31,8 +69,8 @@
     hot_load = min(tok_rows * 3 // 4, 4 * tok_rows * top_count // expert_count)
     cold_total = tok_rows * top_count - HOT * hot_load
     capacity = (cold_total + expert_count - HOT - 1) // (expert_count - HOT)
-    host_count = pair_count
-    spare_slots = max(1, math.ceil(hot_load / host_count))
+    spare_slots = 1
+    model_rows = gate_weight.shape[1]
     primary_slots = exp_dev * capacity
 
     flat_ids = expert_ids.reshape(-1)
@@ -41,27 +79,40 @@
     expert_loads = jnp.sum(matches, axis=0)
     _, hot_ids = lax.top_k(expert_loads * expert_count + (expert_count - 1 - expert_range), HOT)
 
-    own = (gate_weight[0], up_weight[0], down_weight[0])
-    swapped = tuple(lax.ppermute(w, "c", [(0, 1), (1, 0)]) for w in own)
-    mine = hot_ids[parity]
-    my_expert = ep_index
-    sibling_expert = ep_index ^ 1
-    take_own = mine == my_expert
-    take_sib = mine == sibling_expert
-    contrib = tuple(
-        jnp.where(take_own, a, jnp.where(take_sib, b, jnp.zeros_like(a)))
-        for a, b in zip(own, swapped)
-    )
-    spare_gate, spare_up, spare_down = (lax.psum(w, "eph") for w in contrib)
-    tokens, contrib = lax.optimization_barrier((tokens, contrib))
+    anchors, hosts, round_one, round_two = plan
+    assert len(hosts[0]) == hot_load
+    own = jnp.concatenate(
+        [gate_weight[0], up_weight[0], down_weight[0].reshape(-1, gate_weight.shape[2])], axis=0
+    )
+    held = jnp.zeros_like(own)
+    for position in range(HOT):
+        anchor = anchors[position]
+
+        def move(w, source, anchor=anchor):
+            if source == anchor:
+                return w
+            return lax.ppermute(w, EP, [(source, anchor)])
+
+        branches = [lambda w, source=source: move(w, source) for source in range(ep_count)]
+        moved = lax.switch(hot_ids[position], branches, own)
+        held = jnp.where(ep_index == anchor, moved, held)
+    tokens, held = lax.optimization_barrier((tokens, held))
+    for stage in (round_one, round_two):
+        received = [lax.ppermute(held, EP, pairs) for pairs in stage]
+        for pairs, value in zip(stage, received):
+            takers = jnp.array([d for _, d in pairs], jnp.int32)
+            held = jnp.where(jnp.any(takers == ep_index), value, held)
+    spare_gate = held[:model_rows]
+    spare_up = held[model_rows : 2 * model_rows]
+    spare_down = held[2 * model_rows :].reshape(down_weight.shape[1], down_weight.shape[2])
+    host_table = jnp.array(hosts, jnp.int32)
 
     earlier = jnp.cumsum(matches, axis=0) - matches
     order_rank = jnp.sum(earlier * matches, axis=1)
     hot_match = (flat_ids[:, None] == hot_ids[None, :]).astype(jnp.int32)
     is_hot = jnp.sum(hot_match, axis=1) > 0
     which_hot = jnp.sum(hot_match * jnp.arange(HOT, dtype=jnp.int32)[None, :], axis=1)
-    spread = (ep_index * hot_load + order_rank) % host_count
-    hot_target = (spread * HOT + which_hot) * spare_slots + order_rank // host_count
+    hot_target = host_table[which_hot, order_rank] * spare_slots
     cold_target = (
         flat_ids // exp_dev * primary_slots + flat_ids % exp_dev * capacity + order_rank
     )
@@ -146,4 +197,5 @@
         P(EP, None, "dp"),
     )
     out_specs = P(EP, "dp")
-    return jax.shard_map(local, mesh=split, in_specs=in_specs, out_specs=out_specs, check_vma=False)
+    plan = copy_plan(mesh)
+    return jax.shard_map(functools.partial(local, plan), mesh=split, in_specs=in_specs, out_specs=out_specs, check_vma=False)

time: 375 us -> 505 us (1.35); the launches traced: 374 us -> 496 us
  starting transfers between devices: 63.9 us -> 321 us
  waiting for transfers between devices: 227 us -> 97.9 us
  blocking collectives: 16.7 us -> 0 us
  between operations: 15.1 us -> 2.3 us
  local copies, waits for them, and re-layouts: 27.8 us -> 38.7 us
  other arithmetic: 13.7 us -> 24.4 us
    ppermute x3 -> x9, starting transfers between devices: 13.2 us -> 232 us  [the longest x7 158 us: local(): received = [lax.ppermute(held, EP, pairs) for pairs in stage]]
    psum x1 -> x0, waiting for transfers between devices: 83.5 us -> none  [local(): spare_gate, spare_up, spare_down = (lax.psum(w, 'eph') for w in contrib)]
    all_to_all x1, waiting for transfers between devices: 101 us -> 53.4 us  [local(): lax.all_to_all(outgoing, EP, split_axis=0, concat_axis=0, tiled=True)]
    all_to_all x1, starting transfers between devices: 14.8 us -> 52.3 us  [local(): lax.all_to_all(out_primary.reshape(ep_count, primary_slots, feature_local...]
    all_to_all x1 -> x0, blocking collectives: 16.7 us -> none  [gather_dp(): lax.all_to_all(stacked, 'dp', split_axis=0, concat_axis=0, tiled=True)]
    all_to_all x1, starting transfers between devices: 14.8 us -> 5.62 us  [local(): lax.all_to_all(out_spare, EP, split_axis=0, concat_axis=0, tiled=True)]
    select_n x4 -> x3, other arithmetic: 3.44 us -> 9.22 us  [the longest x2 7.22 us: local(): held = jnp.where(jnp.any(takers == ep_index), value, held)]
    all_to_all x1, starting transfers between devices: 13.4 us -> 18.7 us  [local(): lax.all_to_all(outgoing, EP, split_axis=0, concat_axis=0, tiled=True)]
  transfers between devices with their start and end apart: 9 -> 15, of which waited for: 6 -> 5; matrix products, arithmetic and copies ran while one was open for 7% -> 10% of each run, Pallas kernels for 0% -> 0%
where the time goes in v3:
time: 505 us; the launch traced here: 496 us
  starting transfers between devices  321 us (64%)
  waiting for transfers between devices  97.9 us (19%)
  local copies, waits for them, and re-layouts  38.7 us (8%)
  other arithmetic  24.4 us (5%)
  matrix products  10.9 us (2%)
    ppermute x7, starting transfers between devices, local(): received = [lax.ppermute(held, EP, pairs) for pairs in stage]  158 us
    ppermute x2, starting transfers between devices, move(): return lax.ppermute(w, EP, [(source, anchor)])  74 us
    all_to_all x1, waiting for transfers between devices, local(): lax.all_to_all(outgoing, EP, split_axis=0, concat_axis=0, tiled=True)  53.4 us
    all_to_all x1, starting transfers between devices, local(): lax.all_to_all(out_primary.reshape(ep_count, primary_slots, feature_local...  52.3 us
    all_to_all x1, starting transfers between devices, local(): lax.all_to_all(outgoing, EP, split_axis=0, concat_axis=0, tiled=True)  18.7 us
    all_to_all x1, waiting for transfers between devices, local(): lax.all_to_all(out_primary.reshape(ep_count, primary_slots, feature_local...  16.8 us
    all_to_all x3, waiting for transfers between devices, gather_dp(): lax.all_to_all(stacked, 'dp', split_axis=0, concat_axis=0, tiled=True)  15.3 us
    all_to_all x1, waiting for transfers between devices, local(): lax.all_to_all(out_spare, EP, split_axis=0, concat_axis=0, tiled=True)  12.4 us
  transfers between devices with their start and end apart: 15, of which 5 were waited for; matrix products, arithmetic and copies ran while one was open for 10% of the time, Pallas kernels for 0%

profile of v3, /device:TPU:1, one launch (start us, length us, event | category | flops | bytes accessed | tf_op | source)
XLA Modules:
  0.0 495.6 jit_solution(8788376932306342745)
XLA Ops:
  1.6 2.5 top_k.11
  10.4 20.8 %conditional.2 = (bf16[6144,256]{1,0:T(8,128)(2,1)}) conditional(s32[]{:T(128)} %bitcast.10, bf16[6144,256]{1,0:T(8,128)(2,1)S(1)} %pad_maximum_fusion, bf16[6144,256]{1,0:T(8,128)(2,1)S(1)} %pad_maximum_fusion, bf16[6144,256]{1,0:T(8,128)(2,1)S(1)} %pad_maximum_fusion, ...), branch_computations={%region_9.0_spmd, %region_10.0_spmd, %region_11.0_spmd, %region_12... | conditional | bytes 12582960 | solution.py:97
  10.5 20.6 %collective-permute-start.112 = (bf16[6144,256]{1,0:T(8,128)(2,1)S(1)}, bf16[6144,256]{1,0:T(8,128)(2,1)}, u32[]{:S(2)}, u32[]{:S(2)}) collective-permute-start(bf16[6144,256]{1,0:T(8,128)(2,1)S(1)} %param.113), channel_id=1, source_target_pairs={{452,288},{453,289},{454,290},{455,291}} | collective-permute-start | bytes 9437192 | tf_op jit(solution)/shard_map/cond/branch_113_fun/ppermute | solution.py:94
  31.2 53.5 %conditional.3 = (bf16[6144,256]{1,0:T(8,128)(2,1)}) conditional(s32[]{:T(128)} %bitcast.13, bf16[6144,256]{1,0:T(8,128)(2,1)S(1)} %pad_maximum_fusion, bf16[6144,256]{1,0:T(8,128)(2,1)S(1)} %pad_maximum_fusion, bf16[6144,256]{1,0:T(8,128)(2,1)S(1)} %pad_maximum_fusion, ...), branch_computations={%region_137.138_spmd, %region_138.139_spmd, %region_139.140_spmd, ... | conditional | bytes 12582960 | solution.py:97
  31.3 53.4 %collective-permute-start.210 = (bf16[6144,256]{1,0:T(8,128)(2,1)S(1)}, bf16[6144,256]{1,0:T(8,128)(2,1)}, u32[]{:S(2)}, u32[]{:S(2)}) collective-permute-start(bf16[6144,256]{1,0:T(8,128)(2,1)S(1)} %param.212), channel_id=1, source_target_pairs={{336,0},{337,1},{338,2},{339,3}} | collective-permute-start | bytes 9437192 | tf_op jit(solution)/shard_map/cond/branch_84_fun/ppermute | solution.py:94
  86.7 51.0 %collective-permute-start.254 = (bf16[6144,256]{1,0:T(8,128)(2,1)}, bf16[6144,256]{1,0:T(8,128)(2,1)}, u32[]{:S(2)}, u32[]{:S(2)}) collective-permute-start(bf16[6144,256]{1,0:T(8,128)(2,1)} %select_select_fusion.2), channel_id=1, source_target_pairs={{0,448},{288,224},{1,449},{289,225},{2,450},{290,226},{3,451},{291... | collective-permute-start | bytes 9437192 | tf_op jit(solution)/shard_map/ppermute | solution.py:101
  137.7 18.4 %collective-permute-start.255 = (bf16[6144,256]{1,0:T(8,128)(2,1)}, bf16[6144,256]{1,0:T(8,128)(2,1)}, u32[]{:S(2)}, u32[]{:S(2)}) collective-permute-start(bf16[6144,256]{1,0:T(8,128)(2,1)} %select_select_fusion.2), channel_id=1, source_target_pairs={{0,64},{288,352},{1,65},{289,353},{2,66},{290,354},{3,67},{291,355}} | collective-permute-start | bytes 9437192 | tf_op jit(solution)/shard_map/ppermute | solution.py:101
  156.1 18.4 %collective-permute-start.256 = (bf16[6144,256]{1,0:T(8,128)(2,1)}, bf16[6144,256]{1,0:T(8,128)(2,1)}, u32[]{:S(2)}, u32[]{:S(2)}) collective-permute-start(bf16[6144,256]{1,0:T(8,128)(2,1)} %select_select_fusion.2), channel_id=1, source_target_pairs={{0,56},{288,280},{1,57},{289,281},{2,58},{290,282},{3,59},{291,283}} | collective-permute-start | bytes 9437192 | tf_op jit(solution)/shard_map/ppermute | solution.py:101
  174.5 18.5 %collective-permute-start.257 = (bf16[6144,256]{1,0:T(8,128)(2,1)}, bf16[6144,256]{1,0:T(8,128)(2,1)}, u32[]{:S(2)}, u32[]{:S(2)}) collective-permute-start(bf16[6144,256]{1,0:T(8,128)(2,1)} %select_select_fusion.2), channel_id=1, source_target_pairs={{0,8},{288,296},{1,9},{289,297},{2,10},{290,298},{3,11},{291,299}} | collective-permute-start | bytes 9437192 | tf_op jit(solution)/shard_map/ppermute | solution.py:101
  193.0 16.7 %collective-permute-start.258 = (bf16[6144,256]{1,0:T(8,128)(2,1)}, bf16[6144,256]{1,0:T(8,128)(2,1)}, u32[]{:S(2)}, u32[]{:S(2)}) collective-permute-start(bf16[6144,256]{1,0:T(8,128)(2,1)} %select_select_fusion.2), channel_id=1, source_target_pairs={{0,4},{288,292},{1,5},{289,293},{2,6},{290,294},{3,7},{291,295}} | collective-permute-start | bytes 9437192 | tf_op jit(solution)/shard_map/ppermute | solution.py:101
  210.4 4.2 all-to-all-start
  214.8 4.8 gather_fusion
  219.6 2.4 scatter_custom_fusion
  222.3 2.5 scatter_custom_fusion.1
  225.4 3.4 gather_fusion.1
  228.8 2.9 reshape.344
  231.7 4.6 broadcast_select_fusion
  236.4 18.7 %all-to-all-start.1 = ((bf16[128,5,2048]{2,1,0:T(8,128)(2,1)}), bf16[128,5,2048]{2,1,0:T(8,128)(2,1)}, u32[]{:S(2)}, u32[]{:S(2)}) async-start(bf16[128,5,2048]{2,1,0:T(8,128)(2,1)} %broadcast_select_fusion), calls=%async_computation.1 | async-start | bytes 8388608 | tf_op jit(solution)/shard_map/all_to_all | solution.py:139
  257.2 5.5 %select_select_fusion.1 = bf16[6144,256]{1,0:T(8,128)(2,1)S(1)} fusion(bf16[6144,256]{1,0:T(8,128)(2,1)} %collective-permute-done.254, bf16[6144,256]{1,0:T(8,128)(2,1)} %collective-permute-done.255, bf16[6144,256]{1,0:T(8,128)(2,1)} %collective-permute-done.256, bf16[6144,256]{1,0:T(8,128)(2,1)} %collective-permute-done.257, ...), kind=kLoop, calls=%fused_computation.8 | loop fusion | flops 7864320 | bytes 22020100 | tf_op jit(solution)/shard_map/jit(_where)/select_n | solution.py:104
  262.8 16.5 %collective-permute-start.259 = (bf16[6144,256]{1,0:T(8,128)(2,1)S(1)}, bf16[6144,256]{1,0:T(8,128)(2,1)}, u32[]{:S(2)}, u32[]{:S(2)}) collective-permute-start(bf16[6144,256]{1,0:T(8,128)(2,1)S(1)} %select_select_fusion.1), channel_id=1, source_target_pairs={{8,16},{56,48},{64,72},{448,504},{296,304},{280,272},{352,360},{22... | collective-permute-start | bytes 9437192 | tf_op jit(solution)/shard_map/ppermute | solution.py:101
  279.3 18.9 %collective-permute-start.260 = (bf16[6144,256]{1,0:T(8,128)(2,1)S(1)}, bf16[6144,256]{1,0:T(8,128)(2,1)}, u32[]{:S(2)}, u32[]{:S(2)}) collective-permute-start(bf16[6144,256]{1,0:T(8,128)(2,1)S(1)} %select_select_fusion.1), channel_id=1, source_target_pairs={{8,12},{56,60},{64,68},{448,452},{0,128},{4,388},{296,300},{280,28... | collective-permute-start | bytes 9437192 | tf_op jit(solution)/shard_map/ppermute | solution.py:101
  298.2 53.4 %all-to-all-done.1 = bf16[128,5,2048]{2,1,0:T(8,128)(2,1)} async-done(((bf16[128,5,2048]{2,1,0:T(8,128)(2,1)}), bf16[128,5,2048]{2,1,0:T(8,128)(2,1)}, u32[]{:S(2)}, u32[]{:S(2)}) %all-to-all-start.1) | async-done | bytes 2621472 | tf_op jit(solution)/shard_map/all_to_all | solution.py:139
  351.6 3.3 slice.47
  360.8 4.5 all-to-all-start.2
  366.6 4.4 slice.51
  371.0 8.2 %all-to-all-done.2 = bf16[4,128,1,4,256]{4,1,3,2,0:T(8,128)(2,1)} async-done(((bf16[4,128,1,4,256]{4,1,3,2,0:T(8,128)(2,1)}), bf16[4,128,1,4,256]{4,1,3,2,0:T(8,128)(2,1)}, u32[]{:S(2)}, u32[]{:S(2)}) %all-to-all-start.2) | async-done | bytes 1048608 | tf_op jit(solution)/shard_map/all_to_all | solution.py:53
  382.7 52.3 %all-to-all-start.3 = ((bf16[128,4,512]{2,1,0:T(4,128)(2,1)}), bf16[128,4,512]{2,1,0:T(4,128)(2,1)}, u32[]{:S(2)}, u32[]{:S(2)}) async-start(bf16[128,4,512]{2,1,0:T(4,128)(2,1)} %copy.73), calls=%async_computation.3 | async-start | bytes 1048576 | tf_op jit(solution)/shard_map/all_to_all | solution.py:156
  438.3 16.8 %all-to-all-done.3 = bf16[128,4,512]{2,1,0:T(4,128)(2,1)} async-done(((bf16[128,4,512]{2,1,0:T(4,128)(2,1)}), bf16[128,4,512]{2,1,0:T(4,128)(2,1)}, u32[]{:S(2)}, u32[]{:S(2)}) %all-to-all-start.3) | async-done | bytes 524320 | tf_op jit(solution)/shard_map/all_to_all | solution.py:156
  460.7 3.4 all-to-all-start.4
  464.1 7.1 %all-to-all-done.4 = bf16[4,128,1,256]{3,1,2,0:T(8,128)(2,1)S(1)} async-done(((bf16[4,128,1,256]{3,1,2,0:T(8,128)(2,1)}), bf16[4,128,1,256]{3,1,2,0:T(8,128)(2,1)S(1)}, u32[]{:S(2)}, u32[]{:S(2)}) %all-to-all-start.4) | async-done | bytes 262176 | tf_op jit(solution)/shard_map/all_to_all | solution.py:53
  473.4 5.6 %all-to-all-start.5 = ((bf16[128,2,256]{2,1,0:T(2,128)(2,1)}), bf16[128,2,256]{2,1,0:T(2,128)(2,1)S(1)}, u32[]{:S(2)}, u32[]{:S(2)}) async-start(bf16[128,2,256]{2,1,0:T(2,128)(2,1)} %reshape.385), calls=%async_computation.5 | async-start | bytes 262144 | tf_op jit(solution)/shard_map/all_to_all | solution.py:177
  479.5 12.4 %all-to-all-done.5 = bf16[128,2,256]{2,1,0:T(2,128)(2,1)S(1)} async-done(((bf16[128,2,256]{2,1,0:T(2,128)(2,1)}), bf16[128,2,256]{2,1,0:T(2,128)(2,1)S(1)}, u32[]{:S(2)}, u32[]{:S(2)}) %all-to-all-start.5) | async-done | bytes 131104 | tf_op jit(solution)/shard_map/all_to_all | solution.py:177
  (104 shorter events, 37.6 us)
Async XLA Ops:
  10.5 20.6 %collective-permute-start.112 = (bf16[6144,256]{1,0:T(8,128)(2,1)S(1)}, bf16[6144,256]{1,0:T(8,128)(2,1)}, u32[]{:S(2)}, u32[]{:S(2)}) collective-permute-start(bf16[6144,256]{1,0:T(8,128)(2,1)S(1)} %param.113), channel_id=1, source_target_pairs={{452,288},{453,289},{454,290},{455,291}} | collective-permute-start | bytes 9437192 | tf_op jit(solution)/shard_map/cond/branch_113_fun/ppermute | solution.py:94
  31.3 53.4 %collective-permute-start.210 = (bf16[6144,256]{1,0:T(8,128)(2,1)S(1)}, bf16[6144,256]{1,0:T(8,128)(2,1)}, u32[]{:S(2)}, u32[]{:S(2)}) collective-permute-start(bf16[6144,256]{1,0:T(8,128)(2,1)S(1)} %param.212), channel_id=1, source_target_pairs={{336,0},{337,1},{338,2},{339,3}} | collective-permute-start | bytes 9437192 | tf_op jit(solution)/shard_map/cond/branch_84_fun/ppermute | solution.py:94
  84.7 124.9 %copy-start.3 = (bf16[64,512]{1,0:T(8,128)(2,1)S(1)}, bf16[64,512]{1,0:T(8,128)(2,1)}, u32[]{:S(2)}) copy-start(bf16[64,512]{1,0:T(8,128)(2,1)} %param.270) | copy-start | bytes 196612
  84.7 130.1 %copy-start = (s32[2,16]{1,0:T(2,128)S(1)}, s32[2,16]{1,0:T(2,128)}, u32[]{:S(2)}) copy-start(s32[2,16]{1,0:T(2,128)} %constant.153.clone) | copy-start | bytes 388
  86.7 170.5 %collective-permute-start.254 = (bf16[6144,256]{1,0:T(8,128)(2,1)}, bf16[6144,256]{1,0:T(8,128)(2,1)}, u32[]{:S(2)}, u32[]{:S(2)}) collective-permute-start(bf16[6144,256]{1,0:T(8,128)(2,1)} %select_select_fusion.2), channel_id=1, source_target_pairs={{0,448},{288,224},{1,449},{289,225},{2,450},{290,226},{3,451},{291... | collective-permute-start | bytes 9437192 | tf_op jit(solution)/shard_map/ppermute | solution.py:101
  137.7 119.5 %collective-permute-start.255 = (bf16[6144,256]{1,0:T(8,128)(2,1)}, bf16[6144,256]{1,0:T(8,128)(2,1)}, u32[]{:S(2)}, u32[]{:S(2)}) collective-permute-start(bf16[6144,256]{1,0:T(8,128)(2,1)} %select_select_fusion.2), channel_id=1, source_target_pairs={{0,64},{288,352},{1,65},{289,353},{2,66},{290,354},{3,67},{291,355}} | collective-permute-start | bytes 9437192 | tf_op jit(solution)/shard_map/ppermute | solution.py:101
  156.1 101.1 %collective-permute-start.256 = (bf16[6144,256]{1,0:T(8,128)(2,1)}, bf16[6144,256]{1,0:T(8,128)(2,1)}, u32[]{:S(2)}, u32[]{:S(2)}) collective-permute-start(bf16[6144,256]{1,0:T(8,128)(2,1)} %select_select_fusion.2), channel_id=1, source_target_pairs={{0,56},{288,280},{1,57},{289,281},{2,58},{290,282},{3,59},{291,283}} | collective-permute-start | bytes 9437192 | tf_op jit(solution)/shard_map/ppermute | solution.py:101
  174.5 82.7 %collective-permute-start.257 = (bf16[6144,256]{1,0:T(8,128)(2,1)}, bf16[6144,256]{1,0:T(8,128)(2,1)}, u32[]{:S(2)}, u32[]{:S(2)}) collective-permute-start(bf16[6144,256]{1,0:T(8,128)(2,1)} %select_select_fusion.2), channel_id=1, source_target_pairs={{0,8},{288,296},{1,9},{289,297},{2,10},{290,298},{3,11},{291,299}} | collective-permute-start | bytes 9437192 | tf_op jit(solution)/shard_map/ppermute | solution.py:101
  193.0 64.3 %collective-permute-start.258 = (bf16[6144,256]{1,0:T(8,128)(2,1)}, bf16[6144,256]{1,0:T(8,128)(2,1)}, u32[]{:S(2)}, u32[]{:S(2)}) collective-permute-start(bf16[6144,256]{1,0:T(8,128)(2,1)} %select_select_fusion.2), channel_id=1, source_target_pairs={{0,4},{288,292},{1,5},{289,293},{2,6},{290,294},{3,7},{291,295}} | collective-permute-start | bytes 9437192 | tf_op jit(solution)/shard_map/ppermute | solution.py:101
  210.4 14.9 %all-to-all-start = ((bf16[4,64,512]{2,1,0:T(8,128)(2,1)}), bf16[4,64,512]{2,1,0:T(8,128)(2,1)S(1)}, u32[]{:S(2)}, u32[]{:S(2)}) async-start(bf16[4,64,512]{2,1,0:T(8,128)(2,1)} %broadcast_in_dim.69), calls=%async_computation | async-start | bytes 524288 | tf_op jit(solution)/shard_map/all_to_all | solution.py:53
  236.3 18.8 %copy-start.11 = (s32[2]{0:T(128)S(1)}, s32[2]{0:T(128)}, u32[]{:S(2)}) copy-start(s32[2]{0:T(128)} %constant.150.clone) | copy-start | bytes 28
  236.4 19.5 %copy-start.7 = (s32[2]{0:T(128)S(1)}, s32[2]{0:T(128)}, u32[]{:S(2)}) copy-start(s32[2]{0:T(128)} %constant.146.clone) | copy-start | bytes 28
  236.4 19.5 %copy-start.8 = (s32[2]{0:T(128)S(1)}, s32[2]{0:T(128)}, u32[]{:S(2)}) copy-start(s32[2]{0:T(128)} %constant.147.clone) | copy-start | bytes 28
  236.4 20.1 %copy-start.5 = (s32[2]{0:T(128)S(1)}, s32[2]{0:T(128)}, u32[]{:S(2)}) copy-start(s32[2]{0:T(128)} %constant.148.clone) | copy-start | bytes 28
  236.4 20.1 %copy-start.6 = (s32[2]{0:T(128)S(1)}, s32[2]{0:T(128)}, u32[]{:S(2)}) copy-start(s32[2]{0:T(128)} %constant.149.clone) | copy-start | bytes 28
  236.4 115.2 %all-to-all-start.1 = ((bf16[128,5,2048]{2,1,0:T(8,128)(2,1)}), bf16[128,5,2048]{2,1,0:T(8,128)(2,1)}, u32[]{:S(2)}, u32[]{:S(2)}) async-start(bf16[128,5,2048]{2,1,0:T(8,128)(2,1)} %broadcast_select_fusion), calls=%async_computation.1 | async-start | bytes 8388608 | tf_op jit(solution)/shard_map/all_to_all | solution.py:139
  262.8 172.3 %collective-permute-start.259 = (bf16[6144,256]{1,0:T(8,128)(2,1)S(1)}, bf16[6144,256]{1,0:T(8,128)(2,1)}, u32[]{:S(2)}, u32[]{:S(2)}) collective-permute-start(bf16[6144,256]{1,0:T(8,128)(2,1)S(1)} %select_select_fusion.1), channel_id=1, source_target_pairs={{8,16},{56,48},{64,72},{448,504},{296,304},{280,272},{352,360},{22... | collective-permute-start | bytes 9437192 | tf_op jit(solution)/shard_map/ppermute | solution.py:101
  279.3 155.7 %collective-permute-start.260 = (bf16[6144,256]{1,0:T(8,128)(2,1)S(1)}, bf16[6144,256]{1,0:T(8,128)(2,1)}, u32[]{:S(2)}, u32[]{:S(2)}) collective-permute-start(bf16[6144,256]{1,0:T(8,128)(2,1)S(1)} %select_select_fusion.1), channel_id=1, source_target_pairs={{8,12},{56,60},{64,68},{448,452},{0,128},{4,388},{296,300},{280,28... | collective-permute-start | bytes 9437192 | tf_op jit(solution)/shard_map/ppermute | solution.py:101
  351.6 3.3 copy-start.1
  354.9 2.4 copy-start.2
  359.7 5.6 %copy-start.10 = (s32[12]{0:T(128)S(1)}, s32[12]{0:T(128)}, u32[]{:S(2)}) copy-start(s32[12]{0:T(128)} %constant.151.clone) | copy-start | bytes 148
  359.7 6.2 %copy-start.9 = (s32[8]{0:T(128)S(1)}, s32[8]{0:T(128)}, u32[]{:S(2)}) copy-start(s32[8]{0:T(128)} %constant.152.clone) | copy-start | bytes 100
  360.8 18.4 %all-to-all-start.2 = ((bf16[4,128,1,4,256]{4,1,3,2,0:T(8,128)(2,1)}), bf16[4,128,1,4,256]{4,1,3,2,0:T(8,128)(2,1)}, u32[]{:S(2)}, u32[]{:S(2)}) async-start(bf16[4,128,1,4,256]{4,1,3,2,0:T(8,128)(2,1)} %broadcast_in_dim.72), calls=%async_computation.2 | async-start | bytes 2097152 | tf_op jit(solution)/shard_map/all_to_all | solution.py:53
  382.7 72.4 %all-to-all-start.3 = ((bf16[128,4,512]{2,1,0:T(4,128)(2,1)}), bf16[128,4,512]{2,1,0:T(4,128)(2,1)}, u32[]{:S(2)}, u32[]{:S(2)}) async-start(bf16[128,4,512]{2,1,0:T(4,128)(2,1)} %copy.73), calls=%async_computation.3 | async-start | bytes 1048576 | tf_op jit(solution)/shard_map/all_to_all | solution.py:156
  456.3 23.1 %copy-start.4 = (f32[64,8]{0,1:T(8,128)S(1)}, f32[64,8]{0,1:T(8,128)}, u32[]{:S(2)}) copy-start(f32[64,8]{0,1:T(8,128)} %param.272) | copy-start | bytes 6148
  460.7 10.6 %all-to-all-start.4 = ((bf16[4,128,1,256]{3,1,2,0:T(8,128)(2,1)}), bf16[4,128,1,256]{3,1,2,0:T(8,128)(2,1)S(1)}, u32[]{:S(2)}, u32[]{:S(2)}) async-start(bf16[4,128,1,256]{3,1,2,0:T(8,128)(2,1)} %broadcast_in_dim.73), calls=%async_computation.4 | async-start | bytes 524288 | tf_op jit(solution)/shard_map/all_to_all | solution.py:53
  473.4 18.5 %all-to-all-start.5 = ((bf16[128,2,256]{2,1,0:T(2,128)(2,1)}), bf16[128,2,256]{2,1,0:T(2,128)(2,1)S(1)}, u32[]{:S(2)}, u32[]{:S(2)}) async-start(bf16[128,2,256]{2,1,0:T(2,128)(2,1)} %reshape.385), calls=%async_computation.5 | async-start | bytes 262144 | tf_op jit(solution)/shard_map/all_to_all | solution.py:177

commit v4 on v2

--- a/solution.py
+++ b/solution.py
@@ -52,7 +52,15 @@
         jnp.where(take_own, a, jnp.where(take_sib, b, jnp.zeros_like(a)))
         for a, b in zip(own, swapped)
     )
-    spare_gate, spare_up, spare_down = (lax.psum(w, "eph") for w in contrib)
+    packed = jnp.concatenate(
+        [contrib[0], contrib[1], contrib[2].reshape(-1, contrib[0].shape[1])], axis=0
+    )
+    piece = lax.psum_scatter(packed, "eph", scatter_dimension=0, tiled=True)
+    spread_back = lax.all_gather(piece, "eph", axis=0, tiled=True)
+    model_rows = contrib[0].shape[0]
+    spare_gate = spread_back[:model_rows]
+    spare_up = spread_back[model_rows : 2 * model_rows]
+    spare_down = spread_back[2 * model_rows :].reshape(contrib[2].shape)
     tokens, contrib = lax.optimization_barrier((tokens, contrib))
 
     earlier = jnp.cumsum(matches, axis=0) - matches

time: 375 us -> 510 us (1.36)
  waiting for transfers between devices: 227 us -> 358 us
  local copies, waits for them, and re-layouts: 27.8 us -> 33.6 us
    reduce_scatter x0 -> x1, waiting for transfers between devices: none -> 286 us  [local(): piece = lax.psum_scatter(packed, 'eph', scatter_dimension=0, tiled=True)]
    all_to_all x1, waiting for transfers between devices: 101 us -> 0.01 us  [local(): lax.all_to_all(outgoing, EP, split_axis=0, concat_axis=0, tiled=True)]
    psum x1 -> x0, waiting for transfers between devices: 83.5 us -> none  [local(): spare_gate, spare_up, spare_down = (lax.psum(w, 'eph') for w in contrib)]
    all_gather x0 -> x1, waiting for transfers between devices: none -> 31.1 us  [local(): spread_back = lax.all_gather(piece, 'eph', axis=0, tiled=True)]
  transfers between devices with their start and end apart: 9 -> 10, of which waited for: 6 -> 6; matrix products, arithmetic and copies ran while one was open for 7% -> 8% of each run, Pallas kernels for 0% -> 0%
where the time goes in v4:
time: 510 us; the launch traced here: 509 us
  waiting for transfers between devices  358 us (70%)
  starting transfers between devices  65.3 us (13%)
  local copies, waits for them, and re-layouts  33.6 us (7%)
  between operations  15.2 us (3%)
  other arithmetic  14.4 us (3%)
  blocking collectives  13.7 us (3%)
  matrix products  9.48 us (2%)
    reduce_scatter x1, waiting for transfers between devices, local(): piece = lax.psum_scatter(packed, 'eph', scatter_dimension=0, tiled=True)  286 us
    all_gather x1, waiting for transfers between devices, local(): spread_back = lax.all_gather(piece, 'eph', axis=0, tiled=True)  31.1 us
    all_to_all x1, waiting for transfers between devices, local(): lax.all_to_all(out_primary.reshape(ep_count, primary_slots, feature_local...  16.3 us
    all_to_all x1, starting transfers between devices, local(): lax.all_to_all(out_primary.reshape(ep_count, primary_slots, feature_local...  16.2 us
    all_to_all x1, starting transfers between devices, local(): lax.all_to_all(out_spare, EP, split_axis=0, concat_axis=0, tiled=True)  14.9 us
    all_to_all x1, blocking collectives, gather_dp(): lax.all_to_all(stacked, 'dp', split_axis=0, concat_axis=0, tiled=True)  13.7 us
    all_to_all x1, starting transfers between devices, local(): lax.all_to_all(outgoing, EP, split_axis=0, concat_axis=0, tiled=True)  13.4 us
    ppermute x3, starting transfers between devices, local(): swapped = tuple((lax.ppermute(w, 'c', [(0, 1), (1, 0)]) for w in own))  13.1 us
  transfers between devices with their start and end apart: 10, of which 6 were waited for; matrix products, arithmetic and copies ran while one was open for 8% of the time, Pallas kernels for 0%

profile of v4, /device:TPU:1, one launch (start us, length us, event | category | flops | bytes accessed | tf_op | source)
XLA Modules:
  0.0 509.5 jit_solution(15128064276622270139)
XLA Ops:
  6.5 8.8 %collective-permute-start.2 = (bf16[1024,512]{1,0:T(8,128)(2,1)}, bf16[1024,512]{1,0:T(8,128)(2,1)S(1)}, u32[]{:S(2)}, u32[]{:S(2)}) collective-permute-start(bf16[1024,512]{1,0:T(8,128)(2,1)} %bitcast.98), channel_id=1, source_target_pairs={{0,4},{4,0},{1,5},{5,1},{2,6},{6,2},{3,7},{7,3},{8,12},{12,8},{9,1... | collective-permute-start | bytes 3145736 | tf_op jit(solution)/shard_map/ppermute | solution.py:45
  15.3 1.9 collective-permute-start.1
  17.3 2.4 collective-permute-start
  21.3 2.5 top_k.11
  25.8 1.3 select_select_fusion
  27.5 1.4 select_select_fusion.1
  29.0 1.9 pad_maximum_fusion
  32.0 2.4 scatter_custom_fusion
  34.7 2.4 scatter_custom_fusion.1
  38.3 3.4 all-to-all-start
  41.9 6.6 %all-to-all-done = bf16[4,64,512]{2,1,0:T(8,128)(2,1)S(1)} async-done(((bf16[4,64,512]{2,1,0:T(8,128)(2,1)}), bf16[4,64,512]{2,1,0:T(8,128)(2,1)S(1)}, u32[]{:S(2)}, u32[]{:S(2)}) %all-to-all-start) | async-done | bytes 262176 | tf_op jit(solution)/shard_map/all_to_all | solution.py:15
  48.5 3.4 gather_fusion
  52.0 2.8 reshape.402
  54.8 4.6 broadcast_select_fusion
  59.4 13.4 %all-to-all-start.1 = ((bf16[128,5,2048]{2,1,0:T(8,128)(2,1)}), bf16[128,5,2048]{2,1,0:T(8,128)(2,1)}, u32[]{:S(2)}, u32[]{:S(2)}) async-start(bf16[128,5,2048]{2,1,0:T(8,128)(2,1)} %broadcast_select_fusion), calls=%async_computation.1 | async-start | bytes 8388608 | tf_op jit(solution)/shard_map/all_to_all | solution.py:96
  73.1 286.3 %reduce-scatter.2.cloned.1.call-done = bf16[96,256]{1,0:T(8,128)(2,1)} async-done(((bf16[6144,256]{1,0:T(8,128)(2,1)}), bf16[96,256]{1,0:T(8,128)(2,1)}) %reduce-scatter.2.cloned.1.call-update) | async-done | bytes 49168 | tf_op jit(solution)/shard_map/reduce_scatter | solution.py:58
  359.5 3.2 slice.35
  362.8 2.4 fusion.5
  365.1 2.4 fusion.17
  367.6 13.7 %all_to_all.30 = bf16[4,128,1,4,256]{4,1,3,2,0:T(8,128)(2,1)S(1)} all-to-all(bf16[4,128,1,4,256]{4,1,3,2,0:T(8,128)(2,1)S(1)} %broadcast_in_dim.67), channel_id=1, replica_groups=mesh['eph'=64,'c'=2,'dp'=4] {'dp'}, dimensions={0} | all-to-all | bytes 2097152 | tf_op jit(solution)/shard_map/all_to_all | solution.py:15
  383.2 16.2 %all-to-all-start.3 = ((bf16[128,4,512]{2,1,0:T(4,128)(2,1)}), bf16[128,4,512]{2,1,0:T(4,128)(2,1)S(1)}, u32[]{:S(2)}, u32[]{:S(2)}) async-start(bf16[128,4,512]{2,1,0:T(4,128)(2,1)} %copy.90), calls=%async_computation.3 | async-start | bytes 1048576 | tf_op jit(solution)/shard_map/all_to_all | solution.py:113
  399.4 4.4 slice.39
  403.8 16.3 %all-to-all-done.3 = bf16[128,4,512]{2,1,0:T(4,128)(2,1)S(1)} async-done(((bf16[128,4,512]{2,1,0:T(4,128)(2,1)}), bf16[128,4,512]{2,1,0:T(4,128)(2,1)S(1)}, u32[]{:S(2)}, u32[]{:S(2)}) %all-to-all-start.3) | async-done | bytes 524320 | tf_op jit(solution)/shard_map/all_to_all | solution.py:113
  421.1 31.1 %all-gather.2.cloned.1.call-done = bf16[6144,256]{1,0:T(8,128)(2,1)} async-done(((bf16[96,256]{1,0:T(8,128)(2,1)}), bf16[6144,256]{1,0:T(8,128)(2,1)}) %all-gather.2.cloned.1.call-update) | async-done | bytes 3145744 | tf_op jit(solution)/shard_map/all_gather | solution.py:59
  452.1 3.1 fusion.57
  455.6 1.7 fusion.32
  457.3 2.0 fusion.22
  460.0 4.0 all-to-all-start.4
  464.5 5.1 all-to-all-done.4
  471.7 14.9 %all-to-all-start.5 = ((bf16[128,2,256]{2,1,0:T(2,128)(2,1)}), bf16[128,2,256]{2,1,0:T(2,128)(2,1)S(1)}, u32[]{:S(2)}, u32[]{:S(2)}) async-start(bf16[128,2,256]{2,1,0:T(2,128)(2,1)} %reshape.443), calls=%async_computation.6 | async-start | bytes 262144 | tf_op jit(solution)/shard_map/all_to_all | solution.py:134
  486.9 12.5 %all-to-all-done.5 = bf16[128,2,256]{2,1,0:T(2,128)(2,1)S(1)} async-done(((bf16[128,2,256]{2,1,0:T(2,128)(2,1)}), bf16[128,2,256]{2,1,0:T(2,128)(2,1)S(1)}, u32[]{:S(2)}, u32[]{:S(2)}) %all-to-all-start.5) | async-done | bytes 131104 | tf_op jit(solution)/shard_map/all_to_all | solution.py:134
  499.6 2.0 gather_fusion.1
  (85 shorter events, 13.6 us)
Async XLA Ops:
  6.5 352.9 %reduce-scatter.2.cloned.1.call-start = ((), (), s32[]{:S(2)}) async-start(), calls=%async_computation.7 | async-start | bytes 3194880 | tf_op jit(solution)/shard_map/reduce_scatter | solution.py:58
  6.5 19.2 %collective-permute-start.2 = (bf16[1024,512]{1,0:T(8,128)(2,1)}, bf16[1024,512]{1,0:T(8,128)(2,1)S(1)}, u32[]{:S(2)}, u32[]{:S(2)}) collective-permute-start(bf16[1024,512]{1,0:T(8,128)(2,1)} %bitcast.98), channel_id=1, source_target_pairs={{0,4},{4,0},{1,5},{5,1},{2,6},{6,2},{3,7},{7,3},{8,12},{12,8},{9,1... | collective-permute-start | bytes 3145736 | tf_op jit(solution)/shard_map/ppermute | solution.py:45
  15.3 12.2 %collective-permute-start.1 = (bf16[2048,256]{1,0:T(8,128)(2,1)}, bf16[2048,256]{1,0:T(8,128)(2,1)}, u32[]{:S(2)}, u32[]{:S(2)}) collective-permute-start(bf16[2048,256]{1,0:T(8,128)(2,1)} %bitcast.97), channel_id=1, source_target_pairs={{0,4},{4,0},{1,5},{5,1},{2,6},{6,2},{3,7},{7,3},{8,12},{12,8},{9,1... | collective-permute-start | bytes 3145736 | tf_op jit(solution)/shard_map/ppermute | solution.py:45
  17.3 11.6 %collective-permute-start = (bf16[2048,256]{1,0:T(8,128)(2,1)}, bf16[2048,256]{1,0:T(8,128)(2,1)}, u32[]{:S(2)}, u32[]{:S(2)}) collective-permute-start(bf16[2048,256]{1,0:T(8,128)(2,1)} %bitcast.96), channel_id=1, source_target_pairs={{0,4},{4,0},{1,5},{5,1},{2,6},{6,2},{3,7},{7,3},{8,12},{12,8},{9,1... | collective-permute-start | bytes 3145736 | tf_op jit(solution)/shard_map/ppermute | solution.py:45
  27.1 1.8 copy-start.1
  30.9 0.7 copy-start.6
  30.9 6.6 %copy-start.5 = (bf16[64,512]{1,0:T(8,128)(2,1)S(1)}, bf16[64,512]{1,0:T(8,128)(2,1)}, u32[]{:S(2)}) copy-start(bf16[64,512]{1,0:T(8,128)(2,1)} %param.6) | copy-start | bytes 196612
  38.3 10.2 %all-to-all-start = ((bf16[4,64,512]{2,1,0:T(8,128)(2,1)}), bf16[4,64,512]{2,1,0:T(8,128)(2,1)S(1)}, u32[]{:S(2)}, u32[]{:S(2)}) async-start(bf16[4,64,512]{2,1,0:T(8,128)(2,1)} %broadcast_in_dim.64), calls=%async_computation | async-start | bytes 524288 | tf_op jit(solution)/shard_map/all_to_all | solution.py:15
  59.4 300.0 %all-to-all-start.1 = ((bf16[128,5,2048]{2,1,0:T(8,128)(2,1)}), bf16[128,5,2048]{2,1,0:T(8,128)(2,1)}, u32[]{:S(2)}, u32[]{:S(2)}) async-start(bf16[128,5,2048]{2,1,0:T(8,128)(2,1)} %broadcast_select_fusion), calls=%async_computation.1 | async-start | bytes 8388608 | tf_op jit(solution)/shard_map/all_to_all | solution.py:96
  72.9 289.9 %copy-start.2 = (bf16[1,2048,256]{2,1,0:T(8,128)(2,1)S(1)}, bf16[1,2048,256]{2,1,0:T(8,128)(2,1)}, u32[]{:S(2)}) copy-start(bf16[1,2048,256]{2,1,0:T(8,128)(2,1)} %param.9) | copy-start | bytes 3145732
  72.9 379.2 %all-gather.2.cloned.1.call-start = ((), (), s32[]{:S(2)}) async-start(), calls=%async_computation.8 | async-start | bytes 3194880 | tf_op jit(solution)/shard_map/all_gather | solution.py:59
  362.7 2.4 copy-start.3
  367.5 13.8 %copy-start.4 = (bf16[1,1024,512]{2,1,0:T(8,128)(2,1)S(1)}, bf16[1,1024,512]{2,1,0:T(8,128)(2,1)}, u32[]{:S(2)}) copy-start(bf16[1,1024,512]{2,1,0:T(8,128)(2,1)} %param.11) | copy-start | bytes 3145732
  383.2 36.9 %all-to-all-start.3 = ((bf16[128,4,512]{2,1,0:T(4,128)(2,1)}), bf16[128,4,512]{2,1,0:T(4,128)(2,1)S(1)}, u32[]{:S(2)}, u32[]{:S(2)}) async-start(bf16[128,4,512]{2,1,0:T(4,128)(2,1)} %copy.90), calls=%async_computation.3 | async-start | bytes 1048576 | tf_op jit(solution)/shard_map/all_to_all | solution.py:113
  457.2 29.5 %copy-start.7 = (f32[64,8]{0,1:T(8,128)S(1)}, f32[64,8]{0,1:T(8,128)}, u32[]{:S(2)}) copy-start(f32[64,8]{0,1:T(8,128)} %param.8) | copy-start | bytes 6148
  457.3 42.3 %copy-start = (bf16[512,512]{1,0:T(8,128)(2,1)S(1)}, bf16[512,512]{1,0:T(8,128)(2,1)}, u32[]{:S(2)}) copy-start(bf16[512,512]{1,0:T(8,128)(2,1)} %reshape.394) | copy-start | bytes 1572868
  460.0 9.5 %all-to-all-start.4 = ((bf16[4,128,1,256]{3,1,2,0:T(8,128)(2,1)}), bf16[4,128,1,256]{3,1,2,0:T(8,128)(2,1)S(1)}, u32[]{:S(2)}, u32[]{:S(2)}) async-start(bf16[4,128,1,256]{3,1,2,0:T(8,128)(2,1)} %broadcast_in_dim.68), calls=%async_computation.5 | async-start | bytes 524288 | tf_op jit(solution)/shard_map/all_to_all | solution.py:15
  471.7 27.7 %all-to-all-start.5 = ((bf16[128,2,256]{2,1,0:T(2,128)(2,1)}), bf16[128,2,256]{2,1,0:T(2,128)(2,1)S(1)}, u32[]{:S(2)}, u32[]{:S(2)}) async-start(bf16[128,2,256]{2,1,0:T(2,128)(2,1)} %reshape.443), calls=%async_computation.6 | async-start | bytes 262144 | tf_op jit(solution)/shard_map/all_to_all | solution.py:134
Sparse Core Ops, SparseCore 0:
  31.1 328.3 reduce-scatter.1
  362.5 89.6 all-gather.1

commit v5 on v4

--- a/solution.py
+++ b/solution.py
@@ -55,7 +55,9 @@
     packed = jnp.concatenate(
         [contrib[0], contrib[1], contrib[2].reshape(-1, contrib[0].shape[1])], axis=0
     )
-    piece = lax.psum_scatter(packed, "eph", scatter_dimension=0, tiled=True)
+    blocks = packed.reshape(pair_count, -1, packed.shape[1])
+    pieces = lax.all_to_all(blocks, "eph", split_axis=0, concat_axis=0, tiled=True)
+    piece = lax.dynamic_index_in_dim(pieces, hot_ids[parity] // HOT, axis=0, keepdims=False)
     spread_back = lax.all_gather(piece, "eph", axis=0, tiled=True)
     model_rows = contrib[0].shape[0]
     spare_gate = spread_back[:model_rows]

time: 510 us -> 371 us (0.73)
  waiting for transfers between devices: 358 us -> 193 us
  starting transfers between devices: 65.3 us -> 84.1 us
    reduce_scatter x1 -> x0, waiting for transfers between devices: 286 us -> none  [local(): piece = lax.psum_scatter(packed, 'eph', scatter_dimension=0, tiled=True)]
    all_to_all x1, waiting for transfers between devices: 0.01 us -> 93.7 us  [local(): lax.all_to_all(outgoing, EP, split_axis=0, concat_axis=0, tiled=True)]
    all_to_all x0 -> x1, waiting for transfers between devices: none -> 56.3 us  [local(): lax.all_to_all(blocks, 'eph', split_axis=0, concat_axis=0, tiled=True)]
    all_gather x1, waiting for transfers between devices: 31.1 us -> 0.01 us  [local(): spread_back = lax.all_gather(piece, 'eph', axis=0, tiled=True)]
    all_to_all x1, starting transfers between devices: 13.4 us -> 27.6 us  [local(): lax.all_to_all(outgoing, EP, split_axis=0, concat_axis=0, tiled=True)]
    all_to_all x0 -> x1, starting transfers between devices: none -> 11.3 us  [local(): lax.all_to_all(blocks, 'eph', split_axis=0, concat_axis=0, tiled=True)]
    all_to_all x1, starting transfers between devices: 14.9 us -> 9.69 us  [local(): lax.all_to_all(out_spare, EP, split_axis=0, concat_axis=0, tiled=True)]
  transfers between devices with their start and end apart: 10 -> 10, of which waited for: 6 -> 6; matrix products, arithmetic and copies ran while one was open for 8% -> 12% of each run, Pallas kernels for 0% -> 0%
where the time goes in v5:
time: 371 us; the launch traced here: 370 us
  waiting for transfers between devices  193 us (52%)
  starting transfers between devices  84.1 us (23%)
  local copies, waits for them, and re-layouts  35.4 us (10%)
  between operations  17.9 us (5%)
  blocking collectives  16.7 us (5%)
  other arithmetic  13.1 us (4%)
  matrix products  9.49 us (3%)
    all_to_all x1, waiting for transfers between devices, local(): lax.all_to_all(outgoing, EP, split_axis=0, concat_axis=0, tiled=True)  93.7 us
    all_to_all x1, waiting for transfers between devices, local(): lax.all_to_all(blocks, 'eph', split_axis=0, concat_axis=0, tiled=True)  56.3 us
    all_to_all x1, starting transfers between devices, local(): lax.all_to_all(outgoing, EP, split_axis=0, concat_axis=0, tiled=True)  27.6 us
    all_to_all x1, waiting for transfers between devices, local(): lax.all_to_all(out_primary.reshape(ep_count, primary_slots, feature_local...  20.1 us
    all_to_all x1, blocking collectives, gather_dp(): lax.all_to_all(stacked, 'dp', split_axis=0, concat_axis=0, tiled=True)  16.7 us
    all_to_all x1, starting transfers between devices, local(): lax.all_to_all(out_primary.reshape(ep_count, primary_slots, feature_local...  15.1 us
    ppermute x3, starting transfers between devices, local(): swapped = tuple((lax.ppermute(w, 'c', [(0, 1), (1, 0)]) for w in own))  13.1 us
    all_to_all x1, waiting for transfers between devices, local(): lax.all_to_all(out_spare, EP, split_axis=0, concat_axis=0, tiled=True)  12.5 us
  transfers between devices with their start and end apart: 10, of which 6 were waited for; matrix products, arithmetic and copies ran while one was open for 12% of the time, Pallas kernels for 0%

profile of v5, /device:TPU:1, one launch (start us, length us, event | category | flops | bytes accessed | tf_op | source)
XLA Modules:
  0.0 370.2 jit_solution(5715210194392752780)
XLA Ops:
  6.5 8.8 %collective-permute-start.2 = (bf16[1024,512]{1,0:T(8,128)(2,1)}, bf16[1024,512]{1,0:T(8,128)(2,1)}, u32[]{:S(2)}, u32[]{:S(2)}) collective-permute-start(bf16[1024,512]{1,0:T(8,128)(2,1)} %bitcast.103), channel_id=1, source_target_pairs={{0,4},{4,0},{1,5},{5,1},{2,6},{6,2},{3,7},{7,3},{8,12},{12,8},{9,1... | collective-permute-start | bytes 3145736 | tf_op jit(solution)/shard_map/ppermute | solution.py:45
  15.3 1.9 collective-permute-start.1
  17.3 2.4 collective-permute-start
  21.3 2.5 top_k.11
  29.6 3.4 all-to-all-start
  33.1 1.8 pad_maximum_fusion
  34.9 5.0 %all-to-all-done = bf16[4,64,512]{2,1,0:T(8,128)(2,1)S(1)} async-done(((bf16[4,64,512]{2,1,0:T(8,128)(2,1)}), bf16[4,64,512]{2,1,0:T(8,128)(2,1)S(1)}, u32[]{:S(2)}, u32[]{:S(2)}) %all-to-all-start) | async-done | bytes 262176 | tf_op jit(solution)/shard_map/all_to_all | solution.py:15
  39.8 11.3 %all-to-all-start.4 = ((bf16[64,96,256]{2,1,0:T(8,128)(2,1)}), bf16[64,96,256]{2,1,0:T(8,128)(2,1)}, u32[]{:S(2)}, u32[]{:S(2)}) async-start(bf16[64,96,256]{2,1,0:T(8,128)(2,1)} %bitcast.30), calls=%async_computation.4 | async-start | bytes 6291456 | tf_op jit(solution)/shard_map/all_to_all | solution.py:59
  51.5 2.4 scatter_custom_fusion
  54.2 2.4 scatter_custom_fusion.1
  57.3 3.4 gather_fusion
  60.8 2.8 reshape.406
  63.6 4.6 %broadcast_select_fusion = bf16[128,5,2048]{2,1,0:T(8,128)(2,1)} fusion(bf16[128,5,2048]{2,1,0:T(8,128)(2,1)} %reshape.406, pred[128,5]{1,0:T(8,128)(4,1)S(1)} %copy.84), kind=kLoop, calls=%fused_computation.4 | loop fusion | flops 1310720 | bytes 5243520 | tf_op jit(solution)/shard_map/jit(_take)/select_n | solution.py:97
  68.2 56.3 %all-to-all-done.4 = bf16[64,96,256]{2,1,0:T(8,128)(2,1)} async-done(((bf16[64,96,256]{2,1,0:T(8,128)(2,1)}), bf16[64,96,256]{2,1,0:T(8,128)(2,1)}, u32[]{:S(2)}, u32[]{:S(2)}) %all-to-all-start.4) | async-done | bytes 3145760 | tf_op jit(solution)/shard_map/all_to_all | solution.py:59
  124.5 27.6 %all-to-all-start.1 = ((bf16[128,5,2048]{2,1,0:T(8,128)(2,1)}), bf16[128,5,2048]{2,1,0:T(8,128)(2,1)}, u32[]{:S(2)}, u32[]{:S(2)}) async-start(bf16[128,5,2048]{2,1,0:T(8,128)(2,1)} %broadcast_select_fusion), calls=%async_computation.1 | async-start | bytes 8388608 | tf_op jit(solution)/shard_map/all_to_all | solution.py:98
  155.1 1.4 constant_dynamic-slice_fusion
  156.5 93.7 %all-to-all-done.1 = bf16[128,5,2048]{2,1,0:T(8,128)(2,1)} async-done(((bf16[128,5,2048]{2,1,0:T(8,128)(2,1)}), bf16[128,5,2048]{2,1,0:T(8,128)(2,1)}, u32[]{:S(2)}, u32[]{:S(2)}) %all-to-all-start.1) | async-done | bytes 2621472 | tf_op jit(solution)/shard_map/all_to_all | solution.py:98
  250.2 3.2 slice.38
  253.5 2.4 fusion.5
  255.9 2.4 fusion.17
  258.4 16.7 %all_to_all.35 = bf16[4,128,1,4,256]{4,1,3,2,0:T(8,128)(2,1)S(1)} all-to-all(bf16[4,128,1,4,256]{4,1,3,2,0:T(8,128)(2,1)S(1)} %broadcast_in_dim.67), channel_id=1, replica_groups=mesh['eph'=64,'c'=2,'dp'=4] {'dp'}, dimensions={0} | all-to-all | bytes 2097152 | tf_op jit(solution)/shard_map/all_to_all | solution.py:15
  277.0 15.1 %all-to-all-start.3 = ((bf16[128,4,512]{2,1,0:T(4,128)(2,1)}), bf16[128,4,512]{2,1,0:T(4,128)(2,1)S(1)}, u32[]{:S(2)}, u32[]{:S(2)}) async-start(bf16[128,4,512]{2,1,0:T(4,128)(2,1)} %copy.90), calls=%async_computation.3 | async-start | bytes 1048576 | tf_op jit(solution)/shard_map/all_to_all | solution.py:115
  292.1 4.4 %slice.42 = bf16[128,1,2048]{2,1,0:T(2,128)(2,1)} slice(bf16[128,5,2048]{2,1,0:T(8,128)(2,1)} %all-to-all-done.1), slice={[0:128], [4:5], [0:2048]} | slice | bytes 1048576 | tf_op jit(solution)/shard_map/slice | solution.py:100
  296.5 20.1 %all-to-all-done.3 = bf16[128,4,512]{2,1,0:T(4,128)(2,1)S(1)} async-done(((bf16[128,4,512]{2,1,0:T(4,128)(2,1)}), bf16[128,4,512]{2,1,0:T(4,128)(2,1)S(1)}, u32[]{:S(2)}, u32[]{:S(2)}) %all-to-all-start.3) | async-done | bytes 524320 | tf_op jit(solution)/shard_map/all_to_all | solution.py:115
  317.6 3.1 fusion.57
  321.1 1.7 fusion.32
  322.8 2.0 fusion.22
  325.5 3.6 all-to-all-start.5
  329.7 5.9 %all-to-all-done.5 = bf16[4,128,1,256]{3,1,2,0:T(8,128)(2,1)S(1)} async-done(((bf16[4,128,1,256]{3,1,2,0:T(8,128)(2,1)}), bf16[4,128,1,256]{3,1,2,0:T(8,128)(2,1)S(1)}, u32[]{:S(2)}, u32[]{:S(2)}) %all-to-all-start.5) | async-done | bytes 262176 | tf_op jit(solution)/shard_map/all_to_all | solution.py:15
  337.7 9.7 %all-to-all-start.6 = ((bf16[128,2,256]{2,1,0:T(2,128)(2,1)}), bf16[128,2,256]{2,1,0:T(2,128)(2,1)S(1)}, u32[]{:S(2)}, u32[]{:S(2)}) async-start(bf16[128,2,256]{2,1,0:T(2,128)(2,1)} %reshape.452), calls=%async_computation.6 | async-start | bytes 262144 | tf_op jit(solution)/shard_map/all_to_all | solution.py:136
  347.6 12.5 %all-to-all-done.6 = bf16[128,2,256]{2,1,0:T(2,128)(2,1)S(1)} async-done(((bf16[128,2,256]{2,1,0:T(2,128)(2,1)}), bf16[128,2,256]{2,1,0:T(2,128)(2,1)S(1)}, u32[]{:S(2)}, u32[]{:S(2)}) %all-to-all-start.6) | async-done | bytes 131104 | tf_op jit(solution)/shard_map/all_to_all | solution.py:136
  360.3 2.0 gather_fusion.1
  (87 shorter events, 15.5 us)
Async XLA Ops:
  6.5 19.2 %collective-permute-start.2 = (bf16[1024,512]{1,0:T(8,128)(2,1)}, bf16[1024,512]{1,0:T(8,128)(2,1)}, u32[]{:S(2)}, u32[]{:S(2)}) collective-permute-start(bf16[1024,512]{1,0:T(8,128)(2,1)} %bitcast.103), channel_id=1, source_target_pairs={{0,4},{4,0},{1,5},{5,1},{2,6},{6,2},{3,7},{7,3},{8,12},{12,8},{9,1... | collective-permute-start | bytes 3145736 | tf_op jit(solution)/shard_map/ppermute | solution.py:45
  15.3 12.2 %collective-permute-start.1 = (bf16[2048,256]{1,0:T(8,128)(2,1)}, bf16[2048,256]{1,0:T(8,128)(2,1)}, u32[]{:S(2)}, u32[]{:S(2)}) collective-permute-start(bf16[2048,256]{1,0:T(8,128)(2,1)} %bitcast.102), channel_id=1, source_target_pairs={{0,4},{4,0},{1,5},{5,1},{2,6},{6,2},{3,7},{7,3},{8,12},{12,8},{9,1... | collective-permute-start | bytes 3145736 | tf_op jit(solution)/shard_map/ppermute | solution.py:45
  17.3 10.4 %collective-permute-start = (bf16[2048,256]{1,0:T(8,128)(2,1)}, bf16[2048,256]{1,0:T(8,128)(2,1)}, u32[]{:S(2)}, u32[]{:S(2)}) collective-permute-start(bf16[2048,256]{1,0:T(8,128)(2,1)} %bitcast.101), channel_id=1, source_target_pairs={{0,4},{4,0},{1,5},{5,1},{2,6},{6,2},{3,7},{7,3},{8,12},{12,8},{9,1... | collective-permute-start | bytes 3145736 | tf_op jit(solution)/shard_map/ppermute | solution.py:45
  21.0 6.5 %copy-start.3 = (bf16[1,2048,256]{2,1,0:T(8,128)(2,1)S(1)}, bf16[1,2048,256]{2,1,0:T(8,128)(2,1)}, u32[]{:S(2)}) copy-start(bf16[1,2048,256]{2,1,0:T(8,128)(2,1)} %param.10) | copy-start | bytes 3145732
  27.5 1.2 copy-start.1
  27.5 1.4 copy-start.6
  29.6 10.2 %all-to-all-start = ((bf16[4,64,512]{2,1,0:T(8,128)(2,1)}), bf16[4,64,512]{2,1,0:T(8,128)(2,1)S(1)}, u32[]{:S(2)}, u32[]{:S(2)}) async-start(bf16[4,64,512]{2,1,0:T(8,128)(2,1)} %broadcast_in_dim.64), calls=%async_computation | async-start | bytes 524288 | tf_op jit(solution)/shard_map/all_to_all | solution.py:15
  39.8 11.3 %copy-start.7 = (s32[64,8]{0,1:T(8,128)S(1)}, s32[64,8]{0,1:T(8,128)}, u32[]{:S(2)}) copy-start(s32[64,8]{0,1:T(8,128)} %param.7) | copy-start | bytes 6148
  39.8 84.7 %all-to-all-start.4 = ((bf16[64,96,256]{2,1,0:T(8,128)(2,1)}), bf16[64,96,256]{2,1,0:T(8,128)(2,1)}, u32[]{:S(2)}, u32[]{:S(2)}) async-start(bf16[64,96,256]{2,1,0:T(8,128)(2,1)} %bitcast.30), calls=%async_computation.4 | async-start | bytes 6291456 | tf_op jit(solution)/shard_map/all_to_all | solution.py:59
  124.5 125.7 %all-to-all-start.1 = ((bf16[128,5,2048]{2,1,0:T(8,128)(2,1)}), bf16[128,5,2048]{2,1,0:T(8,128)(2,1)}, u32[]{:S(2)}, u32[]{:S(2)}) async-start(bf16[128,5,2048]{2,1,0:T(8,128)(2,1)} %broadcast_select_fusion), calls=%async_computation.1 | async-start | bytes 8388608 | tf_op jit(solution)/shard_map/all_to_all | solution.py:98
  152.2 101.3 %copy-start.2 = (bf16[1,2048,256]{2,1,0:T(8,128)(2,1)S(1)}, bf16[1,2048,256]{2,1,0:T(8,128)(2,1)}, u32[]{:S(2)}) copy-start(bf16[1,2048,256]{2,1,0:T(8,128)(2,1)} %param.9) | copy-start | bytes 3145732
  152.2 165.4 %all-gather.3.cloned.1.call-start = ((), (), s32[]{:S(2)}) async-start(), calls=%async_computation.7 | async-start | bytes 3194880 | tf_op jit(solution)/shard_map/all_gather | solution.py:61
  253.5 2.4 copy-start.4
  258.3 16.8 %copy-start.5 = (bf16[1,1024,512]{2,1,0:T(8,128)(2,1)S(1)}, bf16[1,1024,512]{2,1,0:T(8,128)(2,1)}, u32[]{:S(2)}) copy-start(bf16[1,1024,512]{2,1,0:T(8,128)(2,1)} %param.11) | copy-start | bytes 3145732
  277.0 39.7 %all-to-all-start.3 = ((bf16[128,4,512]{2,1,0:T(4,128)(2,1)}), bf16[128,4,512]{2,1,0:T(4,128)(2,1)S(1)}, u32[]{:S(2)}, u32[]{:S(2)}) async-start(bf16[128,4,512]{2,1,0:T(4,128)(2,1)} %copy.90), calls=%async_computation.3 | async-start | bytes 1048576 | tf_op jit(solution)/shard_map/all_to_all | solution.py:115
  322.8 24.8 %copy-start.8 = (f32[64,8]{0,1:T(8,128)S(1)}, f32[64,8]{0,1:T(8,128)}, u32[]{:S(2)}) copy-start(f32[64,8]{0,1:T(8,128)} %param.8) | copy-start | bytes 6148
  322.8 37.5 %copy-start = (bf16[512,512]{1,0:T(8,128)(2,1)S(1)}, bf16[512,512]{1,0:T(8,128)(2,1)}, u32[]{:S(2)}) copy-start(bf16[512,512]{1,0:T(8,128)(2,1)} %reshape.397) | copy-start | bytes 1572868
  325.5 10.0 %all-to-all-start.5 = ((bf16[4,128,1,256]{3,1,2,0:T(8,128)(2,1)}), bf16[4,128,1,256]{3,1,2,0:T(8,128)(2,1)S(1)}, u32[]{:S(2)}, u32[]{:S(2)}) async-start(bf16[4,128,1,256]{3,1,2,0:T(8,128)(2,1)} %broadcast_in_dim.68), calls=%async_computation.5 | async-start | bytes 524288 | tf_op jit(solution)/shard_map/all_to_all | solution.py:15
  337.7 22.4 %all-to-all-start.6 = ((bf16[128,2,256]{2,1,0:T(2,128)(2,1)}), bf16[128,2,256]{2,1,0:T(2,128)(2,1)S(1)}, u32[]{:S(2)}, u32[]{:S(2)}) async-start(bf16[128,2,256]{2,1,0:T(2,128)(2,1)} %reshape.452), calls=%async_computation.6 | async-start | bytes 262144 | tf_op jit(solution)/shard_map/all_to_all | solution.py:136
Sparse Core Ops, SparseCore 0:
  156.7 156.5 all-gather.2

commit v6 on v5

--- a/solution.py
+++ b/solution.py
@@ -87,23 +87,26 @@
         pick_row, mode="drop"
     )
 
-    feature_parts = gather_dp(tokens, dp_count)
-    features = jnp.moveaxis(feature_parts, 0, 1).reshape(tok_rows, -1)
-    model_width = features.shape[1]
+    slice_width = tokens.shape[1]
     source_row = jnp.concatenate(
         [cold_source.reshape(ep_count, primary_slots), hot_source.reshape(ep_count, spare_slots)],
         axis=1,
     )
-    outgoing = jnp.take(features, source_row, axis=0, mode="fill", fill_value=0)
-    incoming = lax.all_to_all(outgoing, EP, split_axis=0, concat_axis=0, tiled=True)
-    primary_rows = incoming[:, :primary_slots].reshape(ep_count, exp_dev, capacity, model_width)
-    spare_rows = incoming[:, primary_slots:]
+    outgoing = jnp.take(tokens, source_row, axis=0, mode="fill", fill_value=0)
+    arrived = lax.all_to_all(outgoing, EP, split_axis=0, concat_axis=0, tiled=True)
+    incoming = gather_dp(arrived, dp_count)
+    primary_rows = incoming[:, :, :primary_slots].reshape(
+        dp_count, ep_count, exp_dev, capacity, slice_width
+    )
+    spare_rows = incoming[:, :, primary_slots:]
+    gate_split = gate_weight.reshape(exp_dev, dp_count, slice_width, -1)
+    up_split = up_weight.reshape(exp_dev, dp_count, slice_width, -1)
 
     gate_primary = jnp.einsum(
-        "secd,edf->secf", primary_rows, gate_weight, preferred_element_type=jnp.float32
+        "nsecd,endf->secf", primary_rows, gate_split, preferred_element_type=jnp.float32
     )
     up_primary = jnp.einsum(
-        "secd,edf->secf", primary_rows, up_weight, preferred_element_type=jnp.float32
+        "nsecd,endf->secf", primary_rows, up_split, preferred_element_type=jnp.float32
     )
     hidden_primary = silu_product(gate_primary, up_primary)
     part_primary = gather_dp(hidden_primary, dp_count)
@@ -123,10 +126,14 @@
     back_primary, spare_gate, spare_up, spare_down = lax.optimization_barrier(
         (back_primary, spare_gate, spare_up, spare_down)
     )
+    spare_gate = spare_gate.reshape(dp_count, slice_width, -1)
+    spare_up = spare_up.reshape(dp_count, slice_width, -1)
     gate_spare = jnp.einsum(
-        "srd,df->srf", spare_rows, spare_gate, preferred_element_type=jnp.float32
+        "nsrd,ndf->srf", spare_rows, spare_gate, preferred_element_type=jnp.float32
     )
-    up_spare = jnp.einsum("srd,df->srf", spare_rows, spare_up, preferred_element_type=jnp.float32)
+    up_spare = jnp.einsum(
+        "nsrd,ndf->srf", spare_rows, spare_up, preferred_element_type=jnp.float32
+    )
     hidden_spare = silu_product(gate_spare, up_spare)
     part_spare = gather_dp(hidden_spare, dp_count)
     spare_split = spare_down.reshape(dp_count, -1, feature_local)

time: 371 us -> 317 us (0.85)
  blocking collectives: 16.7 us -> 139 us
  waiting for transfers between devices: 193 us -> 86.2 us
  starting transfers between devices: 84.1 us -> 33.6 us
  local copies, waits for them, and re-layouts: 35.4 us -> 23.7 us
  matrix products: 9.49 us -> 5.53 us
    all_to_all x2 -> x0, waiting for transfers between devices: 114 us -> none  [the longest x1 93.7 us: local(): lax.all_to_all(outgoing, EP, split_axis=0, concat_axis=0, tiled=True)]
    all_to_all x0 -> x2, blocking collectives: none -> 88.6 us  [the longest x1 58.6 us: local(): lax.all_to_all(outgoing, EP, split_axis=0, concat_axis=0, tiled=True)]
    all_to_all x2 -> x0, starting transfers between devices: 42.7 us -> none  [the longest x1 27.6 us: local(): lax.all_to_all(outgoing, EP, split_axis=0, concat_axis=0, tiled=True)]
    all_to_all x1 -> x2, blocking collectives: 16.7 us -> 50.6 us  [gather_dp(): lax.all_to_all(stacked, 'dp', split_axis=0, concat_axis=0, tiled=True)]
    all_to_all x1, waiting for transfers between devices: 56.3 us -> 66.9 us  [local(): lax.all_to_all(blocks, 'eph', split_axis=0, concat_axis=0, tiled=True)]
    slice x2 -> x0, local copies, waits for them, and re-layouts: 7.66 us -> none  [the longest x1 4.43 us: local(): spare_rows = incoming[:, primary_slots:]]
    select_n x2, other arithmetic: 4.62 us -> 0.21 us  [local(): outgoing = jnp.take(tokens, source_row, axis=0, mode='fill', fill_value=0)]
    all_to_all x2 -> x1, waiting for transfers between devices: 10.8 us -> 6.66 us  [gather_dp(): lax.all_to_all(stacked, 'dp', split_axis=0, concat_axis=0, tiled=True)]
  transfers between devices with their start and end apart: 10 -> 7, of which waited for: 6 -> 3; matrix products, arithmetic and copies ran while one was open for 12% -> 7% of each run, Pallas kernels for 0% -> 0%
where the time goes in v6:
time: 317 us; the launch traced here: 316 us
  blocking collectives  139 us (44%)
  waiting for transfers between devices  86.2 us (27%)
  starting transfers between devices  33.6 us (11%)
  local copies, waits for them, and re-layouts  23.7 us (7%)
  between operations  17.8 us (6%)
  other arithmetic  9.9 us (3%)
  matrix products  5.53 us (2%)
    all_to_all x1, waiting for transfers between devices, local(): lax.all_to_all(blocks, 'eph', split_axis=0, concat_axis=0, tiled=True)  66.9 us
    all_to_all x1, blocking collectives, local(): lax.all_to_all(outgoing, EP, split_axis=0, concat_axis=0, tiled=True)  58.6 us
    all_to_all x2, blocking collectives, gather_dp(): lax.all_to_all(stacked, 'dp', split_axis=0, concat_axis=0, tiled=True)  50.6 us
    all_to_all x1, blocking collectives, local(): lax.all_to_all(out_primary.reshape(ep_count, primary_slots, feature_local...  30 us
    ppermute x3, starting transfers between devices, local(): swapped = tuple((lax.ppermute(w, 'c', [(0, 1), (1, 0)]) for w in own))  13.2 us
    all_to_all x1, waiting for transfers between devices, local(): lax.all_to_all(out_spare, EP, split_axis=0, concat_axis=0, tiled=True)  12.6 us
    all_to_all x1, starting transfers between devices, local(): lax.all_to_all(blocks, 'eph', split_axis=0, concat_axis=0, tiled=True)  11.3 us
    all_to_all x1, waiting for transfers between devices, gather_dp(): lax.all_to_all(stacked, 'dp', split_axis=0, concat_axis=0, tiled=True)  6.66 us
  transfers between devices with their start and end apart: 7, of which 3 were waited for; matrix products, arithmetic and copies ran while one was open for 7% of the time, Pallas kernels for 0%

profile of v6, /device:TPU:1, one launch (start us, length us, event | category | flops | bytes accessed | tf_op | source)
XLA Modules:
  0.0 316.0 jit_solution(16756187289291169178)
XLA Ops:
  6.5 8.9 %collective-permute-start.2 = (bf16[1024,512]{1,0:T(8,128)(2,1)}, bf16[1024,512]{1,0:T(8,128)(2,1)S(1)}, u32[]{:S(2)}, u32[]{:S(2)}) collective-permute-start(bf16[1024,512]{1,0:T(8,128)(2,1)} %bitcast.132), channel_id=1, source_target_pairs={{0,4},{4,0},{1,5},{5,1},{2,6},{6,2},{3,7},{7,3},{8,12},{12,8},{9,1... | collective-permute-start | bytes 3145736 | tf_op jit(solution)/shard_map/ppermute | solution.py:45
  15.5 1.9 collective-permute-start.1
  17.4 2.4 collective-permute-start
  19.8 0.8 copy.70
  21.5 2.5 top_k.11
  25.9 1.3 select_select_fusion
  27.7 1.4 select_select_fusion.1
  29.2 1.8 pad_maximum_fusion
  31.0 11.3 %all-to-all-start.4 = ((bf16[64,96,256]{2,1,0:T(8,128)(2,1)}), bf16[64,96,256]{2,1,0:T(8,128)(2,1)}, u32[]{:S(2)}, u32[]{:S(2)}) async-start(bf16[64,96,256]{2,1,0:T(8,128)(2,1)} %bitcast.36), calls=%async_computation.4 | async-start | bytes 6291456 | tf_op jit(solution)/shard_map/all_to_all | solution.py:59
  45.3 2.4 scatter_custom_fusion
  48.0 2.4 scatter_custom_fusion.1
  51.1 2.8 gather_fusion
  54.2 66.9 %all-to-all-done.4 = bf16[64,96,256]{2,1,0:T(8,128)(2,1)} async-done(((bf16[64,96,256]{2,1,0:T(8,128)(2,1)}), bf16[64,96,256]{2,1,0:T(8,128)(2,1)}, u32[]{:S(2)}, u32[]{:S(2)}) %all-to-all-start.4) | async-done | bytes 3145760 | tf_op jit(solution)/shard_map/all_to_all | solution.py:59
  121.1 1.4 constant_dynamic-slice_fusion
  122.7 58.6 %all_to_all.35 = bf16[128,5,512]{2,1,0:T(8,128)(2,1)S(1)} all-to-all(bf16[128,5,512]{2,1,0:T(8,128)(2,1)S(1)} %broadcast_select_fusion), channel_id=1, replica_groups=mesh['eph'=64,'c'=2,'dp'=4] {'eph','c'}, dimensions={0} | all-to-all | bytes 1310720 | tf_op jit(solution)/shard_map/all_to_all | solution.py:96
  181.8 34.9 %all_to_all.36 = bf16[4,128,5,512]{3,1,2,0:T(8,128)(2,1)S(1)} all-to-all(bf16[4,128,5,512]{3,1,2,0:T(8,128)(2,1)S(1)} %broadcast_in_dim.65), channel_id=1, replica_groups=mesh['eph'=64,'c'=2,'dp'=4] {'dp'}, dimensions={0} | all-to-all | bytes 5242880 | tf_op jit(solution)/shard_map/all_to_all | solution.py:15
  216.7 0.7 convolution_bitcast_fusion.2
  217.4 0.8 copy-done.1
  218.7 0.7 fusion.3
  219.5 15.8 %all_to_all.37 = bf16[4,128,1,4,256]{4,1,3,2,0:T(8,128)(2,1)S(1)} all-to-all(bf16[4,128,1,4,256]{4,1,3,2,0:T(8,128)(2,1)S(1)} %broadcast_in_dim.67), channel_id=1, replica_groups=mesh['eph'=64,'c'=2,'dp'=4] {'dp'}, dimensions={0} | all-to-all | bytes 2097152 | tf_op jit(solution)/shard_map/all_to_all | solution.py:15
  236.4 30.0 %all_to_all.38 = bf16[128,4,512]{2,1,0:T(4,128)(2,1)S(1)} all-to-all(bf16[128,4,512]{2,1,0:T(4,128)(2,1)S(1)} %copy.91), channel_id=1, replica_groups=mesh['eph'=64,'c'=2,'dp'=4] {'eph','c'}, dimensions={0} | all-to-all | bytes 1048576 | tf_op jit(solution)/shard_map/all_to_all | solution.py:118
  266.4 0.9 reshape.409
  267.4 3.0 fusion.39
  270.8 1.4 convolution_bitcast_fusion.5
  272.2 1.8 fusion.7
  274.0 0.7 broadcast_in_dim.68
  274.7 3.4 %all-to-all-start.5 = ((bf16[4,128,1,256]{3,1,2,0:T(8,128)(2,1)}), bf16[4,128,1,256]{3,1,2,0:T(8,128)(2,1)S(1)}, u32[]{:S(2)}, u32[]{:S(2)}) async-start(bf16[4,128,1,256]{3,1,2,0:T(8,128)(2,1)} %broadcast_in_dim.68), calls=%async_computation.5 | async-start | bytes 524288 | tf_op jit(solution)/shard_map/all_to_all | solution.py:15
  278.6 6.7 %all-to-all-done.5 = bf16[4,128,1,256]{3,1,2,0:T(8,128)(2,1)S(1)} async-done(((bf16[4,128,1,256]{3,1,2,0:T(8,128)(2,1)}), bf16[4,128,1,256]{3,1,2,0:T(8,128)(2,1)S(1)}, u32[]{:S(2)}, u32[]{:S(2)}) %all-to-all-start.5) | async-done | bytes 262176 | tf_op jit(solution)/shard_map/all_to_all | solution.py:15
  287.4 5.6 %all-to-all-start.6 = ((bf16[128,2,256]{2,1,0:T(2,128)(2,1)}), bf16[128,2,256]{2,1,0:T(2,128)(2,1)S(1)}, u32[]{:S(2)}, u32[]{:S(2)}) async-start(bf16[128,2,256]{2,1,0:T(2,128)(2,1)} %reshape.470), calls=%async_computation.6 | async-start | bytes 262144 | tf_op jit(solution)/shard_map/all_to_all | solution.py:143
  293.3 12.6 %all-to-all-done.6 = bf16[128,2,256]{2,1,0:T(2,128)(2,1)S(1)} async-done(((bf16[128,2,256]{2,1,0:T(2,128)(2,1)}), bf16[128,2,256]{2,1,0:T(2,128)(2,1)S(1)}, u32[]{:S(2)}, u32[]{:S(2)}) %all-to-all-start.6) | async-done | bytes 131104 | tf_op jit(solution)/shard_map/all_to_all | solution.py:143
  306.1 2.0 gather_fusion.1
  308.0 1.1 multiply_reduce_fusion
  (80 shorter events, 9.2 us)
Async XLA Ops:
  6.5 44.6 %copy-start = (bf16[64,512]{1,0:T(8,128)(2,1)S(1)}, bf16[64,512]{1,0:T(8,128)(2,1)}, u32[]{:S(2)}) copy-start(bf16[64,512]{1,0:T(8,128)(2,1)} %param.6) | copy-start | bytes 196612
  6.5 19.3 %collective-permute-start.2 = (bf16[1024,512]{1,0:T(8,128)(2,1)}, bf16[1024,512]{1,0:T(8,128)(2,1)S(1)}, u32[]{:S(2)}, u32[]{:S(2)}) collective-permute-start(bf16[1024,512]{1,0:T(8,128)(2,1)} %bitcast.132), channel_id=1, source_target_pairs={{0,4},{4,0},{1,5},{5,1},{2,6},{6,2},{3,7},{7,3},{8,12},{12,8},{9,1... | collective-permute-start | bytes 3145736 | tf_op jit(solution)/shard_map/ppermute | solution.py:45
  15.5 12.2 %collective-permute-start.1 = (bf16[2048,256]{1,0:T(8,128)(2,1)}, bf16[2048,256]{1,0:T(8,128)(2,1)}, u32[]{:S(2)}, u32[]{:S(2)}) collective-permute-start(bf16[2048,256]{1,0:T(8,128)(2,1)} %bitcast.130), channel_id=1, source_target_pairs={{0,4},{4,0},{1,5},{5,1},{2,6},{6,2},{3,7},{7,3},{8,12},{12,8},{9,1... | collective-permute-start | bytes 3145736 | tf_op jit(solution)/shard_map/ppermute | solution.py:45
  17.4 11.6 %collective-permute-start = (bf16[2048,256]{1,0:T(8,128)(2,1)}, bf16[2048,256]{1,0:T(8,128)(2,1)}, u32[]{:S(2)}, u32[]{:S(2)}) collective-permute-start(bf16[2048,256]{1,0:T(8,128)(2,1)} %bitcast.128), channel_id=1, source_target_pairs={{0,4},{4,0},{1,5},{5,1},{2,6},{6,2},{3,7},{7,3},{8,12},{12,8},{9,1... | collective-permute-start | bytes 3145736 | tf_op jit(solution)/shard_map/ppermute | solution.py:45
  27.2 1.8 copy-start.3
  31.0 14.0 %copy-start.6 = (s32[64,8]{0,1:T(8,128)S(1)}, s32[64,8]{0,1:T(8,128)}, u32[]{:S(2)}) copy-start(s32[64,8]{0,1:T(8,128)} %param.7) | copy-start | bytes 6148
  31.0 90.0 %all-to-all-start.4 = ((bf16[64,96,256]{2,1,0:T(8,128)(2,1)}), bf16[64,96,256]{2,1,0:T(8,128)(2,1)}, u32[]{:S(2)}, u32[]{:S(2)}) async-start(bf16[64,96,256]{2,1,0:T(8,128)(2,1)} %bitcast.36), calls=%async_computation.4 | async-start | bytes 6291456 | tf_op jit(solution)/shard_map/all_to_all | solution.py:59
  42.3 225.1 %all-gather.3.cloned.1.call-start = ((), (), s32[]{:S(2)}) async-start(), calls=%async_computation.7 | async-start | bytes 3194880 | tf_op jit(solution)/shard_map/all_gather | solution.py:61
  216.7 1.5 copy-start.1
  216.7 2.0 copy-start.4
  219.4 15.9 %copy-start.5 = (bf16[1,1024,512]{2,1,0:T(8,128)(2,1)S(1)}, bf16[1,1024,512]{2,1,0:T(8,128)(2,1)}, u32[]{:S(2)}) copy-start(bf16[1,1024,512]{2,1,0:T(8,128)(2,1)} %param.11) | copy-start | bytes 3145732
  272.2 21.0 %copy-start.7 = (f32[64,8]{0,1:T(8,128)S(1)}, f32[64,8]{0,1:T(8,128)}, u32[]{:S(2)}) copy-start(f32[64,8]{0,1:T(8,128)} %param.8) | copy-start | bytes 6148
  272.2 33.8 %copy-start.2 = (bf16[512,512]{1,0:T(8,128)(2,1)S(1)}, bf16[512,512]{1,0:T(8,128)(2,1)}, u32[]{:S(2)}) copy-start(bf16[512,512]{1,0:T(8,128)(2,1)} %reshape.409) | copy-start | bytes 1572868
  274.7 10.6 %all-to-all-start.5 = ((bf16[4,128,1,256]{3,1,2,0:T(8,128)(2,1)}), bf16[4,128,1,256]{3,1,2,0:T(8,128)(2,1)S(1)}, u32[]{:S(2)}, u32[]{:S(2)}) async-start(bf16[4,128,1,256]{3,1,2,0:T(8,128)(2,1)} %broadcast_in_dim.68), calls=%async_computation.5 | async-start | bytes 524288 | tf_op jit(solution)/shard_map/all_to_all | solution.py:15
  287.4 18.5 %all-to-all-start.6 = ((bf16[128,2,256]{2,1,0:T(2,128)(2,1)}), bf16[128,2,256]{2,1,0:T(2,128)(2,1)S(1)}, u32[]{:S(2)}, u32[]{:S(2)}) async-start(bf16[128,2,256]{2,1,0:T(2,128)(2,1)} %reshape.470), calls=%async_computation.6 | async-start | bytes 262144 | tf_op jit(solution)/shard_map/all_to_all | solution.py:143
Sparse Core Ops, SparseCore 0:
  122.6 107.4 all-gather.2

commit v7 on v6

--- a/solution.py
+++ b/solution.py
@@ -115,17 +115,7 @@
     out_primary = jnp.einsum(
         "nsecf,enfd->secd", part_primary, down_split, preferred_element_type=jnp.float32
     ).astype(jnp.bfloat16)
-    back_primary = lax.all_to_all(
-        out_primary.reshape(ep_count, primary_slots, feature_local),
-        EP,
-        split_axis=0,
-        concat_axis=0,
-        tiled=True,
-    ).reshape(primary_total, feature_local)
 
-    back_primary, spare_gate, spare_up, spare_down = lax.optimization_barrier(
-        (back_primary, spare_gate, spare_up, spare_down)
-    )
     spare_gate = spare_gate.reshape(dp_count, slice_width, -1)
     spare_up = spare_up.reshape(dp_count, slice_width, -1)
     gate_spare = jnp.einsum(
@@ -140,12 +130,21 @@
     out_spare = jnp.einsum(
         "nsrf,nfd->srd", part_spare, spare_split, preferred_element_type=jnp.float32
     ).astype(jnp.bfloat16)
-    back_spare = lax.all_to_all(out_spare, EP, split_axis=0, concat_axis=0, tiled=True).reshape(
-        spare_total, feature_local
+
+    per_owner = primary_slots + spare_slots
+    results = jnp.concatenate(
+        [out_primary.reshape(ep_count, primary_slots, feature_local), out_spare], axis=1
     )
-
-    returned = jnp.concatenate([back_primary, back_spare], axis=0)
-    target = jnp.where(is_hot, primary_total + hot_target, cold_target)
+    returned = lax.all_to_all(results, EP, split_axis=0, concat_axis=0, tiled=True).reshape(
+        ep_count * per_owner, feature_local
+    )
+    cold_back = (
+        flat_ids // exp_dev * per_owner + flat_ids % exp_dev * capacity + order_rank
+    )
+    hot_back = (
+        hot_target // spare_slots * per_owner + primary_slots + hot_target % spare_slots
+    )
+    target = jnp.where(is_hot, hot_back, cold_back)
     fetched = jnp.take(returned, target, axis=0).reshape(tok_rows, top_count, feature_local)
     combined = jnp.sum(gate_probs[:, :, None] * fetched.astype(jnp.float32), axis=1)
     return combined.astype(jnp.bfloat16)

time: 317 us -> 309 us (0.975)
  blocking collectives: 139 us -> 92.1 us
  waiting for transfers between devices: 86.2 us -> 117 us
  starting transfers between devices: 33.6 us -> 43.2 us
    all_to_all x1 -> x0, blocking collectives: 30 us -> none  [local(): lax.all_to_all(out_primary.reshape(ep_count, primary_slots, feature_local...]
    all_to_all x1, waiting for transfers between devices: 12.6 us -> 30.2 us  [local(): lax.all_to_all(results, EP, split_axis=0, concat_axis=0, tiled=True)]
    all_to_all x2 -> x1, blocking collectives: 50.6 us -> 34.8 us  [gather_dp(): lax.all_to_all(stacked, 'dp', split_axis=0, concat_axis=0, tiled=True)]
    all_to_all x1, waiting for transfers between devices: 66.9 us -> 75.6 us  [local(): lax.all_to_all(blocks, 'eph', split_axis=0, concat_axis=0, tiled=True)]
    all_to_all x1 -> x2, waiting for transfers between devices: 6.66 us -> 11.7 us  [gather_dp(): lax.all_to_all(stacked, 'dp', split_axis=0, concat_axis=0, tiled=True)]
    all_to_all x1, starting transfers between devices: 5.62 us -> 10.3 us  [local(): lax.all_to_all(results, EP, split_axis=0, concat_axis=0, tiled=True)]
    all_to_all x1 -> x2, starting transfers between devices: 3.4 us -> 7.1 us  [gather_dp(): lax.all_to_all(stacked, 'dp', split_axis=0, concat_axis=0, tiled=True)]
  transfers between devices with their start and end apart: 7 -> 8, of which waited for: 3 -> 4; matrix products, arithmetic and copies ran while one was open for 7% -> 9% of each run, Pallas kernels for 0% -> 0%
where the time goes in v7:
time: 309 us; the launch traced here: 308 us
  waiting for transfers between devices  117 us (38%)
  blocking collectives  92.1 us (30%)
  starting transfers between devices  43.2 us (14%)
  local copies, waits for them, and re-layouts  22.1 us (7%)
  between operations  17.8 us (6%)
  other arithmetic  9.24 us (3%)
  matrix products  6.01 us (2%)
    all_to_all x1, waiting for transfers between devices, local(): lax.all_to_all(blocks, 'eph', split_axis=0, concat_axis=0, tiled=True)  75.6 us
    all_to_all x1, blocking collectives, local(): lax.all_to_all(outgoing, EP, split_axis=0, concat_axis=0, tiled=True)  57.2 us
    all_to_all x1, blocking collectives, gather_dp(): lax.all_to_all(stacked, 'dp', split_axis=0, concat_axis=0, tiled=True)  34.8 us
    all_to_all x1, waiting for transfers between devices, local(): lax.all_to_all(results, EP, split_axis=0, concat_axis=0, tiled=True)  30.2 us
    ppermute x3, starting transfers between devices, local(): swapped = tuple((lax.ppermute(w, 'c', [(0, 1), (1, 0)]) for w in own))  13.2 us
    all_to_all x1, starting transfers between devices, local(): lax.all_to_all(blocks, 'eph', split_axis=0, concat_axis=0, tiled=True)  12.6 us
    all_to_all x2, waiting for transfers between devices, gather_dp(): lax.all_to_all(stacked, 'dp', split_axis=0, concat_axis=0, tiled=True)  11.7 us
    all_to_all x1, starting transfers between devices, local(): lax.all_to_all(results, EP, split_axis=0, concat_axis=0, tiled=True)  10.3 us
  transfers between devices with their start and end apart: 8, of which 4 were waited for; matrix products, arithmetic and copies ran while one was open for 9% of the time, Pallas kernels for 0%

profile of v7, /device:TPU:1, one launch (start us, length us, event | category | flops | bytes accessed | tf_op | source)
XLA Modules:
  0.0 307.9 jit_solution(9539779479698622514)
XLA Ops:
  6.5 8.9 %collective-permute-start.2 = (bf16[1024,512]{1,0:T(8,128)(2,1)}, bf16[1024,512]{1,0:T(8,128)(2,1)S(1)}, u32[]{:S(2)}, u32[]{:S(2)}) collective-permute-start(bf16[1024,512]{1,0:T(8,128)(2,1)} %bitcast.123), channel_id=1, source_target_pairs={{0,4},{4,0},{1,5},{5,1},{2,6},{6,2},{3,7},{7,3},{8,12},{12,8},{9,1... | collective-permute-start | bytes 3145736 | tf_op jit(solution)/shard_map/ppermute | solution.py:45
  15.5 1.9 collective-permute-start.1
  17.4 2.4 collective-permute-start
  19.8 0.8 copy.55
  21.5 2.5 top_k.11
  25.9 1.3 select_select_fusion
  27.6 1.4 select_select_fusion.1
  29.2 1.8 pad_maximum_fusion
  31.0 12.6 %all-to-all-start.3 = ((bf16[64,96,256]{2,1,0:T(8,128)(2,1)}), bf16[64,96,256]{2,1,0:T(8,128)(2,1)S(1)}, u32[]{:S(2)}, u32[]{:S(2)}) async-start(bf16[64,96,256]{2,1,0:T(8,128)(2,1)} %bitcast.37), calls=%async_computation.3 | async-start | bytes 6291456 | tf_op jit(solution)/shard_map/all_to_all | solution.py:59
  46.2 75.6 %all-to-all-done.3 = bf16[64,96,256]{2,1,0:T(8,128)(2,1)S(1)} async-done(((bf16[64,96,256]{2,1,0:T(8,128)(2,1)}), bf16[64,96,256]{2,1,0:T(8,128)(2,1)S(1)}, u32[]{:S(2)}, u32[]{:S(2)}) %all-to-all-start.3) | async-done | bytes 3145760 | tf_op jit(solution)/shard_map/all_to_all | solution.py:59
  123.0 2.4 scatter_custom_fusion
  125.6 2.4 scatter_custom_fusion.1
  128.8 2.8 gather_fusion
  132.0 57.2 %all_to_all.30 = bf16[128,5,512]{2,1,0:T(8,128)(2,1)S(1)} all-to-all(bf16[128,5,512]{2,1,0:T(8,128)(2,1)S(1)} %broadcast_select_fusion), channel_id=1, replica_groups=mesh['eph'=64,'c'=2,'dp'=4] {'eph','c'}, dimensions={0} | all-to-all | bytes 1310720 | tf_op jit(solution)/shard_map/all_to_all | solution.py:96
  189.8 34.8 %all_to_all.31 = bf16[4,128,5,512]{3,1,2,0:T(8,128)(2,1)S(1)} all-to-all(bf16[4,128,5,512]{3,1,2,0:T(8,128)(2,1)S(1)} %broadcast_in_dim.68), channel_id=1, replica_groups=mesh['eph'=64,'c'=2,'dp'=4] {'dp'}, dimensions={0} | all-to-all | bytes 5242880 | tf_op jit(solution)/shard_map/all_to_all | solution.py:15
  224.6 0.7 convolution_bitcast_fusion.2
  225.3 1.3 copy-done.4
  227.3 1.1 broadcast_in_dim.70
  228.4 3.5 %all-to-all-start.2 = ((bf16[4,128,1,4,256]{4,1,3,2,0:T(8,128)(2,1)}), bf16[4,128,1,4,256]{4,1,3,2,0:T(8,128)(2,1)S(1)}, u32[]{:S(2)}, u32[]{:S(2)}) async-start(bf16[4,128,1,4,256]{4,1,3,2,0:T(8,128)(2,1)} %broadcast_in_dim.70), calls=%async_computation.2 | async-start | bytes 2097152 | tf_op jit(solution)/shard_map/all_to_all | solution.py:15
  232.0 2.1 fusion.40
  234.1 1.4 convolution_bitcast_fusion.5
  235.5 1.4 fusion.7
  236.9 8.3 %all-to-all-done.2 = bf16[4,128,1,4,256]{4,1,3,2,0:T(8,128)(2,1)S(1)} async-done(((bf16[4,128,1,4,256]{4,1,3,2,0:T(8,128)(2,1)}), bf16[4,128,1,4,256]{4,1,3,2,0:T(8,128)(2,1)S(1)}, u32[]{:S(2)}, u32[]{:S(2)}) %all-to-all-start.2) | async-done | bytes 1048608 | tf_op jit(solution)/shard_map/all_to_all | solution.py:15
  245.2 0.7 broadcast_in_dim.71
  245.9 3.6 %all-to-all-start.4 = ((bf16[4,128,1,256]{3,1,2,0:T(8,128)(2,1)}), bf16[4,128,1,256]{3,1,2,0:T(8,128)(2,1)S(1)}, u32[]{:S(2)}, u32[]{:S(2)}) async-start(bf16[4,128,1,256]{3,1,2,0:T(8,128)(2,1)} %broadcast_in_dim.71), calls=%async_computation.4 | async-start | bytes 524288 | tf_op jit(solution)/shard_map/all_to_all | solution.py:15
  249.5 1.5 fusion
  251.4 3.4 %all-to-all-done.4 = bf16[4,128,1,256]{3,1,2,0:T(8,128)(2,1)S(1)} async-done(((bf16[4,128,1,256]{3,1,2,0:T(8,128)(2,1)}), bf16[4,128,1,256]{3,1,2,0:T(8,128)(2,1)S(1)}, u32[]{:S(2)}, u32[]{:S(2)}) %all-to-all-start.4) | async-done | bytes 262176 | tf_op jit(solution)/shard_map/all_to_all | solution.py:15
  255.2 1.4 copy.77
  256.5 10.3 %all-to-all-start.5 = ((bf16[128,5,512]{2,1,0:T(8,128)(2,1)}), bf16[128,5,512]{2,1,0:T(8,128)(2,1)S(1)}, u32[]{:S(2)}, u32[]{:S(2)}) async-start(bf16[128,5,512]{2,1,0:T(8,128)(2,1)} %copy.77), calls=%async_computation.5 | async-start | bytes 2097152 | tf_op jit(solution)/shard_map/all_to_all | solution.py:138
  267.6 30.2 %all-to-all-done.5 = bf16[128,5,512]{2,1,0:T(8,128)(2,1)S(1)} async-done(((bf16[128,5,512]{2,1,0:T(8,128)(2,1)}), bf16[128,5,512]{2,1,0:T(8,128)(2,1)S(1)}, u32[]{:S(2)}, u32[]{:S(2)}) %all-to-all-start.5) | async-done | bytes 655392 | tf_op jit(solution)/shard_map/all_to_all | solution.py:138
  298.0 2.0 gather_fusion.1
  300.0 1.1 multiply_reduce_fusion
  (79 shorter events, 7.4 us)
Async XLA Ops:
  6.5 122.2 %copy-start = (bf16[64,512]{1,0:T(8,128)(2,1)S(1)}, bf16[64,512]{1,0:T(8,128)(2,1)}, u32[]{:S(2)}) copy-start(bf16[64,512]{1,0:T(8,128)(2,1)} %param.6) | copy-start | bytes 196612
  6.5 19.3 %collective-permute-start.2 = (bf16[1024,512]{1,0:T(8,128)(2,1)}, bf16[1024,512]{1,0:T(8,128)(2,1)S(1)}, u32[]{:S(2)}, u32[]{:S(2)}) collective-permute-start(bf16[1024,512]{1,0:T(8,128)(2,1)} %bitcast.123), channel_id=1, source_target_pairs={{0,4},{4,0},{1,5},{5,1},{2,6},{6,2},{3,7},{7,3},{8,12},{12,8},{9,1... | collective-permute-start | bytes 3145736 | tf_op jit(solution)/shard_map/ppermute | solution.py:45
  15.5 12.2 %collective-permute-start.1 = (bf16[2048,256]{1,0:T(8,128)(2,1)}, bf16[2048,256]{1,0:T(8,128)(2,1)}, u32[]{:S(2)}, u32[]{:S(2)}) collective-permute-start(bf16[2048,256]{1,0:T(8,128)(2,1)} %bitcast.121), channel_id=1, source_target_pairs={{0,4},{4,0},{1,5},{5,1},{2,6},{6,2},{3,7},{7,3},{8,12},{12,8},{9,1... | collective-permute-start | bytes 3145736 | tf_op jit(solution)/shard_map/ppermute | solution.py:45
  17.4 11.6 %collective-permute-start = (bf16[2048,256]{1,0:T(8,128)(2,1)}, bf16[2048,256]{1,0:T(8,128)(2,1)}, u32[]{:S(2)}, u32[]{:S(2)}) collective-permute-start(bf16[2048,256]{1,0:T(8,128)(2,1)} %bitcast.119), channel_id=1, source_target_pairs={{0,4},{4,0},{1,5},{5,1},{2,6},{6,2},{3,7},{7,3},{8,12},{12,8},{9,1... | collective-permute-start | bytes 3145736 | tf_op jit(solution)/shard_map/ppermute | solution.py:45
  27.2 1.8 copy-start.2
  31.0 91.5 %copy-start.7 = (s32[64,8]{0,1:T(8,128)S(1)}, s32[64,8]{0,1:T(8,128)}, u32[]{:S(2)}) copy-start(s32[64,8]{0,1:T(8,128)} %param.7) | copy-start | bytes 6148
  31.0 90.8 %all-to-all-start.3 = ((bf16[64,96,256]{2,1,0:T(8,128)(2,1)}), bf16[64,96,256]{2,1,0:T(8,128)(2,1)S(1)}, u32[]{:S(2)}, u32[]{:S(2)}) async-start(bf16[64,96,256]{2,1,0:T(8,128)(2,1)} %bitcast.37), calls=%async_computation.3 | async-start | bytes 6291456 | tf_op jit(solution)/shard_map/all_to_all | solution.py:59
  43.6 188.4 %all-gather.3.cloned.1.call-start = ((), (), s32[]{:S(2)}) async-start(), calls=%async_computation.6 | async-start | bytes 3194880 | tf_op jit(solution)/shard_map/all_gather | solution.py:61
  189.7 34.9 %copy-start.3 = (bf16[1,2048,256]{2,1,0:T(8,128)(2,1)S(1)}, bf16[1,2048,256]{2,1,0:T(8,128)(2,1)}, u32[]{:S(2)}) copy-start(bf16[1,2048,256]{2,1,0:T(8,128)(2,1)} %param.9) | copy-start | bytes 3145732
  224.6 2.7 copy-start.1
  224.6 2.0 copy-start.4
  228.4 16.7 %all-to-all-start.2 = ((bf16[4,128,1,4,256]{4,1,3,2,0:T(8,128)(2,1)}), bf16[4,128,1,4,256]{4,1,3,2,0:T(8,128)(2,1)S(1)}, u32[]{:S(2)}, u32[]{:S(2)}) async-start(bf16[4,128,1,4,256]{4,1,3,2,0:T(8,128)(2,1)} %broadcast_in_dim.70), calls=%async_computation.2 | async-start | bytes 2097152 | tf_op jit(solution)/shard_map/all_to_all | solution.py:15
  234.1 15.4 %copy-start.5 = (bf16[1,1024,512]{2,1,0:T(8,128)(2,1)S(1)}, bf16[1,1024,512]{2,1,0:T(8,128)(2,1)}, u32[]{:S(2)}) copy-start(bf16[1,1024,512]{2,1,0:T(8,128)(2,1)} %param.11) | copy-start | bytes 3145732
  245.9 8.9 %all-to-all-start.4 = ((bf16[4,128,1,256]{3,1,2,0:T(8,128)(2,1)}), bf16[4,128,1,256]{3,1,2,0:T(8,128)(2,1)S(1)}, u32[]{:S(2)}, u32[]{:S(2)}) async-start(bf16[4,128,1,256]{3,1,2,0:T(8,128)(2,1)} %broadcast_in_dim.71), calls=%async_computation.4 | async-start | bytes 524288 | tf_op jit(solution)/shard_map/all_to_all | solution.py:15
  251.0 4.1 %copy-start.6 = (bf16[128,4,512]{2,0,1:T(8,128)(2,1)S(1)}, bf16[128,4,512]{2,0,1:T(8,128)(2,1)}, u32[]{:S(2)}) copy-start(bf16[128,4,512]{2,0,1:T(8,128)(2,1)} %fusion) | copy-start | bytes 1572868
  251.4 15.7 %copy-start.8 = (f32[64,8]{0,1:T(8,128)S(1)}, f32[64,8]{0,1:T(8,128)}, u32[]{:S(2)}) copy-start(f32[64,8]{0,1:T(8,128)} %param.8) | copy-start | bytes 6148
  256.5 41.2 %all-to-all-start.5 = ((bf16[128,5,512]{2,1,0:T(8,128)(2,1)}), bf16[128,5,512]{2,1,0:T(8,128)(2,1)S(1)}, u32[]{:S(2)}, u32[]{:S(2)}) async-start(bf16[128,5,512]{2,1,0:T(8,128)(2,1)} %copy.77), calls=%async_computation.5 | async-start | bytes 2097152 | tf_op jit(solution)/shard_map/all_to_all | solution.py:138
Sparse Core Ops, SparseCore 0:
  122.6 109.4 all-gather.2

commit v8 on v7

--- a/solution.py
+++ b/solution.py
@@ -11,8 +11,14 @@
 
 
 def gather_dp(x, dp_count):
-    stacked = jnp.broadcast_to(x[None], (dp_count,) + x.shape)
-    return lax.all_to_all(stacked, "dp", split_axis=0, concat_axis=0, tiled=True)
+    parts = [x] + [
+        lax.ppermute(x, "dp", [(i, (i + k) % dp_count) for i in range(dp_count)])
+        for k in range(1, dp_count)
+    ]
+    stacked = jnp.stack(parts)
+    here = lax.axis_index("dp")
+    order = (here - jnp.arange(dp_count, dtype=jnp.int32)) % dp_count
+    return jnp.take(stacked, order, axis=0)
 
 
 def silu_product(gate_part, up_part):

time: 309 us -> 327 us (1.058)
  blocking collectives: 92.1 us -> 58.6 us
  waiting for transfers between devices: 117 us -> 150 us
  starting transfers between devices: 43.2 us -> 56.1 us
  other arithmetic: 9.24 us -> 13.2 us
    ppermute x0 -> x9, waiting for transfers between devices: none -> 43.8 us  [gather_dp(): lax.ppermute(x, 'dp', [(i, (i + k) % dp_count) for i in range(dp_count)])]
    all_to_all x1 -> x0, blocking collectives: 34.8 us -> none  [gather_dp(): lax.all_to_all(stacked, 'dp', split_axis=0, concat_axis=0, tiled=True)]
    ppermute x0 -> x9, starting transfers between devices: none -> 23.8 us  [gather_dp(): lax.ppermute(x, 'dp', [(i, (i + k) % dp_count) for i in range(dp_count)])]
    all_to_all x2 -> x0, waiting for transfers between devices: 11.7 us -> none  [gather_dp(): lax.all_to_all(stacked, 'dp', split_axis=0, concat_axis=0, tiled=True)]
    all_to_all x2 -> x0, starting transfers between devices: 7.1 us -> none  [gather_dp(): lax.all_to_all(stacked, 'dp', split_axis=0, concat_axis=0, tiled=True)]
    gather x0 -> x3, local copies, waits for them, and re-layouts: none -> 3.44 us  [gather_dp(): return jnp.take(stacked, order, axis=0)]
  transfers between devices with their start and end apart: 8 -> 15, of which waited for: 4 -> 9; matrix products, arithmetic and copies ran while one was open for 9% -> 9% of each run, Pallas kernels for 0% -> 0%
where the time goes in v8:
time: 327 us; the launch traced here: 326 us
  waiting for transfers between devices  150 us (46%)
  blocking collectives  58.6 us (18%)
  starting transfers between devices  56.1 us (17%)
  local copies, waits for them, and re-layouts  25.3 us (8%)
  between operations  17.9 us (5%)
  other arithmetic  13.2 us (4%)
  matrix products  5.29 us (2%)
    all_to_all x1, waiting for transfers between devices, local(): lax.all_to_all(blocks, 'eph', split_axis=0, concat_axis=0, tiled=True)  75.7 us
    all_to_all x1, blocking collectives, local(): lax.all_to_all(outgoing, EP, split_axis=0, concat_axis=0, tiled=True)  58.6 us
    ppermute x9, waiting for transfers between devices, gather_dp(): lax.ppermute(x, 'dp', [(i, (i + k) % dp_count) for i in range(dp_count)])  43.8 us
    all_to_all x1, waiting for transfers between devices, local(): lax.all_to_all(results, EP, split_axis=0, concat_axis=0, tiled=True)  30.2 us
    ppermute x9, starting transfers between devices, gather_dp(): lax.ppermute(x, 'dp', [(i, (i + k) % dp_count) for i in range(dp_count)])  23.8 us
    ppermute x3, starting transfers between devices, local(): swapped = tuple((lax.ppermute(w, 'c', [(0, 1), (1, 0)]) for w in own))  13.2 us
    all_to_all x1, starting transfers between devices, local(): lax.all_to_all(blocks, 'eph', split_axis=0, concat_axis=0, tiled=True)  11.1 us
    all_to_all x1, starting transfers between devices, local(): lax.all_to_all(results, EP, split_axis=0, concat_axis=0, tiled=True)  8.01 us
  transfers between devices with their start and end apart: 15, of which 9 were waited for; matrix products, arithmetic and copies ran while one was open for 9% of the time, Pallas kernels for 0%

profile of v8, /device:TPU:1, one launch (start us, length us, event | category | flops | bytes accessed | tf_op | source)
XLA Modules:
  0.0 326.2 jit_solution(9933363004007859108)
XLA Ops:
  6.5 8.9 %collective-permute-start.2 = (bf16[1024,512]{1,0:T(8,128)(2,1)}, bf16[1024,512]{1,0:T(8,128)(2,1)S(1)}, u32[]{:S(2)}, u32[]{:S(2)}) collective-permute-start(bf16[1024,512]{1,0:T(8,128)(2,1)} %bitcast.126), channel_id=1, source_target_pairs={{0,4},{4,0},{1,5},{5,1},{2,6},{6,2},{3,7},{7,3},{8,12},{12,8},{9,1... | collective-permute-start | bytes 3145736 | tf_op jit(solution)/shard_map/ppermute | solution.py:51
  15.5 1.9 collective-permute-start.1
  17.4 2.4 collective-permute-start
  21.5 2.5 top_k.11
  31.0 11.1 %all-to-all-start.1 = ((bf16[64,96,256]{2,1,0:T(8,128)(2,1)}), bf16[64,96,256]{2,1,0:T(8,128)(2,1)S(1)}, u32[]{:S(2)}, u32[]{:S(2)}) async-start(bf16[64,96,256]{2,1,0:T(8,128)(2,1)} %bitcast.45), calls=%async_computation.1 | async-start | bytes 6291456 | tf_op jit(solution)/shard_map/all_to_all | solution.py:65
  44.7 75.7 %all-to-all-done.1 = bf16[64,96,256]{2,1,0:T(8,128)(2,1)S(1)} async-done(((bf16[64,96,256]{2,1,0:T(8,128)(2,1)}), bf16[64,96,256]{2,1,0:T(8,128)(2,1)S(1)}, u32[]{:S(2)}, u32[]{:S(2)}) %all-to-all-start.1) | async-done | bytes 3145760 | tf_op jit(solution)/shard_map/all_to_all | solution.py:65
  121.6 2.4 scatter_custom_fusion
  124.3 2.4 scatter_custom_fusion.1
  127.4 2.8 gather_fusion
  130.6 58.6 %all_to_all.15 = bf16[128,5,512]{2,1,0:T(8,128)(2,1)S(1)} all-to-all(bf16[128,5,512]{2,1,0:T(8,128)(2,1)S(1)} %broadcast_select_fusion), channel_id=1, replica_groups=mesh['eph'=64,'c'=2,'dp'=4] {'eph','c'}, dimensions={0} | all-to-all | bytes 1310720 | tf_op jit(solution)/shard_map/all_to_all | solution.py:102
  190.3 4.4 %collective-permute-start.5 = (bf16[128,5,512]{2,0,1:T(8,128)(2,1)}, bf16[128,5,512]{2,0,1:T(8,128)(2,1)S(1)}, u32[]{:S(2)}, u32[]{:S(2)}) collective-permute-start(bf16[128,5,512]{2,0,1:T(8,128)(2,1)} %copy.79), channel_id=1, source_target_pairs={{0,3},{1,0},{2,1},{3,2},{4,7},{5,4},{6,5},{7,6},{8,11},{9,8},{10,9... | collective-permute-start | bytes 1966088 | tf_op jit(solution)/shard_map/ppermute | solution.py:15
  194.7 2.3 collective-permute-start.4
  197.0 2.5 collective-permute-start.3
  199.8 9.6 %collective-permute-done.5 = bf16[128,5,512]{2,0,1:T(8,128)(2,1)S(1)} collective-permute-done((bf16[128,5,512]{2,0,1:T(8,128)(2,1)}, bf16[128,5,512]{2,0,1:T(8,128)(2,1)S(1)}, u32[]{:S(2)}, u32[]{:S(2)}) %collective-permute-start.5) | collective-permute-done | bytes 655392 | tf_op jit(solution)/shard_map/ppermute | solution.py:15
  209.4 4.5 %collective-permute-done.4 = bf16[128,5,512]{2,0,1:T(8,128)(2,1)S(1)} collective-permute-done((bf16[128,5,512]{2,0,1:T(8,128)(2,1)}, bf16[128,5,512]{2,0,1:T(8,128)(2,1)S(1)}, u32[]{:S(2)}, u32[]{:S(2)}) %collective-permute-start.4) | collective-permute-done | bytes 655392 | tf_op jit(solution)/shard_map/ppermute | solution.py:15
  213.9 15.1 %collective-permute-done.3 = bf16[128,5,512]{2,0,1:T(8,128)(2,1)S(1)} collective-permute-done((bf16[128,5,512]{2,0,1:T(8,128)(2,1)}, bf16[128,5,512]{2,0,1:T(8,128)(2,1)S(1)}, u32[]{:S(2)}, u32[]{:S(2)}) %collective-permute-start.3) | collective-permute-done | bytes 655392 | tf_op jit(solution)/shard_map/ppermute | solution.py:15
  231.5 2.3 gather_fusion.1
  233.7 2.1 copy_select_fusion
  238.6 1.9 collective-permute-start.8
  240.5 2.5 collective-permute-start.7
  243.0 3.0 collective-permute-start.6
  246.0 1.9 collective-permute-done.8
  247.9 2.7 collective-permute-done.7
  250.6 7.2 %collective-permute-done.6 = bf16[128,1,4,256]{3,0,2,1:T(8,128)(2,1)S(1)} collective-permute-done((bf16[128,1,4,256]{3,0,2,1:T(8,128)(2,1)S(1)}, bf16[128,1,4,256]{3,0,2,1:T(8,128)(2,1)S(1)}, u32[]{:S(2)}, u32[]{:S(2)}) %collective-permute-start.6) | collective-permute-done | bytes 262176 | tf_op jit(solution)/shard_map/ppermute | solution.py:15
  258.6 2.1 fusion.47
  263.4 1.9 collective-permute-start.11
  265.4 2.2 collective-permute-start.10
  267.6 3.0 collective-permute-start.9
  271.9 2.8 collective-permute-done.9
  277.1 8.0 %all-to-all-start.2 = ((bf16[128,5,512]{2,1,0:T(8,128)(2,1)}), bf16[128,5,512]{2,1,0:T(8,128)(2,1)S(1)}, u32[]{:S(2)}, u32[]{:S(2)}) async-start(bf16[128,5,512]{2,1,0:T(8,128)(2,1)} %copy.84), calls=%async_computation.2 | async-start | bytes 2097152 | tf_op jit(solution)/shard_map/all_to_all | solution.py:144
  285.9 30.2 %all-to-all-done.2 = bf16[128,5,512]{2,1,0:T(8,128)(2,1)S(1)} async-done(((bf16[128,5,512]{2,1,0:T(8,128)(2,1)}), bf16[128,5,512]{2,1,0:T(8,128)(2,1)S(1)}, u32[]{:S(2)}, u32[]{:S(2)}) %all-to-all-start.2) | async-done | bytes 655392 | tf_op jit(solution)/shard_map/all_to_all | solution.py:144
  316.3 2.0 gather_fusion.4
  (102 shorter events, 25.3 us)
Async XLA Ops:
  6.5 120.8 %copy-start = (bf16[64,512]{1,0:T(8,128)(2,1)S(1)}, bf16[64,512]{1,0:T(8,128)(2,1)}, u32[]{:S(2)}) copy-start(bf16[64,512]{1,0:T(8,128)(2,1)} %param.6) | copy-start | bytes 196612
  6.5 19.3 %collective-permute-start.2 = (bf16[1024,512]{1,0:T(8,128)(2,1)}, bf16[1024,512]{1,0:T(8,128)(2,1)S(1)}, u32[]{:S(2)}, u32[]{:S(2)}) collective-permute-start(bf16[1024,512]{1,0:T(8,128)(2,1)} %bitcast.126), channel_id=1, source_target_pairs={{0,4},{4,0},{1,5},{5,1},{2,6},{6,2},{3,7},{7,3},{8,12},{12,8},{9,1... | collective-permute-start | bytes 3145736 | tf_op jit(solution)/shard_map/ppermute | solution.py:51
  15.5 12.2 %collective-permute-start.1 = (bf16[2048,256]{1,0:T(8,128)(2,1)}, bf16[2048,256]{1,0:T(8,128)(2,1)}, u32[]{:S(2)}, u32[]{:S(2)}) collective-permute-start(bf16[2048,256]{1,0:T(8,128)(2,1)} %bitcast.124), channel_id=1, source_target_pairs={{0,4},{4,0},{1,5},{5,1},{2,6},{6,2},{3,7},{7,3},{8,12},{12,8},{9,1... | collective-permute-start | bytes 3145736 | tf_op jit(solution)/shard_map/ppermute | solution.py:51
  17.4 11.6 %collective-permute-start = (bf16[2048,256]{1,0:T(8,128)(2,1)}, bf16[2048,256]{1,0:T(8,128)(2,1)}, u32[]{:S(2)}, u32[]{:S(2)}) collective-permute-start(bf16[2048,256]{1,0:T(8,128)(2,1)} %bitcast.122), channel_id=1, source_target_pairs={{0,4},{4,0},{1,5},{5,1},{2,6},{6,2},{3,7},{7,3},{8,12},{12,8},{9,1... | collective-permute-start | bytes 3145736 | tf_op jit(solution)/shard_map/ppermute | solution.py:51
  27.2 1.8 copy-start.2
  31.0 90.1 %copy-start.8 = (s32[64,8]{0,1:T(8,128)S(1)}, s32[64,8]{0,1:T(8,128)}, u32[]{:S(2)}) copy-start(s32[64,8]{0,1:T(8,128)} %param.7) | copy-start | bytes 6148
  31.0 89.4 %all-to-all-start.1 = ((bf16[64,96,256]{2,1,0:T(8,128)(2,1)}), bf16[64,96,256]{2,1,0:T(8,128)(2,1)S(1)}, u32[]{:S(2)}, u32[]{:S(2)}) async-start(bf16[64,96,256]{2,1,0:T(8,128)(2,1)} %bitcast.45), calls=%async_computation.1 | async-start | bytes 6291456 | tf_op jit(solution)/shard_map/all_to_all | solution.py:65
  42.1 216.5 %all-gather.3.cloned.1.call-start = ((), (), s32[]{:S(2)}) async-start(), calls=%async_computation.3 | async-start | bytes 3194880 | tf_op jit(solution)/shard_map/all_gather | solution.py:67
  190.3 19.1 %collective-permute-start.5 = (bf16[128,5,512]{2,0,1:T(8,128)(2,1)}, bf16[128,5,512]{2,0,1:T(8,128)(2,1)S(1)}, u32[]{:S(2)}, u32[]{:S(2)}) collective-permute-start(bf16[128,5,512]{2,0,1:T(8,128)(2,1)} %copy.79), channel_id=1, source_target_pairs={{0,3},{1,0},{2,1},{3,2},{4,7},{5,4},{6,5},{7,6},{8,11},{9,8},{10,9... | collective-permute-start | bytes 1966088 | tf_op jit(solution)/shard_map/ppermute | solution.py:15
  194.7 19.2 %collective-permute-start.4 = (bf16[128,5,512]{2,0,1:T(8,128)(2,1)}, bf16[128,5,512]{2,0,1:T(8,128)(2,1)S(1)}, u32[]{:S(2)}, u32[]{:S(2)}) collective-permute-start(bf16[128,5,512]{2,0,1:T(8,128)(2,1)} %copy.79), channel_id=1, source_target_pairs={{0,2},{1,3},{2,0},{3,1},{4,6},{5,7},{6,4},{7,5},{8,10},{9,11},{10,... | collective-permute-start | bytes 1966088 | tf_op jit(solution)/shard_map/ppermute | solution.py:15
  197.0 32.0 %collective-permute-start.3 = (bf16[128,5,512]{2,0,1:T(8,128)(2,1)}, bf16[128,5,512]{2,0,1:T(8,128)(2,1)S(1)}, u32[]{:S(2)}, u32[]{:S(2)}) collective-permute-start(bf16[128,5,512]{2,0,1:T(8,128)(2,1)} %copy.79), channel_id=1, source_target_pairs={{0,1},{1,2},{2,3},{3,0},{4,5},{5,6},{6,7},{7,4},{8,9},{9,10},{10,1... | collective-permute-start | bytes 1966088 | tf_op jit(solution)/shard_map/ppermute | solution.py:15
  213.9 15.1 %copy-start.6 = (bf16[128,5,512]{2,0,1:T(8,128)(2,1)}, bf16[128,5,512]{2,0,1:T(8,128)(2,1)S(1)}, u32[]{:S(2)}) copy-start(bf16[128,5,512]{2,0,1:T(8,128)(2,1)S(1)} %collective-permute-done.4) | copy-start | bytes 1966084
  229.0 0.8 copy-start.7
  233.7 2.2 copy-start.3
  235.9 2.7 copy-start.1
  235.9 2.0 copy-start.4
  238.6 9.3 %collective-permute-start.8 = (bf16[128,1,4,256]{3,0,2,1:T(8,128)(2,1)S(1)}, bf16[128,1,4,256]{3,0,2,1:T(8,128)(2,1)S(1)}, u32[]{:S(2)}, u32[]{:S(2)}) collective-permute-start(bf16[128,1,4,256]{3,0,2,1:T(8,128)(2,1)S(1)} %fusion.2), channel_id=1, source_target_pairs={{0,3},{1,0},{2,1},{3,2},{4,7},{5,4},{6,5},{7,6},{8,11},{9,8},{10,9... | collective-permute-start | bytes 786440 | tf_op jit(solution)/shard_map/ppermute | solution.py:15
  240.5 10.1 %collective-permute-start.7 = (bf16[128,1,4,256]{3,0,2,1:T(8,128)(2,1)S(1)}, bf16[128,1,4,256]{3,0,2,1:T(8,128)(2,1)S(1)}, u32[]{:S(2)}, u32[]{:S(2)}) collective-permute-start(bf16[128,1,4,256]{3,0,2,1:T(8,128)(2,1)S(1)} %fusion.2), channel_id=1, source_target_pairs={{0,2},{1,3},{2,0},{3,1},{4,6},{5,7},{6,4},{7,5},{8,10},{9,11},{10,... | collective-permute-start | bytes 786440 | tf_op jit(solution)/shard_map/ppermute | solution.py:15
  243.0 14.8 %collective-permute-start.6 = (bf16[128,1,4,256]{3,0,2,1:T(8,128)(2,1)S(1)}, bf16[128,1,4,256]{3,0,2,1:T(8,128)(2,1)S(1)}, u32[]{:S(2)}, u32[]{:S(2)}) collective-permute-start(bf16[128,1,4,256]{3,0,2,1:T(8,128)(2,1)S(1)} %fusion.2), channel_id=1, source_target_pairs={{0,1},{1,2},{2,3},{3,0},{4,5},{5,6},{6,7},{7,4},{8,9},{9,10},{10,1... | collective-permute-start | bytes 786440 | tf_op jit(solution)/shard_map/ppermute | solution.py:15
  260.6 10.0 %copy-start.5 = (bf16[1,1024,512]{2,1,0:T(8,128)(2,1)S(1)}, bf16[1,1024,512]{2,1,0:T(8,128)(2,1)}, u32[]{:S(2)}) copy-start(bf16[1,1024,512]{2,1,0:T(8,128)(2,1)} %param.11) | copy-start | bytes 3145732
  263.4 8.4 %collective-permute-start.11 = (bf16[128,1,256]{2,0,1:T(8,128)(2,1)S(1)}, bf16[128,1,256]{2,0,1:T(8,128)(2,1)S(1)}, u32[]{:S(2)}, u32[]{:S(2)}) collective-permute-start(bf16[128,1,256]{2,0,1:T(8,128)(2,1)S(1)} %bitcast.137), channel_id=1, source_target_pairs={{0,3},{1,0},{2,1},{3,2},{4,7},{5,4},{6,5},{7,6},{8,11},{9,8},{10,9... | collective-permute-start | bytes 196616 | tf_op jit(solution)/shard_map/ppermute | solution.py:15
  265.4 6.5 %collective-permute-start.10 = (bf16[128,1,256]{2,0,1:T(8,128)(2,1)S(1)}, bf16[128,1,256]{2,0,1:T(8,128)(2,1)S(1)}, u32[]{:S(2)}, u32[]{:S(2)}) collective-permute-start(bf16[128,1,256]{2,0,1:T(8,128)(2,1)S(1)} %bitcast.138), channel_id=1, source_target_pairs={{0,2},{1,3},{2,0},{3,1},{4,6},{5,7},{6,4},{7,5},{8,10},{9,11},{10,... | collective-permute-start | bytes 196616 | tf_op jit(solution)/shard_map/ppermute | solution.py:15
  267.6 7.1 %collective-permute-start.9 = (bf16[128,1,256]{2,0,1:T(8,128)(2,1)S(1)}, bf16[128,1,256]{2,0,1:T(8,128)(2,1)S(1)}, u32[]{:S(2)}, u32[]{:S(2)}) collective-permute-start(bf16[128,1,256]{2,0,1:T(8,128)(2,1)S(1)} %bitcast.139), channel_id=1, source_target_pairs={{0,1},{1,2},{2,3},{3,0},{4,5},{5,6},{6,7},{7,4},{8,9},{9,10},{10,1... | collective-permute-start | bytes 196616 | tf_op jit(solution)/shard_map/ppermute | solution.py:15
  275.7 9.7 %copy-start.9 = (f32[64,8]{0,1:T(8,128)S(1)}, f32[64,8]{0,1:T(8,128)}, u32[]{:S(2)}) copy-start(f32[64,8]{0,1:T(8,128)} %param.8) | copy-start | bytes 6148
  277.1 38.9 %all-to-all-start.2 = ((bf16[128,5,512]{2,1,0:T(8,128)(2,1)}), bf16[128,5,512]{2,1,0:T(8,128)(2,1)S(1)}, u32[]{:S(2)}, u32[]{:S(2)}) async-start(bf16[128,5,512]{2,1,0:T(8,128)(2,1)} %copy.84), calls=%async_computation.2 | async-start | bytes 2097152 | tf_op jit(solution)/shard_map/all_to_all | solution.py:144
Sparse Core Ops, SparseCore 0:
  121.2 110.7 all-gather.2

commit v9 on v7

--- a/solution.py
+++ b/solution.py
@@ -56,14 +56,6 @@
         [contrib[0], contrib[1], contrib[2].reshape(-1, contrib[0].shape[1])], axis=0
     )
     blocks = packed.reshape(pair_count, -1, packed.shape[1])
-    pieces = lax.all_to_all(blocks, "eph", split_axis=0, concat_axis=0, tiled=True)
-    piece = lax.dynamic_index_in_dim(pieces, hot_ids[parity] // HOT, axis=0, keepdims=False)
-    spread_back = lax.all_gather(piece, "eph", axis=0, tiled=True)
-    model_rows = contrib[0].shape[0]
-    spare_gate = spread_back[:model_rows]
-    spare_up = spread_back[model_rows : 2 * model_rows]
-    spare_down = spread_back[2 * model_rows :].reshape(contrib[2].shape)
-    tokens, contrib = lax.optimization_barrier((tokens, contrib))
 
     earlier = jnp.cumsum(matches, axis=0) - matches
     order_rank = jnp.sum(earlier * matches, axis=1)
@@ -93,7 +85,21 @@
         axis=1,
     )
     outgoing = jnp.take(tokens, source_row, axis=0, mode="fill", fill_value=0)
-    arrived = lax.all_to_all(outgoing, EP, split_axis=0, concat_axis=0, tiled=True)
+    paired = outgoing.reshape(pair_count, HOT, -1, slice_width)
+    paired = lax.all_to_all(paired, "c", split_axis=1, concat_axis=1, tiled=True)
+    piece_size = blocks.shape[1] * blocks.shape[2]
+    merged = jnp.concatenate(
+        [blocks.reshape(pair_count, -1), paired.reshape(pair_count, -1)], axis=1
+    )
+    merged = lax.all_to_all(merged, "eph", split_axis=0, concat_axis=0, tiled=True)
+    pieces = merged[:, :piece_size].reshape(blocks.shape)
+    arrived = merged[:, piece_size:].reshape(ep_count, -1, slice_width)
+    piece = lax.dynamic_index_in_dim(pieces, hot_ids[parity] // HOT, axis=0, keepdims=False)
+    spread_back = lax.all_gather(piece, "eph", axis=0, tiled=True)
+    model_rows = contrib[0].shape[0]
+    spare_gate = spread_back[:model_rows]
+    spare_up = spread_back[model_rows : 2 * model_rows]
+    spare_down = spread_back[2 * model_rows :].reshape(contrib[2].shape)
     incoming = gather_dp(arrived, dp_count)
     primary_rows = incoming[:, :, :primary_slots].reshape(
         dp_count, ep_count, exp_dev, capacity, slice_width

time: 309 us -> 376 us (1.22)
  waiting for transfers between devices: 117 us -> 183 us
  blocking collectives: 92.1 us -> 34.3 us
  local copies, waits for them, and re-layouts: 22.1 us -> 64.8 us
  other arithmetic: 9.24 us -> 18 us
  starting transfers between devices: 43.2 us -> 50.4 us
    all_to_all x1 -> x0, blocking collectives: 57.2 us -> none  [local(): lax.all_to_all(outgoing, EP, split_axis=0, concat_axis=0, tiled=True)]
    all_gather x1, waiting for transfers between devices: 0.05 us -> 56.1 us  [local(): spread_back = lax.all_gather(piece, 'eph', axis=0, tiled=True)]
    unnamed x21 -> x33, local copies, waits for them, and re-layouts: 2.19 us -> 35 us
    all_to_all x1 -> x2, waiting for transfers between devices: 75.6 us -> 93.1 us  [the longest x1 93 us: local(): lax.all_to_all(merged, 'eph', split_axis=0, concat_axis=0, tiled=True)]
    all_to_all x0 -> x2, other arithmetic: none -> 10.5 us  [local(): lax.all_to_all(merged, 'eph', split_axis=0, concat_axis=0, tiled=True)]
    all_to_all x2, waiting for transfers between devices: 11.7 us -> 3.63 us  [gather_dp(): lax.all_to_all(stacked, 'dp', split_axis=0, concat_axis=0, tiled=True)]
    all_to_all x1, starting transfers between devices: 10.3 us -> 14.9 us  [local(): lax.all_to_all(results, EP, split_axis=0, concat_axis=0, tiled=True)]
    all_to_all x1 -> x2, starting transfers between devices: 12.6 us -> 14.7 us  [the longest x1 11.2 us: local(): lax.all_to_all(merged, 'eph', split_axis=0, concat_axis=0, tiled=True)]
  transfers between devices with their start and end apart: 8 -> 9, of which waited for: 4 -> 4; matrix products, arithmetic and copies ran while one was open for 9% -> 9% of each run, Pallas kernels for 0% -> 0%
where the time goes in v9:
time: 376 us; the launch traced here: 374 us
  waiting for transfers between devices  183 us (49%)
  local copies, waits for them, and re-layouts  64.8 us (17%)
  starting transfers between devices  50.4 us (13%)
  blocking collectives  34.3 us (9%)
  other arithmetic  18 us (5%)
  between operations  17.8 us (5%)
  matrix products  6.01 us (2%)
    all_to_all x1, waiting for transfers between devices, local(): lax.all_to_all(merged, 'eph', split_axis=0, concat_axis=0, tiled=True)  93 us
    all_gather x1, waiting for transfers between devices, local(): spread_back = lax.all_gather(piece, 'eph', axis=0, tiled=True)  56.1 us
    unnamed x33, local copies, waits for them, and re-layouts  35 us
    all_to_all x1, blocking collectives, gather_dp(): lax.all_to_all(stacked, 'dp', split_axis=0, concat_axis=0, tiled=True)  34.3 us
    all_to_all x1, waiting for transfers between devices, local(): lax.all_to_all(results, EP, split_axis=0, concat_axis=0, tiled=True)  30.2 us
    all_to_all x1, starting transfers between devices, local(): lax.all_to_all(results, EP, split_axis=0, concat_axis=0, tiled=True)  14.9 us
    ppermute x3, starting transfers between devices, local(): swapped = tuple((lax.ppermute(w, 'c', [(0, 1), (1, 0)]) for w in own))  13.2 us
    all_to_all x1, starting transfers between devices, local(): lax.all_to_all(merged, 'eph', split_axis=0, concat_axis=0, tiled=True)  11.2 us
  transfers between devices with their start and end apart: 9, of which 4 were waited for; matrix products, arithmetic and copies ran while one was open for 9% of the time, Pallas kernels for 0%

profile of v9, /device:TPU:1, one launch (start us, length us, event | category | flops | bytes accessed | tf_op | source)
XLA Modules:
  0.0 374.2 jit_solution(10942389703400213088)
XLA Ops:
  6.5 8.9 %collective-permute-start.2 = (bf16[1024,512]{1,0:T(8,128)(2,1)}, bf16[1024,512]{1,0:T(8,128)(2,1)}, u32[]{:S(2)}, u32[]{:S(2)}) collective-permute-start(bf16[1024,512]{1,0:T(8,128)(2,1)} %bitcast.132), channel_id=1, source_target_pairs={{0,4},{4,0},{1,5},{5,1},{2,6},{6,2},{3,7},{7,3},{8,12},{12,8},{9,1... | collective-permute-start | bytes 3145736 | tf_op jit(solution)/shard_map/ppermute | solution.py:45
  15.5 1.9 collective-permute-start.1
  17.4 2.4 collective-permute-start
  22.1 2.5 top_k.11
  25.2 2.4 scatter_custom_fusion
  27.9 2.4 scatter_custom_fusion.1
  30.9 2.8 gather_fusion
  35.8 3.5 all-to-all-start
  41.6 1.6 reshape.427
  43.2 1.3 select_select_fusion
  47.6 2.9 reshape_reshape.6
  50.5 4.2 %maximum_bitcast_fusion = bf16[64,1,29696]{2,0,1:T(8,128)(2,1)} fusion(bf16[64,5120]{1,0:T(8,128)(2,1)} %reshape.427, bf16[64,24576]{1,0:T(8,128)(2,1)} %reshape_reshape.6), kind=kLoop, calls=%fused_computation.4 | loop fusion | flops 7602176 | bytes 7602176 | tf_op jit(solution)/shard_map/all_to_all | solution.py:94
  55.3 6.4 %reduce = bf16[64,29696]{1,0:T(8,128)(2,1)} reduce(bf16[64,1,29696]{2,0,1:T(8,128)(2,1)} %maximum_bitcast_fusion, bf16[]{:T(256)} %broadcast.635), dimensions={1}, to_apply=%copy.103.reduce_sub_computation | reduce | bytes 7602178 | tf_op jit(solution)/shard_map/all_to_all | solution.py:94
  61.7 5.8 %reshape.492 = bf16[64,2,14848]{2,1,0:T(2,128)(2,1)} reshape(bf16[64,29696]{1,0:T(8,128)(2,1)} %reduce) | data formatting | bytes 7602176
  67.5 11.2 %all-to-all-start.1 = ((bf16[64,2,14848]{2,1,0:T(2,128)(2,1)}), bf16[64,2,14848]{2,1,0:T(2,128)(2,1)}, u32[]{:S(2)}, u32[]{:S(2)}) async-start(bf16[64,2,14848]{2,1,0:T(2,128)(2,1)} %reshape.492), calls=%async_computation.1 | async-start | bytes 7602176 | tf_op jit(solution)/shard_map/all_to_all | solution.py:94
  81.3 93.0 %all-to-all-done.1 = bf16[64,2,14848]{2,1,0:T(2,128)(2,1)} async-done(((bf16[64,2,14848]{2,1,0:T(2,128)(2,1)}), bf16[64,2,14848]{2,1,0:T(2,128)(2,1)}, u32[]{:S(2)}, u32[]{:S(2)}) %all-to-all-start.1) | async-done | bytes 3801120 | tf_op jit(solution)/shard_map/all_to_all | solution.py:94
  174.3 19.2 %reshape.493 = bf16[64,1,29696]{2,1,0:T(2,128)(2,1)} reshape(bf16[64,2,14848]{2,1,0:T(2,128)(2,1)} %all-to-all-done.1) | data formatting | bytes 7602176
  193.5 4.4 %copy.122 = bf16[64,1,29696]{2,0,1:T(8,128)(2,1)S(1)} copy(bf16[64,1,29696]{2,1,0:T(2,128)(2,1)} %reshape.493) | data formatting | bytes 7602176
  198.1 1.6 copy-done.2
  203.6 34.3 %all_to_all.37 = bf16[4,128,5,512]{3,1,2,0:T(8,128)(2,1)S(1)} all-to-all(bf16[4,128,5,512]{3,1,2,0:T(8,128)(2,1)S(1)} %broadcast_in_dim.70), channel_id=1, replica_groups=mesh['eph'=64,'c'=2,'dp'=4] {'dp'}, dimensions={0} | all-to-all | bytes 5242880 | tf_op jit(solution)/shard_map/all_to_all | solution.py:15
  241.8 3.5 all-to-all-start.3
  245.3 56.1 %all-gather.3.cloned.1.call-done = bf16[1,6144,256]{2,1,0:T(8,128)(2,1)} async-done(((bf16[1,96,256]{2,1,0:T(8,128)(2,1)}), bf16[1,6144,256]{2,1,0:T(8,128)(2,1)}) %all-gather.3.cloned.1.call-update) | async-done | bytes 3145744 | tf_op jit(solution)/shard_map/all_gather | solution.py:98
  301.3 2.1 fusion.40
  303.4 1.4 convolution_bitcast_fusion.5
  304.9 1.4 fusion.7
  307.0 4.0 %all-to-all-start.4 = ((bf16[4,128,1,256]{3,1,2,0:T(8,128)(2,1)}), bf16[4,128,1,256]{3,1,2,0:T(8,128)(2,1)S(1)}, u32[]{:S(2)}, u32[]{:S(2)}) async-start(bf16[4,128,1,256]{3,1,2,0:T(8,128)(2,1)} %broadcast_in_dim.73), calls=%async_computation.4 | async-start | bytes 524288 | tf_op jit(solution)/shard_map/all_to_all | solution.py:15
  310.9 1.5 fusion
  312.8 3.6 all-to-all-done.4
  316.8 1.4 copy.108
  318.2 14.9 %all-to-all-start.5 = ((bf16[128,5,512]{2,1,0:T(8,128)(2,1)}), bf16[128,5,512]{2,1,0:T(8,128)(2,1)S(1)}, u32[]{:S(2)}, u32[]{:S(2)}) async-start(bf16[128,5,512]{2,1,0:T(8,128)(2,1)} %copy.108), calls=%async_computation.5 | async-start | bytes 2097152 | tf_op jit(solution)/shard_map/all_to_all | solution.py:144
  333.9 30.2 %all-to-all-done.5 = bf16[128,5,512]{2,1,0:T(8,128)(2,1)S(1)} async-done(((bf16[128,5,512]{2,1,0:T(8,128)(2,1)}), bf16[128,5,512]{2,1,0:T(8,128)(2,1)S(1)}, u32[]{:S(2)}, u32[]{:S(2)}) %all-to-all-start.5) | async-done | bytes 655392 | tf_op jit(solution)/shard_map/all_to_all | solution.py:144
  364.3 2.0 gather_fusion.1
  (104 shorter events, 21.6 us)
Async XLA Ops:
  6.5 24.4 %copy-start = (bf16[64,512]{1,0:T(8,128)(2,1)S(1)}, bf16[64,512]{1,0:T(8,128)(2,1)}, u32[]{:S(2)}) copy-start(bf16[64,512]{1,0:T(8,128)(2,1)} %param.6) | copy-start | bytes 196612
  6.5 36.7 %collective-permute-start.2 = (bf16[1024,512]{1,0:T(8,128)(2,1)}, bf16[1024,512]{1,0:T(8,128)(2,1)}, u32[]{:S(2)}, u32[]{:S(2)}) collective-permute-start(bf16[1024,512]{1,0:T(8,128)(2,1)} %bitcast.132), channel_id=1, source_target_pairs={{0,4},{4,0},{1,5},{5,1},{2,6},{6,2},{3,7},{7,3},{8,12},{12,8},{9,1... | collective-permute-start | bytes 3145736 | tf_op jit(solution)/shard_map/ppermute | solution.py:45
  15.5 30.3 %collective-permute-start.1 = (bf16[2048,256]{1,0:T(8,128)(2,1)}, bf16[2048,256]{1,0:T(8,128)(2,1)}, u32[]{:S(2)}, u32[]{:S(2)}) collective-permute-start(bf16[2048,256]{1,0:T(8,128)(2,1)} %bitcast.130), channel_id=1, source_target_pairs={{0,4},{4,0},{1,5},{5,1},{2,6},{6,2},{3,7},{7,3},{8,12},{12,8},{9,1... | collective-permute-start | bytes 3145736 | tf_op jit(solution)/shard_map/ppermute | solution.py:45
  17.4 28.5 %collective-permute-start = (bf16[2048,256]{1,0:T(8,128)(2,1)}, bf16[2048,256]{1,0:T(8,128)(2,1)}, u32[]{:S(2)}, u32[]{:S(2)}) collective-permute-start(bf16[2048,256]{1,0:T(8,128)(2,1)} %bitcast.128), channel_id=1, source_target_pairs={{0,4},{4,0},{1,5},{5,1},{2,6},{6,2},{3,7},{7,3},{8,12},{12,8},{9,1... | collective-permute-start | bytes 3145736 | tf_op jit(solution)/shard_map/ppermute | solution.py:45
  35.8 5.4 %all-to-all-start = ((bf16[64,2,5,512]{3,0,2,1:T(8,128)(2,1)}), bf16[64,2,5,512]{3,0,2,1:T(8,128)(2,1)S(1)}, u32[]{:S(2)}, u32[]{:S(2)}) async-start(bf16[64,2,5,512]{3,0,2,1:T(8,128)(2,1)} %copy.101), calls=%async_computation | async-start | bytes 1310720 | tf_op jit(solution)/shard_map/all_to_all | solution.py:89
  41.6 4.2 %copy-start.7 = (bf16[1,2048,256]{2,1,0:T(8,128)(2,1)S(1)}, bf16[1,2048,256]{2,1,0:T(8,128)(2,1)}, u32[]{:S(2)}) copy-start(bf16[1,2048,256]{2,1,0:T(8,128)(2,1)} %param.10) | copy-start | bytes 3145732
  44.6 1.5 copy-start.5
  45.8 1.3 copy-start.3
  67.5 106.9 %all-to-all-start.1 = ((bf16[64,2,14848]{2,1,0:T(2,128)(2,1)}), bf16[64,2,14848]{2,1,0:T(2,128)(2,1)}, u32[]{:S(2)}, u32[]{:S(2)}) async-start(bf16[64,2,14848]{2,1,0:T(2,128)(2,1)} %reshape.492), calls=%async_computation.1 | async-start | bytes 7602176 | tf_op jit(solution)/shard_map/all_to_all | solution.py:94
  78.6 222.7 %all-gather.3.cloned.1.call-start = ((), (), s32[]{:S(2)}) async-start(), calls=%async_computation.6 | async-start | bytes 3194880 | tf_op jit(solution)/shard_map/all_gather | solution.py:98
  197.9 1.8 copy-start.2
  203.6 34.3 %copy-start.6 = (bf16[1,2048,256]{2,1,0:T(8,128)(2,1)S(1)}, bf16[1,2048,256]{2,1,0:T(8,128)(2,1)}, u32[]{:S(2)}) copy-start(bf16[1,2048,256]{2,1,0:T(8,128)(2,1)} %param.9) | copy-start | bytes 3145732
  238.0 2.7 copy-start.4
  238.0 2.0 copy-start.8
  241.8 64.5 %all-to-all-start.3 = ((bf16[4,128,1,4,256]{4,1,3,2,0:T(8,128)(2,1)}), bf16[4,128,1,4,256]{4,1,3,2,0:T(8,128)(2,1)S(1)}, u32[]{:S(2)}, u32[]{:S(2)}) async-start(bf16[4,128,1,4,256]{4,1,3,2,0:T(8,128)(2,1)} %broadcast_in_dim.72), calls=%async_computation.3 | async-start | bytes 2097152 | tf_op jit(solution)/shard_map/all_to_all | solution.py:15
  303.4 7.5 %copy-start.9 = (bf16[1,1024,512]{2,1,0:T(8,128)(2,1)S(1)}, bf16[1,1024,512]{2,1,0:T(8,128)(2,1)}, u32[]{:S(2)}) copy-start(bf16[1,1024,512]{2,1,0:T(8,128)(2,1)} %param.11) | copy-start | bytes 3145732
  307.0 9.5 %all-to-all-start.4 = ((bf16[4,128,1,256]{3,1,2,0:T(8,128)(2,1)}), bf16[4,128,1,256]{3,1,2,0:T(8,128)(2,1)S(1)}, u32[]{:S(2)}, u32[]{:S(2)}) async-start(bf16[4,128,1,256]{3,1,2,0:T(8,128)(2,1)} %broadcast_in_dim.73), calls=%async_computation.4 | async-start | bytes 524288 | tf_op jit(solution)/shard_map/all_to_all | solution.py:15
  312.4 4.3 %copy-start.10 = (bf16[128,4,512]{2,0,1:T(8,128)(2,1)S(1)}, bf16[128,4,512]{2,0,1:T(8,128)(2,1)}, u32[]{:S(2)}) copy-start(bf16[128,4,512]{2,0,1:T(8,128)(2,1)} %fusion) | copy-start | bytes 1572868
  312.8 20.8 %copy-start.11 = (s32[64,8]{0,1:T(8,128)S(1)}, s32[64,8]{0,1:T(8,128)}, u32[]{:S(2)}) copy-start(s32[64,8]{0,1:T(8,128)} %param.7) | copy-start | bytes 6148
  312.8 21.0 %copy-start.12 = (f32[64,8]{0,1:T(8,128)S(1)}, f32[64,8]{0,1:T(8,128)}, u32[]{:S(2)}) copy-start(f32[64,8]{0,1:T(8,128)} %param.8) | copy-start | bytes 6148
  318.2 45.8 %all-to-all-start.5 = ((bf16[128,5,512]{2,1,0:T(8,128)(2,1)}), bf16[128,5,512]{2,1,0:T(8,128)(2,1)S(1)}, u32[]{:S(2)}, u32[]{:S(2)}) async-start(bf16[128,5,512]{2,1,0:T(8,128)(2,1)} %copy.108), calls=%async_computation.5 | async-start | bytes 2097152 | tf_op jit(solution)/shard_map/all_to_all | solution.py:144
  333.9 33.5 %copy-start.1 = (bf16[64,512]{1,0:T(8,128)(2,1)S(1)}, bf16[64,512]{1,0:T(8,128)(2,1)}, u32[]{:S(2)}) copy-start(bf16[64,512]{1,0:T(8,128)(2,1)} %param.6) | copy-start | bytes 196612
Sparse Core Ops, SparseCore 0:
  201.3 99.9 all-gather.2

commit v10 on v9

--- a/solution.py
+++ b/solution.py
@@ -87,13 +87,14 @@
     outgoing = jnp.take(tokens, source_row, axis=0, mode="fill", fill_value=0)
     paired = outgoing.reshape(pair_count, HOT, -1, slice_width)
     paired = lax.all_to_all(paired, "c", split_axis=1, concat_axis=1, tiled=True)
-    piece_size = blocks.shape[1] * blocks.shape[2]
+    lane = blocks.shape[2]
+    piece_rows = blocks.shape[1]
     merged = jnp.concatenate(
-        [blocks.reshape(pair_count, -1), paired.reshape(pair_count, -1)], axis=1
+        [blocks, paired.reshape(pair_count, -1, lane)], axis=1
     )
     merged = lax.all_to_all(merged, "eph", split_axis=0, concat_axis=0, tiled=True)
-    pieces = merged[:, :piece_size].reshape(blocks.shape)
-    arrived = merged[:, piece_size:].reshape(ep_count, -1, slice_width)
+    pieces = merged[:, :piece_rows]
+    arrived = merged[:, piece_rows:].reshape(ep_count, -1, slice_width)
     piece = lax.dynamic_index_in_dim(pieces, hot_ids[parity] // HOT, axis=0, keepdims=False)
     spread_back = lax.all_gather(piece, "eph", axis=0, tiled=True)
     model_rows = contrib[0].shape[0]

time: 376 us -> 335 us (0.89)
  local copies, waits for them, and re-layouts: 64.8 us -> 28 us
  other arithmetic: 18 us -> 11 us
  waiting for transfers between devices: 183 us -> 187 us
    unnamed x33 -> x21, local copies, waits for them, and re-layouts: 35 us -> 2.24 us
    all_to_all x2 -> x0, other arithmetic: 10.5 us -> none  [local(): lax.all_to_all(merged, 'eph', split_axis=0, concat_axis=0, tiled=True)]
    all_to_all x1, waiting for transfers between devices: 93 us -> 99.5 us  [local(): lax.all_to_all(merged, 'eph', split_axis=0, concat_axis=0, tiled=True)]
  transfers between devices with their start and end apart: 9 -> 9, of which waited for: 4 -> 4; matrix products, arithmetic and copies ran while one was open for 9% -> 10% of each run, Pallas kernels for 0% -> 0%
where the time goes in v10:
time: 335 us; the launch traced here: 334 us
  waiting for transfers between devices  187 us (56%)
  starting transfers between devices  50.6 us (15%)
  blocking collectives  33.5 us (10%)
  local copies, waits for them, and re-layouts  28 us (8%)
  between operations  17.8 us (5%)
  other arithmetic  11 us (3%)
  matrix products  6.01 us (2%)
    all_to_all x1, waiting for transfers between devices, local(): lax.all_to_all(merged, 'eph', split_axis=0, concat_axis=0, tiled=True)  99.5 us
    all_gather x1, waiting for transfers between devices, local(): spread_back = lax.all_gather(piece, 'eph', axis=0, tiled=True)  53.3 us
    all_to_all x1, blocking collectives, gather_dp(): lax.all_to_all(stacked, 'dp', split_axis=0, concat_axis=0, tiled=True)  33.5 us
    all_to_all x1, waiting for transfers between devices, local(): lax.all_to_all(results, EP, split_axis=0, concat_axis=0, tiled=True)  30.2 us
    all_to_all x1, starting transfers between devices, local(): lax.all_to_all(results, EP, split_axis=0, concat_axis=0, tiled=True)  14.9 us
    ppermute x3, starting transfers between devices, local(): swapped = tuple((lax.ppermute(w, 'c', [(0, 1), (1, 0)]) for w in own))  13.2 us
    all_to_all x1, starting transfers between devices, local(): lax.all_to_all(merged, 'eph', split_axis=0, concat_axis=0, tiled=True)  11.2 us
    all_to_all x2, starting transfers between devices, gather_dp(): lax.all_to_all(stacked, 'dp', split_axis=0, concat_axis=0, tiled=True)  7.66 us
  transfers between devices with their start and end apart: 9, of which 4 were waited for; matrix products, arithmetic and copies ran while one was open for 10% of the time, Pallas kernels for 0%

profile of v10, /device:TPU:1, one launch (start us, length us, event | category | flops | bytes accessed | tf_op | source)
XLA Modules:
  0.0 333.6 jit_solution(1462416489869118564)
XLA Ops:
  6.5 8.9 %collective-permute-start.2 = (bf16[1024,512]{1,0:T(8,128)(2,1)}, bf16[1024,512]{1,0:T(8,128)(2,1)}, u32[]{:S(2)}, u32[]{:S(2)}) collective-permute-start(bf16[1024,512]{1,0:T(8,128)(2,1)} %bitcast.125), channel_id=1, source_target_pairs={{0,4},{4,0},{1,5},{5,1},{2,6},{6,2},{3,7},{7,3},{8,12},{12,8},{9,1... | collective-permute-start | bytes 3145736 | tf_op jit(solution)/shard_map/ppermute | solution.py:45
  15.5 1.9 collective-permute-start.1
  17.4 2.4 collective-permute-start
  22.5 2.5 top_k.11
  25.2 2.4 scatter_custom_fusion
  27.9 2.4 scatter_custom_fusion.1
  31.3 2.8 gather_fusion
  34.6 1.3 copy.80
  35.8 3.5 %all-to-all-start = ((bf16[64,2,5,512]{3,0,2,1:T(8,128)(2,1)}), bf16[64,2,5,512]{3,0,2,1:T(8,128)(2,1)S(1)}, u32[]{:S(2)}, u32[]{:S(2)}) async-start(bf16[64,2,5,512]{3,0,2,1:T(8,128)(2,1)} %copy.80), calls=%async_computation | async-start | bytes 1310720 | tf_op jit(solution)/shard_map/all_to_all | solution.py:89
  42.0 1.4 select_select_fusion
  43.8 1.4 select_select_fusion.1
  46.0 2.2 pad_maximum_fusion
  48.2 11.2 %all-to-all-start.1 = ((bf16[64,116,256]{2,1,0:T(8,128)(2,1)}), bf16[64,116,256]{2,1,0:T(8,128)(2,1)}, u32[]{:S(2)}, u32[]{:S(2)}) async-start(bf16[64,116,256]{2,1,0:T(8,128)(2,1)} %pad_maximum_fusion), calls=%async_computation.1 | async-start | bytes 7864320 | tf_op jit(solution)/shard_map/all_to_all | solution.py:95
  62.0 99.5 %all-to-all-done.1 = bf16[64,116,256]{2,1,0:T(8,128)(2,1)} async-done(((bf16[64,116,256]{2,1,0:T(8,128)(2,1)}), bf16[64,116,256]{2,1,0:T(8,128)(2,1)}, u32[]{:S(2)}, u32[]{:S(2)}) %all-to-all-start.1) | async-done | bytes 3801120 | tf_op jit(solution)/shard_map/all_to_all | solution.py:95
  161.5 2.1 slice.48
  164.3 1.2 slice.46
  166.4 33.5 %all_to_all.30 = bf16[4,128,5,512]{3,1,2,0:T(8,128)(2,1)S(1)} all-to-all(bf16[4,128,5,512]{3,1,2,0:T(8,128)(2,1)S(1)} %broadcast_in_dim.70), channel_id=1, replica_groups=mesh['eph'=64,'c'=2,'dp'=4] {'dp'}, dimensions={0} | all-to-all | bytes 5242880 | tf_op jit(solution)/shard_map/all_to_all | solution.py:15
  200.6 1.3 copy-done.4
  202.6 1.1 broadcast_in_dim.72
  203.7 3.7 %all-to-all-start.3 = ((bf16[4,128,1,4,256]{4,1,3,2,0:T(8,128)(2,1)}), bf16[4,128,1,4,256]{4,1,3,2,0:T(8,128)(2,1)S(1)}, u32[]{:S(2)}, u32[]{:S(2)}) async-start(bf16[4,128,1,4,256]{4,1,3,2,0:T(8,128)(2,1)} %broadcast_in_dim.72), calls=%async_computation.3 | async-start | bytes 2097152 | tf_op jit(solution)/shard_map/all_to_all | solution.py:15
  207.4 53.3 %all-gather.3.cloned.1.call-done = bf16[1,6144,256]{2,1,0:T(8,128)(2,1)} async-done(((bf16[1,96,256]{2,1,0:T(8,128)(2,1)}), bf16[1,6144,256]{2,1,0:T(8,128)(2,1)}) %all-gather.3.cloned.1.call-update) | async-done | bytes 3145744 | tf_op jit(solution)/shard_map/all_gather | solution.py:99
  260.7 2.1 fusion.40
  262.8 1.4 convolution_bitcast_fusion.5
  264.3 1.4 fusion.7
  266.3 4.0 %all-to-all-start.4 = ((bf16[4,128,1,256]{3,1,2,0:T(8,128)(2,1)}), bf16[4,128,1,256]{3,1,2,0:T(8,128)(2,1)S(1)}, u32[]{:S(2)}, u32[]{:S(2)}) async-start(bf16[4,128,1,256]{3,1,2,0:T(8,128)(2,1)} %broadcast_in_dim.73), calls=%async_computation.4 | async-start | bytes 524288 | tf_op jit(solution)/shard_map/all_to_all | solution.py:15
  270.3 1.5 fusion
  272.2 3.6 %all-to-all-done.4 = bf16[4,128,1,256]{3,1,2,0:T(8,128)(2,1)S(1)} async-done(((bf16[4,128,1,256]{3,1,2,0:T(8,128)(2,1)}), bf16[4,128,1,256]{3,1,2,0:T(8,128)(2,1)S(1)}, u32[]{:S(2)}, u32[]{:S(2)}) %all-to-all-start.4) | async-done | bytes 262176 | tf_op jit(solution)/shard_map/all_to_all | solution.py:15
  276.2 1.4 copy.86
  277.6 14.9 %all-to-all-start.5 = ((bf16[128,5,512]{2,1,0:T(8,128)(2,1)}), bf16[128,5,512]{2,1,0:T(8,128)(2,1)S(1)}, u32[]{:S(2)}, u32[]{:S(2)}) async-start(bf16[128,5,512]{2,1,0:T(8,128)(2,1)} %copy.86), calls=%async_computation.5 | async-start | bytes 2097152 | tf_op jit(solution)/shard_map/all_to_all | solution.py:145
  293.3 30.2 %all-to-all-done.5 = bf16[128,5,512]{2,1,0:T(8,128)(2,1)S(1)} async-done(((bf16[128,5,512]{2,1,0:T(8,128)(2,1)}), bf16[128,5,512]{2,1,0:T(8,128)(2,1)S(1)}, u32[]{:S(2)}, u32[]{:S(2)}) %all-to-all-start.5) | async-done | bytes 655392 | tf_op jit(solution)/shard_map/all_to_all | solution.py:145
  323.7 2.0 gather_fusion.1
  325.7 1.1 multiply_reduce_fusion
  (89 shorter events, 12.3 us)
Async XLA Ops:
  6.5 24.7 %copy-start = (bf16[64,512]{1,0:T(8,128)(2,1)S(1)}, bf16[64,512]{1,0:T(8,128)(2,1)}, u32[]{:S(2)}) copy-start(bf16[64,512]{1,0:T(8,128)(2,1)} %param.6) | copy-start | bytes 196612
  6.5 35.4 %collective-permute-start.2 = (bf16[1024,512]{1,0:T(8,128)(2,1)}, bf16[1024,512]{1,0:T(8,128)(2,1)}, u32[]{:S(2)}, u32[]{:S(2)}) collective-permute-start(bf16[1024,512]{1,0:T(8,128)(2,1)} %bitcast.125), channel_id=1, source_target_pairs={{0,4},{4,0},{1,5},{5,1},{2,6},{6,2},{3,7},{7,3},{8,12},{12,8},{9,1... | collective-permute-start | bytes 3145736 | tf_op jit(solution)/shard_map/ppermute | solution.py:45
  15.5 28.3 %collective-permute-start.1 = (bf16[2048,256]{1,0:T(8,128)(2,1)}, bf16[2048,256]{1,0:T(8,128)(2,1)}, u32[]{:S(2)}, u32[]{:S(2)}) collective-permute-start(bf16[2048,256]{1,0:T(8,128)(2,1)} %bitcast.123), channel_id=1, source_target_pairs={{0,4},{4,0},{1,5},{5,1},{2,6},{6,2},{3,7},{7,3},{8,12},{12,8},{9,1... | collective-permute-start | bytes 3145736 | tf_op jit(solution)/shard_map/ppermute | solution.py:45
  17.4 27.8 %collective-permute-start = (bf16[2048,256]{1,0:T(8,128)(2,1)}, bf16[2048,256]{1,0:T(8,128)(2,1)}, u32[]{:S(2)}, u32[]{:S(2)}) collective-permute-start(bf16[2048,256]{1,0:T(8,128)(2,1)} %bitcast.121), channel_id=1, source_target_pairs={{0,4},{4,0},{1,5},{5,1},{2,6},{6,2},{3,7},{7,3},{8,12},{12,8},{9,1... | collective-permute-start | bytes 3145736 | tf_op jit(solution)/shard_map/ppermute | solution.py:45
  35.8 5.4 %all-to-all-start = ((bf16[64,2,5,512]{3,0,2,1:T(8,128)(2,1)}), bf16[64,2,5,512]{3,0,2,1:T(8,128)(2,1)S(1)}, u32[]{:S(2)}, u32[]{:S(2)}) async-start(bf16[64,2,5,512]{3,0,2,1:T(8,128)(2,1)} %copy.80), calls=%async_computation | async-start | bytes 1310720 | tf_op jit(solution)/shard_map/all_to_all | solution.py:89
  43.7 1.5 copy-start.2
  48.2 113.3 %all-to-all-start.1 = ((bf16[64,116,256]{2,1,0:T(8,128)(2,1)}), bf16[64,116,256]{2,1,0:T(8,128)(2,1)}, u32[]{:S(2)}, u32[]{:S(2)}) async-start(bf16[64,116,256]{2,1,0:T(8,128)(2,1)} %pad_maximum_fusion), calls=%async_computation.1 | async-start | bytes 7864320 | tf_op jit(solution)/shard_map/all_to_all | solution.py:95
  59.4 201.4 %all-gather.3.cloned.1.call-start = ((), (), s32[]{:S(2)}) async-start(), calls=%async_computation.6 | async-start | bytes 3194880 | tf_op jit(solution)/shard_map/all_gather | solution.py:99
  166.3 33.6 %copy-start.3 = (bf16[1,2048,256]{2,1,0:T(8,128)(2,1)S(1)}, bf16[1,2048,256]{2,1,0:T(8,128)(2,1)}, u32[]{:S(2)}) copy-start(bf16[1,2048,256]{2,1,0:T(8,128)(2,1)} %param.9) | copy-start | bytes 3145732
  199.9 2.7 copy-start.1
  199.9 2.0 copy-start.4
  203.7 61.9 %all-to-all-start.3 = ((bf16[4,128,1,4,256]{4,1,3,2,0:T(8,128)(2,1)}), bf16[4,128,1,4,256]{4,1,3,2,0:T(8,128)(2,1)S(1)}, u32[]{:S(2)}, u32[]{:S(2)}) async-start(bf16[4,128,1,4,256]{4,1,3,2,0:T(8,128)(2,1)} %broadcast_in_dim.72), calls=%async_computation.3 | async-start | bytes 2097152 | tf_op jit(solution)/shard_map/all_to_all | solution.py:15
  262.8 7.5 %copy-start.5 = (bf16[1,1024,512]{2,1,0:T(8,128)(2,1)S(1)}, bf16[1,1024,512]{2,1,0:T(8,128)(2,1)}, u32[]{:S(2)}) copy-start(bf16[1,1024,512]{2,1,0:T(8,128)(2,1)} %param.11) | copy-start | bytes 3145732
  266.3 9.5 %all-to-all-start.4 = ((bf16[4,128,1,256]{3,1,2,0:T(8,128)(2,1)}), bf16[4,128,1,256]{3,1,2,0:T(8,128)(2,1)S(1)}, u32[]{:S(2)}, u32[]{:S(2)}) async-start(bf16[4,128,1,256]{3,1,2,0:T(8,128)(2,1)} %broadcast_in_dim.73), calls=%async_computation.4 | async-start | bytes 524288 | tf_op jit(solution)/shard_map/all_to_all | solution.py:15
  271.8 4.3 %copy-start.6 = (bf16[128,4,512]{2,0,1:T(8,128)(2,1)S(1)}, bf16[128,4,512]{2,0,1:T(8,128)(2,1)}, u32[]{:S(2)}) copy-start(bf16[128,4,512]{2,0,1:T(8,128)(2,1)} %fusion) | copy-start | bytes 1572868
  272.2 20.6 %copy-start.8 = (f32[64,8]{0,1:T(8,128)S(1)}, f32[64,8]{0,1:T(8,128)}, u32[]{:S(2)}) copy-start(f32[64,8]{0,1:T(8,128)} %param.8) | copy-start | bytes 6148
  272.2 20.9 %copy-start.7 = (s32[64,8]{0,1:T(8,128)S(1)}, s32[64,8]{0,1:T(8,128)}, u32[]{:S(2)}) copy-start(s32[64,8]{0,1:T(8,128)} %param.7) | copy-start | bytes 6148
  277.6 45.8 %all-to-all-start.5 = ((bf16[128,5,512]{2,1,0:T(8,128)(2,1)}), bf16[128,5,512]{2,1,0:T(8,128)(2,1)S(1)}, u32[]{:S(2)}, u32[]{:S(2)}) async-start(bf16[128,5,512]{2,1,0:T(8,128)(2,1)} %copy.86), calls=%async_computation.5 | async-start | bytes 2097152 | tf_op jit(solution)/shard_map/all_to_all | solution.py:145
Sparse Core Ops, SparseCore 0:
  164.4 96.2 all-gather.2

commit v11 on v7

--- a/solution.py
+++ b/solution.py
@@ -109,12 +109,8 @@
         "nsecd,endf->secf", primary_rows, up_split, preferred_element_type=jnp.float32
     )
     hidden_primary = silu_product(gate_primary, up_primary)
-    part_primary = gather_dp(hidden_primary, dp_count)
     feature_local = down_weight.shape[2]
     down_split = down_weight.reshape(exp_dev, dp_count, -1, feature_local)
-    out_primary = jnp.einsum(
-        "nsecf,enfd->secd", part_primary, down_split, preferred_element_type=jnp.float32
-    ).astype(jnp.bfloat16)
 
     spare_gate = spare_gate.reshape(dp_count, slice_width, -1)
     spare_up = spare_up.reshape(dp_count, slice_width, -1)
@@ -125,7 +121,18 @@
         "nsrd,ndf->srf", spare_rows, spare_up, preferred_element_type=jnp.float32
     )
     hidden_spare = silu_product(gate_spare, up_spare)
-    part_spare = gather_dp(hidden_spare, dp_count)
+
+    hidden_all = jnp.concatenate(
+        [hidden_primary.reshape(ep_count, primary_slots, -1), hidden_spare], axis=1
+    )
+    part_all = gather_dp(hidden_all, dp_count)
+    part_primary = part_all[:, :, :primary_slots].reshape(
+        dp_count, ep_count, exp_dev, capacity, -1
+    )
+    part_spare = part_all[:, :, primary_slots:]
+    out_primary = jnp.einsum(
+        "nsecf,enfd->secd", part_primary, down_split, preferred_element_type=jnp.float32
+    ).astype(jnp.bfloat16)
     spare_split = spare_down.reshape(dp_count, -1, feature_local)
     out_spare = jnp.einsum(
         "nsrf,nfd->srd", part_spare, spare_split, preferred_element_type=jnp.float32

time: 309 us -> 314 us (1.016)
  waiting for transfers between devices: 117 us -> 123 us
    all_gather x1, waiting for transfers between devices: 0.05 us -> 4.66 us  [local(): spread_back = lax.all_gather(piece, 'eph', axis=0, tiled=True)]
    all_to_all x1, starting transfers between devices: 10.3 us -> 14.7 us  [local(): lax.all_to_all(results, EP, split_axis=0, concat_axis=0, tiled=True)]
    all_to_all x2 -> x1, starting transfers between devices: 7.1 us -> 3.95 us  [gather_dp(): lax.all_to_all(stacked, 'dp', split_axis=0, concat_axis=0, tiled=True)]
    all_to_all x2 -> x1, waiting for transfers between devices: 11.7 us -> 12.6 us  [gather_dp(): lax.all_to_all(stacked, 'dp', split_axis=0, concat_axis=0, tiled=True)]
  transfers between devices with their start and end apart: 8 -> 7, of which waited for: 4 -> 4; matrix products, arithmetic and copies ran while one was open for 9% -> 6% of each run, Pallas kernels for 0% -> 0%
where the time goes in v11:
time: 314 us; the launch traced here: 313 us
  waiting for transfers between devices  123 us (39%)
  blocking collectives  89.9 us (29%)
  starting transfers between devices  44.5 us (14%)
  local copies, waits for them, and re-layouts  21.5 us (7%)
  between operations  17.8 us (6%)
  other arithmetic  9.27 us (3%)
  matrix products  6.35 us (2%)
    all_to_all x1, waiting for transfers between devices, local(): lax.all_to_all(blocks, 'eph', split_axis=0, concat_axis=0, tiled=True)  75.9 us
    all_to_all x1, blocking collectives, local(): lax.all_to_all(outgoing, EP, split_axis=0, concat_axis=0, tiled=True)  55 us
    all_to_all x1, blocking collectives, gather_dp(): lax.all_to_all(stacked, 'dp', split_axis=0, concat_axis=0, tiled=True)  34.9 us
    all_to_all x1, waiting for transfers between devices, local(): lax.all_to_all(results, EP, split_axis=0, concat_axis=0, tiled=True)  30.2 us
    all_to_all x1, starting transfers between devices, local(): lax.all_to_all(results, EP, split_axis=0, concat_axis=0, tiled=True)  14.7 us
    ppermute x3, starting transfers between devices, local(): swapped = tuple((lax.ppermute(w, 'c', [(0, 1), (1, 0)]) for w in own))  13.2 us
    all_to_all x1, waiting for transfers between devices, gather_dp(): lax.all_to_all(stacked, 'dp', split_axis=0, concat_axis=0, tiled=True)  12.6 us
    all_to_all x1, starting transfers between devices, local(): lax.all_to_all(blocks, 'eph', split_axis=0, concat_axis=0, tiled=True)  12.6 us
  transfers between devices with their start and end apart: 7, of which 4 were waited for; matrix products, arithmetic and copies ran while one was open for 6% of the time, Pallas kernels for 0%

profile of v11, /device:TPU:1, one launch (start us, length us, event | category | flops | bytes accessed | tf_op | source)
XLA Modules:
  0.0 312.7 jit_solution(6917270499855192649)
XLA Ops:
  6.5 8.9 %collective-permute-start.1 = (bf16[2048,256]{1,0:T(8,128)(2,1)}, bf16[2048,256]{1,0:T(8,128)(2,1)}, u32[]{:S(2)}, u32[]{:S(2)}) collective-permute-start(bf16[2048,256]{1,0:T(8,128)(2,1)} %bitcast.129), channel_id=1, source_target_pairs={{0,4},{4,0},{1,5},{5,1},{2,6},{6,2},{3,7},{7,3},{8,12},{12,8},{9,1... | collective-permute-start | bytes 3145736 | tf_op jit(solution)/shard_map/ppermute | solution.py:45
  15.5 1.9 collective-permute-start
  17.4 2.4 collective-permute-start.2
  19.8 0.8 copy.57
  21.5 2.5 top_k.11
  25.9 1.3 select_select_fusion
  27.7 1.4 select_select_fusion.1
  29.2 1.8 pad_maximum_fusion
  31.0 12.6 %all-to-all-start.2 = ((bf16[64,96,256]{2,1,0:T(8,128)(2,1)}), bf16[64,96,256]{2,1,0:T(8,128)(2,1)S(1)}, u32[]{:S(2)}, u32[]{:S(2)}) async-start(bf16[64,96,256]{2,1,0:T(8,128)(2,1)} %bitcast.32), calls=%async_computation.2 | async-start | bytes 6291456 | tf_op jit(solution)/shard_map/all_to_all | solution.py:59
  46.2 75.9 %all-to-all-done.2 = bf16[64,96,256]{2,1,0:T(8,128)(2,1)S(1)} async-done(((bf16[64,96,256]{2,1,0:T(8,128)(2,1)}), bf16[64,96,256]{2,1,0:T(8,128)(2,1)S(1)}, u32[]{:S(2)}, u32[]{:S(2)}) %all-to-all-start.2) | async-done | bytes 3145760 | tf_op jit(solution)/shard_map/all_to_all | solution.py:59
  122.2 0.6 constant_dynamic-slice_fusion
  123.4 2.4 scatter_custom_fusion
  126.0 2.4 scatter_custom_fusion.1
  129.2 2.8 gather_fusion
  132.4 55.0 %all_to_all.25 = bf16[128,5,512]{2,1,0:T(8,128)(2,1)S(1)} all-to-all(bf16[128,5,512]{2,1,0:T(8,128)(2,1)S(1)} %broadcast_select_fusion), channel_id=1, replica_groups=mesh['eph'=64,'c'=2,'dp'=4] {'eph','c'}, dimensions={0} | all-to-all | bytes 1310720 | tf_op jit(solution)/shard_map/all_to_all | solution.py:96
  188.0 34.9 %all_to_all.26 = bf16[4,128,5,512]{3,1,2,0:T(8,128)(2,1)S(1)} all-to-all(bf16[4,128,5,512]{3,1,2,0:T(8,128)(2,1)S(1)} %broadcast_in_dim.60), channel_id=1, replica_groups=mesh['eph'=64,'c'=2,'dp'=4] {'dp'}, dimensions={0} | all-to-all | bytes 5242880 | tf_op jit(solution)/shard_map/all_to_all | solution.py:15
  222.9 0.7 convolution_bitcast_fusion.2
  223.6 0.8 copy-done.1
  224.9 0.7 fusion.3
  225.6 4.7 %all-gather.3.cloned.1.call-done = bf16[1,6144,256]{2,1,0:T(8,128)(2,1)} async-done(((bf16[1,96,256]{2,1,0:T(8,128)(2,1)}), bf16[1,6144,256]{2,1,0:T(8,128)(2,1)}) %all-gather.3.cloned.1.call-update) | async-done | bytes 3145744 | tf_op jit(solution)/shard_map/all_gather | solution.py:61
  230.2 2.1 fusion.38
  232.3 1.4 convolution_bitcast_fusion.5
  233.7 1.4 fusion.8
  235.1 1.2 broadcast_in_dim.61
  236.3 4.0 %all-to-all-start.3 = ((bf16[4,128,5,256]{3,1,2,0:T(8,128)(2,1)}), bf16[4,128,5,256]{3,1,2,0:T(8,128)(2,1)S(1)}, u32[]{:S(2)}, u32[]{:S(2)}) async-start(bf16[4,128,5,256]{3,1,2,0:T(8,128)(2,1)} %broadcast_in_dim.61), calls=%async_computation.3 | async-start | bytes 2621440 | tf_op jit(solution)/shard_map/all_to_all | solution.py:15
  240.6 12.6 %all-to-all-done.3 = bf16[4,128,5,256]{3,1,2,0:T(8,128)(2,1)S(1)} async-done(((bf16[4,128,5,256]{3,1,2,0:T(8,128)(2,1)}), bf16[4,128,5,256]{3,1,2,0:T(8,128)(2,1)S(1)}, u32[]{:S(2)}, u32[]{:S(2)}) %all-to-all-start.3) | async-done | bytes 1310752 | tf_op jit(solution)/shard_map/all_to_all | solution.py:15
  253.2 1.9 fusion
  255.6 1.4 copy.80
  256.9 14.7 %all-to-all-start.4 = ((bf16[128,5,512]{2,1,0:T(8,128)(2,1)}), bf16[128,5,512]{2,1,0:T(8,128)(2,1)S(1)}, u32[]{:S(2)}, u32[]{:S(2)}) async-start(bf16[128,5,512]{2,1,0:T(8,128)(2,1)} %copy.80), calls=%async_computation.4 | async-start | bytes 2097152 | tf_op jit(solution)/shard_map/all_to_all | solution.py:145
  272.4 30.2 %all-to-all-done.4 = bf16[128,5,512]{2,1,0:T(8,128)(2,1)S(1)} async-done(((bf16[128,5,512]{2,1,0:T(8,128)(2,1)}), bf16[128,5,512]{2,1,0:T(8,128)(2,1)S(1)}, u32[]{:S(2)}, u32[]{:S(2)}) %all-to-all-start.4) | async-done | bytes 655392 | tf_op jit(solution)/shard_map/all_to_all | solution.py:145
  302.8 2.0 gather_fusion.1
  304.8 1.1 multiply_reduce_fusion
  (73 shorter events, 6.5 us)
Async XLA Ops:
  6.5 122.6 %copy-start = (bf16[64,512]{1,0:T(8,128)(2,1)S(1)}, bf16[64,512]{1,0:T(8,128)(2,1)}, u32[]{:S(2)}) copy-start(bf16[64,512]{1,0:T(8,128)(2,1)} %param.6) | copy-start | bytes 196612
  6.5 21.1 %collective-permute-start.1 = (bf16[2048,256]{1,0:T(8,128)(2,1)}, bf16[2048,256]{1,0:T(8,128)(2,1)}, u32[]{:S(2)}, u32[]{:S(2)}) collective-permute-start(bf16[2048,256]{1,0:T(8,128)(2,1)} %bitcast.129), channel_id=1, source_target_pairs={{0,4},{4,0},{1,5},{5,1},{2,6},{6,2},{3,7},{7,3},{8,12},{12,8},{9,1... | collective-permute-start | bytes 3145736 | tf_op jit(solution)/shard_map/ppermute | solution.py:45
  15.5 13.6 %collective-permute-start = (bf16[2048,256]{1,0:T(8,128)(2,1)}, bf16[2048,256]{1,0:T(8,128)(2,1)}, u32[]{:S(2)}, u32[]{:S(2)}) collective-permute-start(bf16[2048,256]{1,0:T(8,128)(2,1)} %bitcast.127), channel_id=1, source_target_pairs={{0,4},{4,0},{1,5},{5,1},{2,6},{6,2},{3,7},{7,3},{8,12},{12,8},{9,1... | collective-permute-start | bytes 3145736 | tf_op jit(solution)/shard_map/ppermute | solution.py:45
  17.4 8.5 %collective-permute-start.2 = (bf16[1024,512]{1,0:T(8,128)(2,1)}, bf16[1024,512]{1,0:T(8,128)(2,1)S(1)}, u32[]{:S(2)}, u32[]{:S(2)}) collective-permute-start(bf16[1024,512]{1,0:T(8,128)(2,1)} %bitcast.131), channel_id=1, source_target_pairs={{0,4},{4,0},{1,5},{5,1},{2,6},{6,2},{3,7},{7,3},{8,12},{12,8},{9,1... | collective-permute-start | bytes 3145736 | tf_op jit(solution)/shard_map/ppermute | solution.py:45
  27.2 1.8 copy-start.2
  31.0 91.8 %copy-start.5 = (s32[64,8]{0,1:T(8,128)S(1)}, s32[64,8]{0,1:T(8,128)}, u32[]{:S(2)}) copy-start(s32[64,8]{0,1:T(8,128)} %param.7) | copy-start | bytes 6148
  31.0 91.2 %all-to-all-start.2 = ((bf16[64,96,256]{2,1,0:T(8,128)(2,1)}), bf16[64,96,256]{2,1,0:T(8,128)(2,1)S(1)}, u32[]{:S(2)}, u32[]{:S(2)}) async-start(bf16[64,96,256]{2,1,0:T(8,128)(2,1)} %bitcast.32), calls=%async_computation.2 | async-start | bytes 6291456 | tf_op jit(solution)/shard_map/all_to_all | solution.py:59
  43.6 186.7 %all-gather.3.cloned.1.call-start = ((), (), s32[]{:S(2)}) async-start(), calls=%async_computation.5 | async-start | bytes 3194880 | tf_op jit(solution)/shard_map/all_gather | solution.py:61
  188.0 34.9 %copy-start.3 = (bf16[1,2048,256]{2,1,0:T(8,128)(2,1)S(1)}, bf16[1,2048,256]{2,1,0:T(8,128)(2,1)}, u32[]{:S(2)}) copy-start(bf16[1,2048,256]{2,1,0:T(8,128)(2,1)} %param.9) | copy-start | bytes 3145732
  222.9 1.5 copy-start.1
  222.9 2.0 copy-start.4
  236.3 17.0 %all-to-all-start.3 = ((bf16[4,128,5,256]{3,1,2,0:T(8,128)(2,1)}), bf16[4,128,5,256]{3,1,2,0:T(8,128)(2,1)S(1)}, u32[]{:S(2)}, u32[]{:S(2)}) async-start(bf16[4,128,5,256]{3,1,2,0:T(8,128)(2,1)} %broadcast_in_dim.61), calls=%async_computation.3 | async-start | bytes 2621440 | tf_op jit(solution)/shard_map/all_to_all | solution.py:15
  255.5 16.8 %copy-start.6 = (f32[64,8]{0,1:T(8,128)S(1)}, f32[64,8]{0,1:T(8,128)}, u32[]{:S(2)}) copy-start(f32[64,8]{0,1:T(8,128)} %param.8) | copy-start | bytes 6148
  256.9 45.6 %all-to-all-start.4 = ((bf16[128,5,512]{2,1,0:T(8,128)(2,1)}), bf16[128,5,512]{2,1,0:T(8,128)(2,1)S(1)}, u32[]{:S(2)}, u32[]{:S(2)}) async-start(bf16[128,5,512]{2,1,0:T(8,128)(2,1)} %copy.80), calls=%async_computation.4 | async-start | bytes 2097152 | tf_op jit(solution)/shard_map/all_to_all | solution.py:145
Sparse Core Ops, SparseCore 0:
  122.9 107.2 all-gather.2

commit v12 on v7

--- a/solution.py
+++ b/solution.py
@@ -41,29 +41,26 @@
     expert_loads = jnp.sum(matches, axis=0)
     _, hot_ids = lax.top_k(expert_loads * expert_count + (expert_count - 1 - expert_range), HOT)
 
-    own = (gate_weight[0], up_weight[0], down_weight[0])
-    swapped = tuple(lax.ppermute(w, "c", [(0, 1), (1, 0)]) for w in own)
+    lane = gate_weight.shape[2]
+    own = jnp.concatenate(
+        [gate_weight[0], up_weight[0], down_weight[0].reshape(-1, lane)], axis=0
+    )
+    swapped = lax.ppermute(own, "c", [(0, 1), (1, 0)])
     mine = hot_ids[parity]
     my_expert = ep_index
     sibling_expert = ep_index ^ 1
     take_own = mine == my_expert
     take_sib = mine == sibling_expert
-    contrib = tuple(
-        jnp.where(take_own, a, jnp.where(take_sib, b, jnp.zeros_like(a)))
-        for a, b in zip(own, swapped)
-    )
-    packed = jnp.concatenate(
-        [contrib[0], contrib[1], contrib[2].reshape(-1, contrib[0].shape[1])], axis=0
-    )
+    packed = jnp.where(take_own, own, jnp.where(take_sib, swapped, jnp.zeros_like(own)))
     blocks = packed.reshape(pair_count, -1, packed.shape[1])
     pieces = lax.all_to_all(blocks, "eph", split_axis=0, concat_axis=0, tiled=True)
     piece = lax.dynamic_index_in_dim(pieces, hot_ids[parity] // HOT, axis=0, keepdims=False)
     spread_back = lax.all_gather(piece, "eph", axis=0, tiled=True)
-    model_rows = contrib[0].shape[0]
+    model_rows = gate_weight.shape[1]
     spare_gate = spread_back[:model_rows]
     spare_up = spread_back[model_rows : 2 * model_rows]
-    spare_down = spread_back[2 * model_rows :].reshape(contrib[2].shape)
-    tokens, contrib = lax.optimization_barrier((tokens, contrib))
+    spare_down = spread_back[2 * model_rows :].reshape(down_weight.shape[1:])
+    tokens, packed = lax.optimization_barrier((tokens, packed))
 
     earlier = jnp.cumsum(matches, axis=0) - matches
     order_rank = jnp.sum(earlier * matches, axis=1)

time: 309 us -> 306 us (level)
  starting transfers between devices: 43.2 us -> 38.7 us
    ppermute x3 -> x1, starting transfers between devices: 13.2 us -> 8.78 us  [local(): swapped = lax.ppermute(own, 'c', [(0, 1), (1, 0)])]
  transfers between devices with their start and end apart: 8 -> 6, of which waited for: 4 -> 5; matrix products, arithmetic and copies ran while one was open for 9% -> 9% of each run, Pallas kernels for 0% -> 0%
where the time goes in v12:
time: 306 us
  waiting for transfers between devices  117 us (38%)
  blocking collectives  90.8 us (30%)
  starting transfers between devices  38.7 us (13%)
  local copies, waits for them, and re-layouts  23 us (8%)
  between operations  17.7 us (6%)
  other arithmetic  11.3 us (4%)
  matrix products  7.24 us (2%)
    all_to_all x1, waiting for transfers between devices, local(): lax.all_to_all(blocks, 'eph', split_axis=0, concat_axis=0, tiled=True)  76 us
    all_to_all x1, blocking collectives, local(): lax.all_to_all(outgoing, EP, split_axis=0, concat_axis=0, tiled=True)  55.9 us
    all_to_all x1, blocking collectives, gather_dp(): lax.all_to_all(stacked, 'dp', split_axis=0, concat_axis=0, tiled=True)  34.9 us
    all_to_all x1, waiting for transfers between devices, local(): lax.all_to_all(results, EP, split_axis=0, concat_axis=0, tiled=True)  30.2 us
    all_to_all x1, starting transfers between devices, local(): lax.all_to_all(blocks, 'eph', split_axis=0, concat_axis=0, tiled=True)  11.2 us
    all_to_all x1, starting transfers between devices, local(): lax.all_to_all(results, EP, split_axis=0, concat_axis=0, tiled=True)  10.9 us
    all_to_all x2, waiting for transfers between devices, gather_dp(): lax.all_to_all(stacked, 'dp', split_axis=0, concat_axis=0, tiled=True)  10.5 us
    ppermute x1, starting transfers between devices, local(): swapped = lax.ppermute(own, 'c', [(0, 1), (1, 0)])  8.78 us
  transfers between devices with their start and end apart: 6, of which 5 were waited for; matrix products, arithmetic and copies ran while one was open for 9% of the time, Pallas kernels for 0%

profile of v12, /device:TPU:1, one launch (start us, length us, event | category | flops | bytes accessed | tf_op | source)
XLA Modules:
  0.0 305.6 jit_solution(15513212131598283962)
XLA Ops:
  6.5 1.4 reshape_squeeze.3
  8.0 3.2 %pad_maximum_fusion = bf16[6144,256]{1,0:T(8,128)(2,1)} fusion(bf16[2048,256]{1,0:T(8,128)(2,1)S(1)} %reshape_squeeze.3, bf16[2048,256]{1,0:T(8,128)(2,1)} %bitcast.118, bf16[2048,256]{1,0:T(8,128)(2,1)} %bitcast.115), kind=kLoop, calls=%fused_computation.4 | loop fusion | flops 9437184 | bytes 6291456 | tf_op jit(solution)/shard_map/concatenate | solution.py:45
  11.2 8.8 %collective-permute-start = (bf16[6144,256]{1,0:T(8,128)(2,1)}, bf16[6144,256]{1,0:T(8,128)(2,1)}, u32[]{:S(2)}, u32[]{:S(2)}) collective-permute-start(bf16[6144,256]{1,0:T(8,128)(2,1)} %pad_maximum_fusion), channel_id=1, source_target_pairs={{0,4},{4,0},{1,5},{5,1},{2,6},{6,2},{3,7},{7,3},{8,12},{12,8},{9,1... | collective-permute-start | bytes 9437192 | tf_op jit(solution)/shard_map/ppermute | solution.py:48
  21.0 2.5 top_k.11
  25.6 2.3 select_select_fusion
  27.9 11.2 %all-to-all-start.3 = ((bf16[64,96,256]{2,1,0:T(8,128)(2,1)}), bf16[64,96,256]{2,1,0:T(8,128)(2,1)}, u32[]{:S(2)}, u32[]{:S(2)}) async-start(bf16[64,96,256]{2,1,0:T(8,128)(2,1)} %bitcast.36), calls=%async_computation.3 | async-start | bytes 6291456 | tf_op jit(solution)/shard_map/all_to_all | solution.py:56
  41.7 76.0 %all-to-all-done.3 = bf16[64,96,256]{2,1,0:T(8,128)(2,1)} async-done(((bf16[64,96,256]{2,1,0:T(8,128)(2,1)}), bf16[64,96,256]{2,1,0:T(8,128)(2,1)}, u32[]{:S(2)}, u32[]{:S(2)}) %all-to-all-start.3) | async-done | bytes 3145760 | tf_op jit(solution)/shard_map/all_to_all | solution.py:56
  117.7 1.4 constant_dynamic-slice_fusion
  119.7 2.4 scatter_custom_fusion
  122.4 2.4 scatter_custom_fusion.1
  125.5 2.8 gather_fusion
  128.3 1.2 reshape.422
  129.5 1.4 broadcast_select_fusion
  130.9 55.9 %all_to_all.30 = bf16[128,5,512]{2,1,0:T(8,128)(2,1)S(1)} all-to-all(bf16[128,5,512]{2,1,0:T(8,128)(2,1)S(1)} %broadcast_select_fusion), channel_id=1, replica_groups=mesh['eph'=64,'c'=2,'dp'=4] {'eph','c'}, dimensions={0} | all-to-all | bytes 1310720 | tf_op jit(solution)/shard_map/all_to_all | solution.py:93
  187.4 34.9 %all_to_all.31 = bf16[4,128,5,512]{3,1,2,0:T(8,128)(2,1)S(1)} all-to-all(bf16[4,128,5,512]{3,1,2,0:T(8,128)(2,1)S(1)} %broadcast_in_dim.68), channel_id=1, replica_groups=mesh['eph'=64,'c'=2,'dp'=4] {'dp'}, dimensions={0} | all-to-all | bytes 5242880 | tf_op jit(solution)/shard_map/all_to_all | solution.py:15
  222.3 0.7 convolution_bitcast_fusion.2
  223.0 0.7 fusion.3
  223.8 1.1 broadcast_in_dim.70
  224.9 4.3 %all-to-all-start.2 = ((bf16[4,128,1,4,256]{4,1,3,2,0:T(8,128)(2,1)}), bf16[4,128,1,4,256]{4,1,3,2,0:T(8,128)(2,1)}, u32[]{:S(2)}, u32[]{:S(2)}) async-start(bf16[4,128,1,4,256]{4,1,3,2,0:T(8,128)(2,1)} %broadcast_in_dim.70), calls=%async_computation.2 | async-start | bytes 2097152 | tf_op jit(solution)/shard_map/all_to_all | solution.py:15
  229.1 2.1 fusion.40
  231.2 1.4 convolution_bitcast_fusion.5
  232.7 1.4 fusion.7
  234.0 8.3 %all-to-all-done.2 = bf16[4,128,1,4,256]{4,1,3,2,0:T(8,128)(2,1)} async-done(((bf16[4,128,1,4,256]{4,1,3,2,0:T(8,128)(2,1)}), bf16[4,128,1,4,256]{4,1,3,2,0:T(8,128)(2,1)}, u32[]{:S(2)}, u32[]{:S(2)}) %all-to-all-start.2) | async-done | bytes 1048608 | tf_op jit(solution)/shard_map/all_to_all | solution.py:15
  242.3 0.7 broadcast_in_dim.71
  243.0 3.6 %all-to-all-start.4 = ((bf16[4,128,1,256]{3,1,2,0:T(8,128)(2,1)}), bf16[4,128,1,256]{3,1,2,0:T(8,128)(2,1)S(1)}, u32[]{:S(2)}, u32[]{:S(2)}) async-start(bf16[4,128,1,256]{3,1,2,0:T(8,128)(2,1)} %broadcast_in_dim.71), calls=%async_computation.4 | async-start | bytes 524288 | tf_op jit(solution)/shard_map/all_to_all | solution.py:15
  246.6 2.7 fusion
  249.8 2.2 all-to-all-done.4
  252.3 1.4 copy.77
  253.7 10.9 %all-to-all-start.5 = ((bf16[128,5,512]{2,1,0:T(8,128)(2,1)}), bf16[128,5,512]{2,1,0:T(8,128)(2,1)S(1)}, u32[]{:S(2)}, u32[]{:S(2)}) async-start(bf16[128,5,512]{2,1,0:T(8,128)(2,1)} %copy.77), calls=%async_computation.5 | async-start | bytes 2097152 | tf_op jit(solution)/shard_map/all_to_all | solution.py:135
  265.3 30.2 %all-to-all-done.5 = bf16[128,5,512]{2,1,0:T(8,128)(2,1)S(1)} async-done(((bf16[128,5,512]{2,1,0:T(8,128)(2,1)}), bf16[128,5,512]{2,1,0:T(8,128)(2,1)S(1)}, u32[]{:S(2)}, u32[]{:S(2)}) %all-to-all-start.5) | async-done | bytes 655392 | tf_op jit(solution)/shard_map/all_to_all | solution.py:135
  295.8 2.0 gather_fusion.1
  297.7 1.1 multiply_reduce_fusion
  (71 shorter events, 5.5 us)
Async XLA Ops:
  6.5 118.9 %copy-start = (bf16[64,512]{1,0:T(8,128)(2,1)S(1)}, bf16[64,512]{1,0:T(8,128)(2,1)}, u32[]{:S(2)}) copy-start(bf16[64,512]{1,0:T(8,128)(2,1)} %param.6) | copy-start | bytes 196612
  8.0 12.0 %copy-start.6 = (s32[64,8]{0,1:T(8,128)S(1)}, s32[64,8]{0,1:T(8,128)}, u32[]{:S(2)}) copy-start(s32[64,8]{0,1:T(8,128)} %param.7) | copy-start | bytes 6148
  8.0 17.6 %copy-start.1 = (bf16[1,2048,256]{2,1,0:T(8,128)(2,1)S(1)}, bf16[1,2048,256]{2,1,0:T(8,128)(2,1)}, u32[]{:S(2)}) copy-start(bf16[1,2048,256]{2,1,0:T(8,128)(2,1)} %param.9) | copy-start | bytes 3145732
  8.0 17.6 %copy-start.2 = (bf16[1,2048,256]{2,1,0:T(8,128)(2,1)S(1)}, bf16[1,2048,256]{2,1,0:T(8,128)(2,1)}, u32[]{:S(2)}) copy-start(bf16[1,2048,256]{2,1,0:T(8,128)(2,1)} %param.10) | copy-start | bytes 3145732
  11.2 14.4 %collective-permute-start = (bf16[6144,256]{1,0:T(8,128)(2,1)}, bf16[6144,256]{1,0:T(8,128)(2,1)}, u32[]{:S(2)}, u32[]{:S(2)}) collective-permute-start(bf16[6144,256]{1,0:T(8,128)(2,1)} %pad_maximum_fusion), channel_id=1, source_target_pairs={{0,4},{4,0},{1,5},{5,1},{2,6},{6,2},{3,7},{7,3},{8,12},{12,8},{9,1... | collective-permute-start | bytes 9437192 | tf_op jit(solution)/shard_map/ppermute | solution.py:48
  27.9 89.8 %all-to-all-start.3 = ((bf16[64,96,256]{2,1,0:T(8,128)(2,1)}), bf16[64,96,256]{2,1,0:T(8,128)(2,1)}, u32[]{:S(2)}, u32[]{:S(2)}) async-start(bf16[64,96,256]{2,1,0:T(8,128)(2,1)} %bitcast.36), calls=%async_computation.3 | async-start | bytes 6291456 | tf_op jit(solution)/shard_map/all_to_all | solution.py:56
  39.1 190.1 %all-gather.3.cloned.1.call-start = ((), (), s32[]{:S(2)}) async-start(), calls=%async_computation.6 | async-start | bytes 3194880 | tf_op jit(solution)/shard_map/all_gather | solution.py:58
  222.3 1.5 copy-start.3
  224.9 17.5 %all-to-all-start.2 = ((bf16[4,128,1,4,256]{4,1,3,2,0:T(8,128)(2,1)}), bf16[4,128,1,4,256]{4,1,3,2,0:T(8,128)(2,1)}, u32[]{:S(2)}, u32[]{:S(2)}) async-start(bf16[4,128,1,4,256]{4,1,3,2,0:T(8,128)(2,1)} %broadcast_in_dim.70), calls=%async_computation.2 | async-start | bytes 2097152 | tf_op jit(solution)/shard_map/all_to_all | solution.py:15
  231.2 15.4 %copy-start.4 = (bf16[1,1024,512]{2,1,0:T(8,128)(2,1)S(1)}, bf16[1,1024,512]{2,1,0:T(8,128)(2,1)}, u32[]{:S(2)}) copy-start(bf16[1,1024,512]{2,1,0:T(8,128)(2,1)} %param.11) | copy-start | bytes 3145732
  243.0 8.9 %all-to-all-start.4 = ((bf16[4,128,1,256]{3,1,2,0:T(8,128)(2,1)}), bf16[4,128,1,256]{3,1,2,0:T(8,128)(2,1)S(1)}, u32[]{:S(2)}, u32[]{:S(2)}) async-start(bf16[4,128,1,256]{3,1,2,0:T(8,128)(2,1)} %broadcast_in_dim.71), calls=%async_computation.4 | async-start | bytes 524288 | tf_op jit(solution)/shard_map/all_to_all | solution.py:15
  249.4 2.9 copy-start.5
  249.8 15.1 %copy-start.7 = (f32[64,8]{0,1:T(8,128)S(1)}, f32[64,8]{0,1:T(8,128)}, u32[]{:S(2)}) copy-start(f32[64,8]{0,1:T(8,128)} %param.8) | copy-start | bytes 6148
  253.7 41.8 %all-to-all-start.5 = ((bf16[128,5,512]{2,1,0:T(8,128)(2,1)}), bf16[128,5,512]{2,1,0:T(8,128)(2,1)S(1)}, u32[]{:S(2)}, u32[]{:S(2)}) async-start(bf16[128,5,512]{2,1,0:T(8,128)(2,1)} %copy.77), calls=%async_computation.5 | async-start | bytes 2097152 | tf_op jit(solution)/shard_map/all_to_all | solution.py:135
Sparse Core Ops, SparseCore 0:
  119.3 107.8 all-gather.2

commit v13 on v12

--- a/solution.py
+++ b/solution.py
@@ -52,16 +52,6 @@
     take_own = mine == my_expert
     take_sib = mine == sibling_expert
     packed = jnp.where(take_own, own, jnp.where(take_sib, swapped, jnp.zeros_like(own)))
-    blocks = packed.reshape(pair_count, -1, packed.shape[1])
-    pieces = lax.all_to_all(blocks, "eph", split_axis=0, concat_axis=0, tiled=True)
-    piece = lax.dynamic_index_in_dim(pieces, hot_ids[parity] // HOT, axis=0, keepdims=False)
-    spread_back = lax.all_gather(piece, "eph", axis=0, tiled=True)
-    model_rows = gate_weight.shape[1]
-    spare_gate = spread_back[:model_rows]
-    spare_up = spread_back[model_rows : 2 * model_rows]
-    spare_down = spread_back[2 * model_rows :].reshape(down_weight.shape[1:])
-    tokens, packed = lax.optimization_barrier((tokens, packed))
-
     earlier = jnp.cumsum(matches, axis=0) - matches
     order_rank = jnp.sum(earlier * matches, axis=1)
     hot_match = (flat_ids[:, None] == hot_ids[None, :]).astype(jnp.int32)
@@ -91,6 +81,17 @@
     )
     outgoing = jnp.take(tokens, source_row, axis=0, mode="fill", fill_value=0)
     arrived = lax.all_to_all(outgoing, EP, split_axis=0, concat_axis=0, tiled=True)
+    arrived, packed = lax.optimization_barrier((arrived, packed))
+    blocks = packed.reshape(pair_count, -1, packed.shape[1])
+    pieces = lax.all_to_all(blocks, "eph", split_axis=0, concat_axis=0, tiled=True)
+    piece = lax.dynamic_index_in_dim(pieces, hot_ids[parity] // HOT, axis=0, keepdims=False)
+    spread_back = lax.all_gather(piece, "eph", axis=0, tiled=True)
+    model_rows = gate_weight.shape[1]
+    spare_gate = spread_back[:model_rows]
+    spare_up = spread_back[model_rows : 2 * model_rows]
+    spare_down = spread_back[2 * model_rows :].reshape(down_weight.shape[1:])
+
+    arrived, piece = lax.optimization_barrier((arrived, piece))
     incoming = gather_dp(arrived, dp_count)
     primary_rows = incoming[:, :, :primary_slots].reshape(
         dp_count, ep_count, exp_dev, capacity, slice_width

time: 306 us -> 331 us (1.082)
  waiting for transfers between devices: 117 us -> 190 us
  blocking collectives: 90.8 us -> 30.6 us
  starting transfers between devices: 38.7 us -> 48.9 us
    all_gather x1, waiting for transfers between devices: 0.02 us -> 57.7 us  [local(): spread_back = lax.all_gather(piece, 'eph', axis=0, tiled=True)]
    all_to_all x1 -> x0, blocking collectives: 55.9 us -> none  [local(): lax.all_to_all(outgoing, EP, split_axis=0, concat_axis=0, tiled=True)]
    all_to_all x0 -> x1, waiting for transfers between devices: none -> 26.3 us  [local(): lax.all_to_all(outgoing, EP, split_axis=0, concat_axis=0, tiled=True)]
    all_to_all x0 -> x1, starting transfers between devices: none -> 12.1 us  [local(): lax.all_to_all(outgoing, EP, split_axis=0, concat_axis=0, tiled=True)]
    all_to_all x2, waiting for transfers between devices: 10.5 us -> 3.64 us  [gather_dp(): lax.all_to_all(stacked, 'dp', split_axis=0, concat_axis=0, tiled=True)]
    all_to_all x1, starting transfers between devices: 11.2 us -> 5.59 us  [local(): lax.all_to_all(blocks, 'eph', split_axis=0, concat_axis=0, tiled=True)]
    all_to_all x1, blocking collectives: 34.9 us -> 30.6 us  [gather_dp(): lax.all_to_all(stacked, 'dp', split_axis=0, concat_axis=0, tiled=True)]
    all_to_all x1, starting transfers between devices: 10.9 us -> 14.9 us  [local(): lax.all_to_all(results, EP, split_axis=0, concat_axis=0, tiled=True)]
  transfers between devices with their start and end apart: 6 -> 7, of which waited for: 5 -> 5; matrix products, arithmetic and copies ran while one was open for 9% -> 9% of each run, Pallas kernels for 0% -> 0%
where the time goes in v13:
time: 331 us; the launch traced here: 330 us
  waiting for transfers between devices  190 us (57%)
  starting transfers between devices  48.9 us (15%)
  blocking collectives  30.6 us (9%)
  local copies, waits for them, and re-layouts  24.3 us (7%)
  between operations  17.7 us (5%)
  other arithmetic  12.2 us (4%)
  matrix products  6.01 us (2%)
    all_to_all x1, waiting for transfers between devices, local(): lax.all_to_all(blocks, 'eph', split_axis=0, concat_axis=0, tiled=True)  72.5 us
    all_gather x1, waiting for transfers between devices, local(): spread_back = lax.all_gather(piece, 'eph', axis=0, tiled=True)  57.7 us
    all_to_all x1, blocking collectives, gather_dp(): lax.all_to_all(stacked, 'dp', split_axis=0, concat_axis=0, tiled=True)  30.6 us
    all_to_all x1, waiting for transfers between devices, local(): lax.all_to_all(results, EP, split_axis=0, concat_axis=0, tiled=True)  30.2 us
    all_to_all x1, waiting for transfers between devices, local(): lax.all_to_all(outgoing, EP, split_axis=0, concat_axis=0, tiled=True)  26.3 us
    all_to_all x1, starting transfers between devices, local(): lax.all_to_all(results, EP, split_axis=0, concat_axis=0, tiled=True)  14.9 us
    all_to_all x1, starting transfers between devices, local(): lax.all_to_all(outgoing, EP, split_axis=0, concat_axis=0, tiled=True)  12.1 us
    ppermute x1, starting transfers between devices, local(): swapped = lax.ppermute(own, 'c', [(0, 1), (1, 0)])  8.78 us
  transfers between devices with their start and end apart: 7, of which 5 were waited for; matrix products, arithmetic and copies ran while one was open for 9% of the time, Pallas kernels for 0%

profile of v13, /device:TPU:1, one launch (start us, length us, event | category | flops | bytes accessed | tf_op | source)
XLA Modules:
  0.0 330.1 jit_solution(9895177212127518017)
XLA Ops:
  6.5 1.4 reshape_squeeze.3
  8.0 3.0 pad_maximum_fusion
  11.0 8.8 %collective-permute-start = (bf16[6144,256]{1,0:T(8,128)(2,1)}, bf16[6144,256]{1,0:T(8,128)(2,1)}, u32[]{:S(2)}, u32[]{:S(2)}) collective-permute-start(bf16[6144,256]{1,0:T(8,128)(2,1)} %pad_maximum_fusion), channel_id=1, source_target_pairs={{0,4},{4,0},{1,5},{5,1},{2,6},{6,2},{3,7},{7,3},{8,12},{12,8},{9,1... | collective-permute-start | bytes 9437192 | tf_op jit(solution)/shard_map/ppermute | solution.py:48
  21.2 2.5 top_k.11
  23.8 2.4 scatter_custom_fusion
  26.5 2.4 scatter_custom_fusion.1
  29.4 2.8 gather_fusion
  32.2 1.2 reshape.422
  33.7 2.5 broadcast_select_fusion
  36.2 12.1 %all-to-all-start = ((bf16[128,5,512]{2,1,0:T(8,128)(2,1)}), bf16[128,5,512]{2,1,0:T(8,128)(2,1)}, u32[]{:S(2)}, u32[]{:S(2)}) async-start(bf16[128,5,512]{2,1,0:T(8,128)(2,1)} %broadcast_select_fusion), calls=%async_computation | async-start | bytes 2097152 | tf_op jit(solution)/shard_map/all_to_all | solution.py:83
  50.2 2.3 select_select_fusion
  52.5 26.3 %all-to-all-done = bf16[128,5,512]{2,1,0:T(8,128)(2,1)} async-done(((bf16[128,5,512]{2,1,0:T(8,128)(2,1)}), bf16[128,5,512]{2,1,0:T(8,128)(2,1)}, u32[]{:S(2)}, u32[]{:S(2)}) %all-to-all-start) | async-done | bytes 655392 | tf_op jit(solution)/shard_map/all_to_all | solution.py:83
  78.8 5.6 %all-to-all-start.1 = ((bf16[64,96,256]{2,1,0:T(8,128)(2,1)}), bf16[64,96,256]{2,1,0:T(8,128)(2,1)}, u32[]{:S(2)}, u32[]{:S(2)}) async-start(bf16[64,96,256]{2,1,0:T(8,128)(2,1)} %bitcast.36), calls=%async_computation.1 | async-start | bytes 6291456 | tf_op jit(solution)/shard_map/all_to_all | solution.py:86
  87.1 72.5 %all-to-all-done.1 = bf16[64,96,256]{2,1,0:T(8,128)(2,1)} async-done(((bf16[64,96,256]{2,1,0:T(8,128)(2,1)}), bf16[64,96,256]{2,1,0:T(8,128)(2,1)}, u32[]{:S(2)}, u32[]{:S(2)}) %all-to-all-start.1) | async-done | bytes 3145760 | tf_op jit(solution)/shard_map/all_to_all | solution.py:86
  159.6 1.4 constant_dynamic-slice_fusion
  161.1 1.5 copy.73
  162.8 30.6 %all_to_all.30 = bf16[4,128,5,512]{3,1,2,0:T(8,128)(2,1)S(1)} all-to-all(bf16[4,128,5,512]{3,1,2,0:T(8,128)(2,1)S(1)} %broadcast_in_dim.68), channel_id=1, replica_groups=mesh['eph'=64,'c'=2,'dp'=4] {'dp'}, dimensions={0} | all-to-all | bytes 5242880 | tf_op jit(solution)/shard_map/all_to_all | solution.py:15
  194.9 1.1 broadcast_in_dim.70
  196.0 3.5 %all-to-all-start.3 = ((bf16[4,128,1,4,256]{4,1,3,2,0:T(8,128)(2,1)}), bf16[4,128,1,4,256]{4,1,3,2,0:T(8,128)(2,1)S(1)}, u32[]{:S(2)}, u32[]{:S(2)}) async-start(bf16[4,128,1,4,256]{4,1,3,2,0:T(8,128)(2,1)} %broadcast_in_dim.70), calls=%async_computation.3 | async-start | bytes 2097152 | tf_op jit(solution)/shard_map/all_to_all | solution.py:15
  199.5 57.7 %all-gather.3.cloned.1.call-done = bf16[1,6144,256]{2,1,0:T(8,128)(2,1)} async-done(((bf16[1,96,256]{2,1,0:T(8,128)(2,1)}), bf16[1,6144,256]{2,1,0:T(8,128)(2,1)}) %all-gather.3.cloned.1.call-update) | async-done | bytes 3145744 | tf_op jit(solution)/shard_map/all_gather | solution.py:88
  257.2 2.1 fusion.40
  259.3 1.4 convolution_bitcast_fusion.5
  260.7 1.4 fusion.7
  262.1 0.7 broadcast_in_dim.71
  262.8 4.0 %all-to-all-start.4 = ((bf16[4,128,1,256]{3,1,2,0:T(8,128)(2,1)}), bf16[4,128,1,256]{3,1,2,0:T(8,128)(2,1)S(1)}, u32[]{:S(2)}, u32[]{:S(2)}) async-start(bf16[4,128,1,256]{3,1,2,0:T(8,128)(2,1)} %broadcast_in_dim.71), calls=%async_computation.4 | async-start | bytes 524288 | tf_op jit(solution)/shard_map/all_to_all | solution.py:15
  266.8 1.5 fusion
  268.7 3.6 %all-to-all-done.4 = bf16[4,128,1,256]{3,1,2,0:T(8,128)(2,1)S(1)} async-done(((bf16[4,128,1,256]{3,1,2,0:T(8,128)(2,1)}), bf16[4,128,1,256]{3,1,2,0:T(8,128)(2,1)S(1)}, u32[]{:S(2)}, u32[]{:S(2)}) %all-to-all-start.4) | async-done | bytes 262176 | tf_op jit(solution)/shard_map/all_to_all | solution.py:15
  272.7 1.4 copy.77
  274.1 14.9 %all-to-all-start.5 = ((bf16[128,5,512]{2,1,0:T(8,128)(2,1)}), bf16[128,5,512]{2,1,0:T(8,128)(2,1)S(1)}, u32[]{:S(2)}, u32[]{:S(2)}) async-start(bf16[128,5,512]{2,1,0:T(8,128)(2,1)} %copy.77), calls=%async_computation.5 | async-start | bytes 2097152 | tf_op jit(solution)/shard_map/all_to_all | solution.py:136
  289.8 30.2 %all-to-all-done.5 = bf16[128,5,512]{2,1,0:T(8,128)(2,1)S(1)} async-done(((bf16[128,5,512]{2,1,0:T(8,128)(2,1)}), bf16[128,5,512]{2,1,0:T(8,128)(2,1)S(1)}, u32[]{:S(2)}, u32[]{:S(2)}) %all-to-all-start.5) | async-done | bytes 655392 | tf_op jit(solution)/shard_map/all_to_all | solution.py:136
  320.2 2.0 gather_fusion.1
  322.2 1.1 multiply_reduce_fusion
  (72 shorter events, 6.4 us)
Async XLA Ops:
  6.5 22.9 %copy-start = (bf16[64,512]{1,0:T(8,128)(2,1)S(1)}, bf16[64,512]{1,0:T(8,128)(2,1)}, u32[]{:S(2)}) copy-start(bf16[64,512]{1,0:T(8,128)(2,1)} %param.6) | copy-start | bytes 196612
  8.0 11.8 %copy-start.6 = (s32[64,8]{0,1:T(8,128)S(1)}, s32[64,8]{0,1:T(8,128)}, u32[]{:S(2)}) copy-start(s32[64,8]{0,1:T(8,128)} %param.7) | copy-start | bytes 6148
  11.0 39.1 %collective-permute-start = (bf16[6144,256]{1,0:T(8,128)(2,1)}, bf16[6144,256]{1,0:T(8,128)(2,1)}, u32[]{:S(2)}, u32[]{:S(2)}) collective-permute-start(bf16[6144,256]{1,0:T(8,128)(2,1)} %pad_maximum_fusion), channel_id=1, source_target_pairs={{0,4},{4,0},{1,5},{5,1},{2,6},{6,2},{3,7},{7,3},{8,12},{12,8},{9,1... | collective-permute-start | bytes 9437192 | tf_op jit(solution)/shard_map/ppermute | solution.py:48
  32.2 18.0 %copy-start.1 = (bf16[1,2048,256]{2,1,0:T(8,128)(2,1)S(1)}, bf16[1,2048,256]{2,1,0:T(8,128)(2,1)}, u32[]{:S(2)}) copy-start(bf16[1,2048,256]{2,1,0:T(8,128)(2,1)} %param.9) | copy-start | bytes 3145732
  33.4 16.8 %copy-start.2 = (bf16[1,2048,256]{2,1,0:T(8,128)(2,1)S(1)}, bf16[1,2048,256]{2,1,0:T(8,128)(2,1)}, u32[]{:S(2)}) copy-start(bf16[1,2048,256]{2,1,0:T(8,128)(2,1)} %param.10) | copy-start | bytes 3145732
  36.2 42.7 %all-to-all-start = ((bf16[128,5,512]{2,1,0:T(8,128)(2,1)}), bf16[128,5,512]{2,1,0:T(8,128)(2,1)}, u32[]{:S(2)}, u32[]{:S(2)}) async-start(bf16[128,5,512]{2,1,0:T(8,128)(2,1)} %broadcast_select_fusion), calls=%async_computation | async-start | bytes 2097152 | tf_op jit(solution)/shard_map/all_to_all | solution.py:83
  78.8 80.8 %all-to-all-start.1 = ((bf16[64,96,256]{2,1,0:T(8,128)(2,1)}), bf16[64,96,256]{2,1,0:T(8,128)(2,1)}, u32[]{:S(2)}, u32[]{:S(2)}) async-start(bf16[64,96,256]{2,1,0:T(8,128)(2,1)} %bitcast.36), calls=%async_computation.1 | async-start | bytes 6291456 | tf_op jit(solution)/shard_map/all_to_all | solution.py:86
  84.4 172.8 %all-gather.3.cloned.1.call-start = ((), (), s32[]{:S(2)}) async-start(), calls=%async_computation.6 | async-start | bytes 3194880 | tf_op jit(solution)/shard_map/all_gather | solution.py:88
  193.4 1.5 copy-start.3
  196.0 66.1 %all-to-all-start.3 = ((bf16[4,128,1,4,256]{4,1,3,2,0:T(8,128)(2,1)}), bf16[4,128,1,4,256]{4,1,3,2,0:T(8,128)(2,1)S(1)}, u32[]{:S(2)}, u32[]{:S(2)}) async-start(bf16[4,128,1,4,256]{4,1,3,2,0:T(8,128)(2,1)} %broadcast_in_dim.70), calls=%async_computation.3 | async-start | bytes 2097152 | tf_op jit(solution)/shard_map/all_to_all | solution.py:15
  259.3 7.5 %copy-start.4 = (bf16[1,1024,512]{2,1,0:T(8,128)(2,1)S(1)}, bf16[1,1024,512]{2,1,0:T(8,128)(2,1)}, u32[]{:S(2)}) copy-start(bf16[1,1024,512]{2,1,0:T(8,128)(2,1)} %param.11) | copy-start | bytes 3145732
  262.8 9.5 %all-to-all-start.4 = ((bf16[4,128,1,256]{3,1,2,0:T(8,128)(2,1)}), bf16[4,128,1,256]{3,1,2,0:T(8,128)(2,1)S(1)}, u32[]{:S(2)}, u32[]{:S(2)}) async-start(bf16[4,128,1,256]{3,1,2,0:T(8,128)(2,1)} %broadcast_in_dim.71), calls=%async_computation.4 | async-start | bytes 524288 | tf_op jit(solution)/shard_map/all_to_all | solution.py:15
  268.3 4.3 %copy-start.5 = (bf16[128,4,512]{2,0,1:T(8,128)(2,1)S(1)}, bf16[128,4,512]{2,0,1:T(8,128)(2,1)}, u32[]{:S(2)}) copy-start(bf16[128,4,512]{2,0,1:T(8,128)(2,1)} %fusion) | copy-start | bytes 1572868
  268.7 20.6 %copy-start.7 = (f32[64,8]{0,1:T(8,128)S(1)}, f32[64,8]{0,1:T(8,128)}, u32[]{:S(2)}) copy-start(f32[64,8]{0,1:T(8,128)} %param.8) | copy-start | bytes 6148
  274.1 45.9 %all-to-all-start.5 = ((bf16[128,5,512]{2,1,0:T(8,128)(2,1)}), bf16[128,5,512]{2,1,0:T(8,128)(2,1)S(1)}, u32[]{:S(2)}, u32[]{:S(2)}) async-start(bf16[128,5,512]{2,1,0:T(8,128)(2,1)} %copy.77), calls=%async_computation.5 | async-start | bytes 2097152 | tf_op jit(solution)/shard_map/all_to_all | solution.py:136
Sparse Core Ops, SparseCore 0:
  161.2 95.9 all-gather.2

commit v14 on v12

--- a/solution.py
+++ b/solution.py
@@ -60,7 +60,6 @@
     spare_gate = spread_back[:model_rows]
     spare_up = spread_back[model_rows : 2 * model_rows]
     spare_down = spread_back[2 * model_rows :].reshape(down_weight.shape[1:])
-    tokens, packed = lax.optimization_barrier((tokens, packed))
 
     earlier = jnp.cumsum(matches, axis=0) - matches
     order_rank = jnp.sum(earlier * matches, axis=1)

time: 306 us -> 306 us (level)
  no operation moved by 1% of the time
where the time goes in v14:
time: 306 us
  waiting for transfers between devices  117 us (38%)
  blocking collectives  90.8 us (30%)
  starting transfers between devices  38.5 us (13%)
  local copies, waits for them, and re-layouts  23 us (8%)
  between operations  17.7 us (6%)
  other arithmetic  11.3 us (4%)
  matrix products  7.23 us (2%)
    all_to_all x1, waiting for transfers between devices, local(): lax.all_to_all(blocks, 'eph', split_axis=0, concat_axis=0, tiled=True)  76 us
    all_to_all x1, blocking collectives, local(): lax.all_to_all(outgoing, EP, split_axis=0, concat_axis=0, tiled=True)  55.9 us
    all_to_all x1, blocking collectives, gather_dp(): lax.all_to_all(stacked, 'dp', split_axis=0, concat_axis=0, tiled=True)  34.9 us
    all_to_all x1, waiting for transfers between devices, local(): lax.all_to_all(results, EP, split_axis=0, concat_axis=0, tiled=True)  30.2 us
    all_to_all x1, starting transfers between devices, local(): lax.all_to_all(blocks, 'eph', split_axis=0, concat_axis=0, tiled=True)  11.2 us
    all_to_all x1, starting transfers between devices, local(): lax.all_to_all(results, EP, split_axis=0, concat_axis=0, tiled=True)  10.7 us
    all_to_all x2, waiting for transfers between devices, gather_dp(): lax.all_to_all(stacked, 'dp', split_axis=0, concat_axis=0, tiled=True)  10.7 us
    ppermute x1, starting transfers between devices, local(): swapped = lax.ppermute(own, 'c', [(0, 1), (1, 0)])  8.78 us
  transfers between devices with their start and end apart: 6, of which 5 were waited for; matrix products, arithmetic and copies ran while one was open for 9% of the time, Pallas kernels for 0%

profile of v14, /device:TPU:1, one launch (start us, length us, event | category | flops | bytes accessed | tf_op | source)
XLA Modules:
  0.0 305.7 jit_solution(9045438319003991885)
XLA Ops:
  6.5 1.4 reshape_squeeze.3
  8.0 3.2 %pad_maximum_fusion = bf16[6144,256]{1,0:T(8,128)(2,1)} fusion(bf16[2048,256]{1,0:T(8,128)(2,1)S(1)} %reshape_squeeze.3, bf16[2048,256]{1,0:T(8,128)(2,1)} %bitcast.116, bf16[2048,256]{1,0:T(8,128)(2,1)} %bitcast.113), kind=kLoop, calls=%fused_computation.4 | loop fusion | flops 9437184 | bytes 6291456 | tf_op jit(solution)/shard_map/concatenate | solution.py:45
  11.2 8.8 %collective-permute-start = (bf16[6144,256]{1,0:T(8,128)(2,1)}, bf16[6144,256]{1,0:T(8,128)(2,1)}, u32[]{:S(2)}, u32[]{:S(2)}) collective-permute-start(bf16[6144,256]{1,0:T(8,128)(2,1)} %pad_maximum_fusion), channel_id=1, source_target_pairs={{0,4},{4,0},{1,5},{5,1},{2,6},{6,2},{3,7},{7,3},{8,12},{12,8},{9,1... | collective-permute-start | bytes 9437192 | tf_op jit(solution)/shard_map/ppermute | solution.py:48
  21.0 2.5 top_k.11
  25.6 2.3 select_select_fusion
  27.9 11.2 %all-to-all-start.3 = ((bf16[64,96,256]{2,1,0:T(8,128)(2,1)}), bf16[64,96,256]{2,1,0:T(8,128)(2,1)}, u32[]{:S(2)}, u32[]{:S(2)}) async-start(bf16[64,96,256]{2,1,0:T(8,128)(2,1)} %bitcast.36), calls=%async_computation.3 | async-start | bytes 6291456 | tf_op jit(solution)/shard_map/all_to_all | solution.py:56
  41.7 76.0 %all-to-all-done.3 = bf16[64,96,256]{2,1,0:T(8,128)(2,1)} async-done(((bf16[64,96,256]{2,1,0:T(8,128)(2,1)}), bf16[64,96,256]{2,1,0:T(8,128)(2,1)}, u32[]{:S(2)}, u32[]{:S(2)}) %all-to-all-start.3) | async-done | bytes 3145760 | tf_op jit(solution)/shard_map/all_to_all | solution.py:56
  117.7 1.4 constant_dynamic-slice_fusion
  119.7 2.4 scatter_custom_fusion
  122.4 2.4 scatter_custom_fusion.1
  125.2 2.8 gather_fusion
  128.0 1.2 reshape.422
  129.5 1.4 broadcast_select_fusion
  130.9 55.9 %all_to_all.30 = bf16[128,5,512]{2,1,0:T(8,128)(2,1)S(1)} all-to-all(bf16[128,5,512]{2,1,0:T(8,128)(2,1)S(1)} %broadcast_select_fusion), channel_id=1, replica_groups=mesh['eph'=64,'c'=2,'dp'=4] {'eph','c'}, dimensions={0} | all-to-all | bytes 1310720 | tf_op jit(solution)/shard_map/all_to_all | solution.py:92
  187.3 34.9 %all_to_all.31 = bf16[4,128,5,512]{3,1,2,0:T(8,128)(2,1)S(1)} all-to-all(bf16[4,128,5,512]{3,1,2,0:T(8,128)(2,1)S(1)} %broadcast_in_dim.67), channel_id=1, replica_groups=mesh['eph'=64,'c'=2,'dp'=4] {'dp'}, dimensions={0} | all-to-all | bytes 5242880 | tf_op jit(solution)/shard_map/all_to_all | solution.py:15
  222.3 0.7 convolution_bitcast_fusion.2
  223.0 0.7 fusion.3
  223.8 1.1 broadcast_in_dim.69
  224.9 4.3 %all-to-all-start.2 = ((bf16[4,128,1,4,256]{4,1,3,2,0:T(8,128)(2,1)}), bf16[4,128,1,4,256]{4,1,3,2,0:T(8,128)(2,1)}, u32[]{:S(2)}, u32[]{:S(2)}) async-start(bf16[4,128,1,4,256]{4,1,3,2,0:T(8,128)(2,1)} %broadcast_in_dim.69), calls=%async_computation.2 | async-start | bytes 2097152 | tf_op jit(solution)/shard_map/all_to_all | solution.py:15
  229.2 2.1 fusion.40
  231.3 1.4 convolution_bitcast_fusion.5
  232.7 1.4 fusion.7
  234.1 8.5 %all-to-all-done.2 = bf16[4,128,1,4,256]{4,1,3,2,0:T(8,128)(2,1)} async-done(((bf16[4,128,1,4,256]{4,1,3,2,0:T(8,128)(2,1)}), bf16[4,128,1,4,256]{4,1,3,2,0:T(8,128)(2,1)}, u32[]{:S(2)}, u32[]{:S(2)}) %all-to-all-start.2) | async-done | bytes 1048608 | tf_op jit(solution)/shard_map/all_to_all | solution.py:15
  242.5 0.7 broadcast_in_dim.71
  243.3 3.6 %all-to-all-start.4 = ((bf16[4,128,1,256]{3,1,2,0:T(8,128)(2,1)}), bf16[4,128,1,256]{3,1,2,0:T(8,128)(2,1)S(1)}, u32[]{:S(2)}, u32[]{:S(2)}) async-start(bf16[4,128,1,256]{3,1,2,0:T(8,128)(2,1)} %broadcast_in_dim.71), calls=%async_computation.4 | async-start | bytes 524288 | tf_op jit(solution)/shard_map/all_to_all | solution.py:15
  246.9 2.7 fusion
  250.0 2.2 all-to-all-done.4
  252.6 1.4 copy.77
  253.9 10.7 %all-to-all-start.5 = ((bf16[128,5,512]{2,1,0:T(8,128)(2,1)}), bf16[128,5,512]{2,1,0:T(8,128)(2,1)S(1)}, u32[]{:S(2)}, u32[]{:S(2)}) async-start(bf16[128,5,512]{2,1,0:T(8,128)(2,1)} %copy.77), calls=%async_computation.5 | async-start | bytes 2097152 | tf_op jit(solution)/shard_map/all_to_all | solution.py:134
  265.4 30.2 %all-to-all-done.5 = bf16[128,5,512]{2,1,0:T(8,128)(2,1)S(1)} async-done(((bf16[128,5,512]{2,1,0:T(8,128)(2,1)}), bf16[128,5,512]{2,1,0:T(8,128)(2,1)S(1)}, u32[]{:S(2)}, u32[]{:S(2)}) %all-to-all-start.5) | async-done | bytes 655392 | tf_op jit(solution)/shard_map/all_to_all | solution.py:134
  295.8 2.0 gather_fusion.1
  297.8 1.1 multiply_reduce_fusion
  (71 shorter events, 5.5 us)
Async XLA Ops:
  6.5 118.7 %copy-start = (bf16[64,512]{1,0:T(8,128)(2,1)S(1)}, bf16[64,512]{1,0:T(8,128)(2,1)}, u32[]{:S(2)}) copy-start(bf16[64,512]{1,0:T(8,128)(2,1)} %param.6) | copy-start | bytes 196612
  8.0 12.0 %copy-start.6 = (s32[64,8]{0,1:T(8,128)S(1)}, s32[64,8]{0,1:T(8,128)}, u32[]{:S(2)}) copy-start(s32[64,8]{0,1:T(8,128)} %param.7) | copy-start | bytes 6148
  8.0 17.6 %copy-start.1 = (bf16[1,2048,256]{2,1,0:T(8,128)(2,1)S(1)}, bf16[1,2048,256]{2,1,0:T(8,128)(2,1)}, u32[]{:S(2)}) copy-start(bf16[1,2048,256]{2,1,0:T(8,128)(2,1)} %param.9) | copy-start | bytes 3145732
  8.0 17.6 %copy-start.2 = (bf16[1,2048,256]{2,1,0:T(8,128)(2,1)S(1)}, bf16[1,2048,256]{2,1,0:T(8,128)(2,1)}, u32[]{:S(2)}) copy-start(bf16[1,2048,256]{2,1,0:T(8,128)(2,1)} %param.10) | copy-start | bytes 3145732
  11.2 14.4 %collective-permute-start = (bf16[6144,256]{1,0:T(8,128)(2,1)}, bf16[6144,256]{1,0:T(8,128)(2,1)}, u32[]{:S(2)}, u32[]{:S(2)}) collective-permute-start(bf16[6144,256]{1,0:T(8,128)(2,1)} %pad_maximum_fusion), channel_id=1, source_target_pairs={{0,4},{4,0},{1,5},{5,1},{2,6},{6,2},{3,7},{7,3},{8,12},{12,8},{9,1... | collective-permute-start | bytes 9437192 | tf_op jit(solution)/shard_map/ppermute | solution.py:48
  27.9 89.8 %all-to-all-start.3 = ((bf16[64,96,256]{2,1,0:T(8,128)(2,1)}), bf16[64,96,256]{2,1,0:T(8,128)(2,1)}, u32[]{:S(2)}, u32[]{:S(2)}) async-start(bf16[64,96,256]{2,1,0:T(8,128)(2,1)} %bitcast.36), calls=%async_computation.3 | async-start | bytes 6291456 | tf_op jit(solution)/shard_map/all_to_all | solution.py:56
  39.1 190.1 %all-gather.3.cloned.1.call-start = ((), (), s32[]{:S(2)}) async-start(), calls=%async_computation.6 | async-start | bytes 3194880 | tf_op jit(solution)/shard_map/all_gather | solution.py:58
  222.3 1.5 copy-start.3
  224.9 17.6 %all-to-all-start.2 = ((bf16[4,128,1,4,256]{4,1,3,2,0:T(8,128)(2,1)}), bf16[4,128,1,4,256]{4,1,3,2,0:T(8,128)(2,1)}, u32[]{:S(2)}, u32[]{:S(2)}) async-start(bf16[4,128,1,4,256]{4,1,3,2,0:T(8,128)(2,1)} %broadcast_in_dim.69), calls=%async_computation.2 | async-start | bytes 2097152 | tf_op jit(solution)/shard_map/all_to_all | solution.py:15
  231.2 15.6 %copy-start.4 = (bf16[1,1024,512]{2,1,0:T(8,128)(2,1)S(1)}, bf16[1,1024,512]{2,1,0:T(8,128)(2,1)}, u32[]{:S(2)}) copy-start(bf16[1,1024,512]{2,1,0:T(8,128)(2,1)} %param.11) | copy-start | bytes 3145732
  243.3 8.9 %all-to-all-start.4 = ((bf16[4,128,1,256]{3,1,2,0:T(8,128)(2,1)}), bf16[4,128,1,256]{3,1,2,0:T(8,128)(2,1)S(1)}, u32[]{:S(2)}, u32[]{:S(2)}) async-start(bf16[4,128,1,256]{3,1,2,0:T(8,128)(2,1)} %broadcast_in_dim.71), calls=%async_computation.4 | async-start | bytes 524288 | tf_op jit(solution)/shard_map/all_to_all | solution.py:15
  249.6 2.9 copy-start.5
  250.0 14.9 %copy-start.7 = (f32[64,8]{0,1:T(8,128)S(1)}, f32[64,8]{0,1:T(8,128)}, u32[]{:S(2)}) copy-start(f32[64,8]{0,1:T(8,128)} %param.8) | copy-start | bytes 6148
  253.9 41.6 %all-to-all-start.5 = ((bf16[128,5,512]{2,1,0:T(8,128)(2,1)}), bf16[128,5,512]{2,1,0:T(8,128)(2,1)S(1)}, u32[]{:S(2)}, u32[]{:S(2)}) async-start(bf16[128,5,512]{2,1,0:T(8,128)(2,1)} %copy.77), calls=%async_computation.5 | async-start | bytes 2097152 | tf_op jit(solution)/shard_map/all_to_all | solution.py:134
Sparse Core Ops, SparseCore 0:
  119.3 107.9 all-gather.2
